TPU v7x, 512 devices: a whole 4x4x16 slice. The times are simulated.
512 devices in a mesh: seq: 64 (over x, z), tp: 8 (over y, core).
Axes of the slice: x: 4, y: 4, z: 16, core: 2. Of those that a mesh axis runs over, the one named last changes fastest.
Arguments:
- hidden_in: bfloat16 [8192, 2048], P('seq', 'tp'), may hold values from -3 to 3
- norm_gain: float32 [2048], replicated, may hold values from 0.1 to 1.9
- w_query: bfloat16 [2048, 2048], P(None, 'tp'), may hold values from -0.125 to 0.125
- w_key: bfloat16 [2048, 1024], P(None, 'tp'), may hold values from -0.125 to 0.125
- w_value: bfloat16 [2048, 1024], P(None, 'tp'), may hold values from -0.125 to 0.125
- w_headgate: bfloat16 [2048, 16], P(None, 'tp'), may hold values from -0.125 to 0.125
- w_out: bfloat16 [2048, 2048], P('tp'), may hold values from -0.125 to 0.125
- q_gain: float32 [128], replicated, may hold values from 1.5 to 4
- k_gain: float32 [128], replicated, may hold values from 0.1 to 1.9
- cache_keys: bfloat16 [2, 8192, 1024], P(None, 'seq', 'tp'), as said below
- cache_values: bfloat16 [2, 8192, 1024], P(None, 'seq', 'tp'), may hold values from -6 to 6
- cached_len: int32 [8], replicated, may hold values from 0 to 8192, as said below
- group_of: int32 [8], replicated, may hold values from 0 to 1, as said below
Outputs:
- layer_out: bfloat16 [8192, 2048], P('seq', 'tp')
Inputs may be any that keep to these rules, and one draw needn't show every extreme that they name: `cache_keys`: keys of the cached positions, of order one and larger. `cached_len`: some request attends to all 8192 cached positions of its prompt, and some to none. `group_of`: every shared prompt is used by some request.
All inputs are finite; a program needn't handle non-finite values.
Results may differ from a plain program's by a relative error of at most 0.018.
Values may be sent and summed in bfloat16 or wider, within the bound.
No kernel may reach another device: no remote copies, remote signals or barrier semaphores. Data moves between devices by JAX's collectives and lax.ppermute only.
A program may use at most 64 MiB of HBM per device.

v0:
```python
import math

import jax
import jax.numpy as jnp
from jax import lax
from jax.sharding import PartitionSpec as P

SPAN = 1024


norm_eps = 1e-06
rope_base = 1000000.0
masked_score = -1e30


def shifted(value, axis, by):
    peers = lax.axis_size(axis)
    pairs = [(i, i + by) for i in range(peers) if 0 <= i + by < peers]
    return lax.ppermute(value, axis, pairs)


def head_norm(vec, gain):
    return vec * lax.rsqrt(jnp.mean(vec * vec, -1, keepdims=True) + norm_eps) * gain


def rotate(vec, positions):
    half = vec.shape[-1] // 2
    freq = jnp.exp(
        jnp.arange(half, dtype=jnp.float32) * (-2.0 * math.log(rope_base) / vec.shape[-1])
    )
    angle = positions.astype(jnp.float32)[:, None] * freq[None, :]
    shape_out = (vec.shape[0],) + (1,) * (vec.ndim - 2) + (half,)
    cosine = jnp.cos(angle).reshape(shape_out)
    sine = jnp.sin(angle).reshape(shape_out)
    first = vec[..., :half]
    second = vec[..., half:]
    return jnp.concatenate([first * cosine - second * sine, second * cosine + first * sine], -1)


def attend(state_now, queries, keys_block, values_block, visible):
    running_max, running_sum, running_acc = state_now
    scores = jnp.einsum(
        "tcgd,kcd->tcgk", queries, keys_block, preferred_element_type=jnp.float32
    ) * queries.shape[-1] ** (-0.5)
    scores = jnp.where(visible[:, None, None, :], scores, masked_score)
    new_max = jnp.maximum(running_max, jnp.max(scores, -1))
    rescale = jnp.exp(running_max - new_max)
    expo = jnp.exp(scores - new_max[..., None])
    new_sum = running_sum * rescale + jnp.sum(expo, -1)
    update = jnp.einsum(
        "tcgk,kcd->tcgd",
        expo.astype(jnp.bfloat16),
        values_block,
        preferred_element_type=jnp.float32,
    )
    return (new_max, new_sum, running_acc * rescale[..., None] + update)


def per_device(
    hidden_in,
    norm_gain,
    w_query,
    w_key,
    w_value,
    w_headgate,
    w_out,
    q_gain,
    k_gain,
    cache_keys,
    cache_values,
    cached_len,
    group_of,
):
    tok_rows = hidden_in.shape[0]
    head_dim = q_gain.shape[0]
    kv_local = w_key.shape[1] // head_dim
    heads_local = w_query.shape[1] // head_dim
    group_size = heads_local // kv_local
    per_request = SPAN // tok_rows
    seq_size = lax.axis_size("seq")
    req_count = seq_size // per_request
    gathered = lax.all_gather(hidden_in, "tp", axis=1, tiled=True)
    widened = gathered.astype(jnp.float32)
    normed = (
        widened * lax.rsqrt(jnp.mean(widened * widened, -1, keepdims=True) + norm_eps) * norm_gain
    ).astype(jnp.bfloat16)
    seq_index = lax.axis_index("seq")
    local_part = seq_index // req_count
    request = seq_index % req_count
    length = cached_len[request]
    group_id = group_of[request]
    positions = length + local_part * tok_rows + jnp.arange(tok_rows, dtype=jnp.int32)
    query_raw = jnp.dot(normed, w_query, preferred_element_type=jnp.float32).reshape(
        tok_rows, kv_local, group_size, head_dim
    )
    queries = rotate(head_norm(query_raw, q_gain), positions).astype(jnp.bfloat16)
    key_raw = jnp.dot(normed, w_key, preferred_element_type=jnp.float32).reshape(
        tok_rows, kv_local, head_dim
    )
    keys_new = rotate(head_norm(key_raw, k_gain), positions).astype(jnp.bfloat16)
    values_new = (
        jnp.dot(normed, w_value, preferred_element_type=jnp.float32)
        .astype(jnp.bfloat16)
        .reshape(tok_rows, kv_local, head_dim)
    )
    gates = jax.nn.sigmoid(jnp.dot(normed, w_headgate, preferred_element_type=jnp.float32)).reshape(
        tok_rows, kv_local, group_size
    )
    state_now = (
        jnp.full((tok_rows, kv_local, group_size), masked_score, jnp.float32),
        jnp.zeros((tok_rows, kv_local, group_size), jnp.float32),
        jnp.zeros((tok_rows, kv_local, group_size, head_dim), jnp.float32),
    )
    row_ids = jnp.arange(tok_rows, dtype=jnp.int32)
    state_now = attend(
        state_now, queries, keys_new, values_new, row_ids[None, :] <= row_ids[:, None]
    )
    all_seen = jnp.ones((1, tok_rows), bool)
    for distance in range(1, per_request):
        earlier_keys, earlier_values = shifted((keys_new, values_new), "seq", distance * req_count)
        state_now = lax.cond(
            local_part >= distance,
            lambda state_in: attend(state_in, queries, earlier_keys, earlier_values, all_seen),
            lambda state_in: state_in,
            state_now,
        )
    keys_piece = lax.all_gather(cache_keys, "seq", axis=1, tiled=True)
    values_piece = lax.all_gather(cache_values, "seq", axis=1, tiled=True)
    row_count = keys_piece.shape[1]
    keys_block = lax.dynamic_index_in_dim(keys_piece, group_id, 0, keepdims=False).reshape(
        row_count, kv_local, head_dim
    )
    values_block = lax.dynamic_index_in_dim(values_piece, group_id, 0, keepdims=False).reshape(
        row_count, kv_local, head_dim
    )
    visible = (jnp.arange(row_count, dtype=jnp.int32) < length)[None, :]
    state_now = lax.cond(
        jnp.int32(0) < length,
        lambda state_old: attend(state_old, queries, keys_block, values_block, visible),
        lambda state_old: state_old,
        state_now,
    )
    running_max, running_sum, running_acc = state_now
    mixed = (
        (running_acc / running_sum[..., None] * gates[..., None])
        .astype(jnp.bfloat16)
        .reshape(tok_rows, heads_local * head_dim)
    )
    partial_out = jnp.dot(mixed, w_out, preferred_element_type=jnp.float32)
    summed = lax.psum_scatter(
        partial_out.astype(jnp.bfloat16), "tp", scatter_dimension=1, tiled=True
    ).astype(jnp.float32)
    return (hidden_in.astype(jnp.float32) + summed).astype(jnp.bfloat16)


def solution(mesh):
    in_specs = (
        P("seq", "tp"),
        P(),
        P(None, "tp"),
        P(None, "tp"),
        P(None, "tp"),
        P(None, "tp"),
        P("tp", None),
        P(),
        P(),
        P(None, "seq", "tp"),
        P(None, "seq", "tp"),
        P(),
        P(),
    )
    out_specs = P("seq", "tp")
    return jax.shard_map(
        per_device, mesh=mesh, in_specs=in_specs, out_specs=out_specs, check_vma=False
    )
```

profile of v0, /device:TPU:1, one launch (start us, length us, event | category | flops | bytes accessed | tf_op | source)
XLA Modules:
  0.0 362.8 jit_solution(5019279901672864416)
XLA Ops:
  7.3 1.6 copy.86
  9.0 20.0 %all_gather.9 = bf16[128,2048]{1,0:T(8,128)(2,1)S(1)} all-gather(bf16[128,256]{1,0:T(8,128)(2,1)} %param.29), channel_id=1, replica_groups=mesh['seq'=64,'tp'=8] {'tp'}, dimensions={1}, use_global_device_ids=true | all-gather | bytes 589824 | tf_op jit(solution)/shard_map/all_gather | solution.py:82
  29.2 1.4 convolution_convert_fusion.1
  30.6 13.0 %collective-permute-start.9 = (bf16[128,1,128]{2,0,1:T(8,128)(2,1)S(1)}, bf16[128,1,128]{2,0,1:T(8,128)(2,1)S(1)}, u32[]{:S(2)}, u32[]{:S(2)}) collective-permute-start(bf16[128,1,128]{2,0,1:T(8,128)(2,1)S(1)} %bitcast.382), channel_id=1, source_target_pairs={{0,320},{8,328},{16,336},{24,344},{32,352},{40,360},{48,368},{56,3... | collective-permute-start | bytes 98312 | tf_op jit(solution)/shard_map/ppermute | solution.py:19
  43.7 1.3 collective-permute-start.7
  45.0 2.2 collective-permute-start.5
  47.2 1.3 collective-permute-start.3
  48.5 2.8 collective-permute-start.1
  51.4 1.6 fusion.139
  53.3 1.3 dynamic_slice.27
  55.4 1.5 multiply_reduce_fusion.1
  59.9 1.6 collective-permute-start.6
  61.5 10.6 %collective-permute-start.4 = (bf16[128,1,128]{0,2,1:T(8,128)(2,1)S(1)}, bf16[128,1,128]{0,2,1:T(8,128)(2,1)S(1)}, u32[]{:S(2)}, u32[]{:S(2)}) collective-permute-start(bf16[128,1,128]{0,2,1:T(8,128)(2,1)S(1)} %pad_maximum_fusion.1), channel_id=1, source_target_pairs={{0,192},{8,200},{16,208},{24,216},{32,224},{40,232},{48,240},{56,2... | collective-permute-start | bytes 98312 | tf_op jit(solution)/shard_map/ppermute | solution.py:19
  72.1 1.3 collective-permute-start.2
  73.4 2.8 collective-permute-start
  76.3 1.3 collective-permute-start.13
  77.6 1.3 collective-permute-start.11
  78.9 1.3 collective-permute-start.12
  80.2 1.3 collective-permute-start.10
  81.5 1.3 collective-permute-start.8
  83.9 75.0 %all-gather.3.cloned.1.call-done = bf16[2,8192,128]{2,1,0:T(8,128)(2,1)} async-done(((bf16[2,128,128]{2,1,0:T(8,128)(2,1)}), bf16[2,8192,128]{2,1,0:T(8,128)(2,1)}) %all-gather.3.cloned.1.call-update) | async-done | bytes 4194320 | tf_op jit(solution)/shard_map/all_gather | solution.py:127
  159.0 142.1 %all-gather.5.cloned.1.call-done = bf16[2,8192,128]{1,2,0:T(8,128)(2,1)} async-done(((bf16[2,128,128]{1,2,0:T(8,128)(2,1)}), bf16[2,8192,128]{1,2,0:T(8,128)(2,1)}) %all-gather.5.cloned.1.call-update) | async-done | bytes 4194320 | tf_op jit(solution)/shard_map/all_gather | solution.py:128
  302.4 52.4 %reduce-scatter.2.cloned.1.call-done = bf16[128,256]{1,0:T(8,128)(2,1)} async-done(((bf16[128,2048]{1,0:T(8,128)(2,1)}), bf16[128,256]{1,0:T(8,128)(2,1)}) %reduce-scatter.2.cloned.1.call-update) | async-done | bytes 65552 | tf_op jit(solution)/shard_map/reduce_scatter | solution.py:150
  354.8 1.5 add_convert_fusion
  (66 shorter events, 6.2 us)
Async XLA Ops:
  6.5 294.7 %copy-start = (bf16[256,2048]{1,0:T(8,128)(2,1)S(1)}, bf16[256,2048]{1,0:T(8,128)(2,1)}, u32[]{:S(2)}) copy-start(bf16[256,2048]{1,0:T(8,128)(2,1)} %param.35) | copy-start | bytes 3145732
  6.5 53.0 %copy-start.3 = (f32[2048]{0:T(1024)S(1)}, f32[2048]{0:T(1024)}, u32[]{:S(2)}) copy-start(f32[2048]{0:T(1024)} %param.30) | copy-start | bytes 24580
  6.5 53.0 %copy-start.4 = (bf16[2048,2]{0,1:T(2,128)(2,1)S(1)}, bf16[2048,2]{0,1:T(2,128)(2,1)}, u32[]{:S(2)}) copy-start(bf16[2048,2]{0,1:T(2,128)(2,1)} %param.34) | copy-start | bytes 24580
  6.5 294.6 %copy-start.5 = (s32[8]{0:T(128)S(1)}, s32[8]{0:T(128)}, u32[]{:S(2)}) copy-start(s32[8]{0:T(128)} %param.41) | copy-start | bytes 100
  6.5 152.4 %all-gather.3.cloned.1.call-start = ((), (), s32[]{:S(2)}) async-start(), calls=%async_computation.1 | async-start | bytes 4259840 | tf_op jit(solution)/shard_map/all_gather | solution.py:127
  7.3 293.8 %all-gather.5.cloned.1.call-start = ((), (), s32[]{:S(2)}) async-start(), calls=%async_computation.2 | async-start | bytes 4259840 | tf_op jit(solution)/shard_map/all_gather | solution.py:128
  8.9 345.9 %reduce-scatter.2.cloned.1.call-start = ((), (), s32[]{:S(2)}) async-start(), calls=%async_computation.3 | async-start | bytes 589824 | tf_op jit(solution)/shard_map/reduce_scatter | solution.py:150
  30.6 29.3 %collective-permute-start.9 = (bf16[128,1,128]{2,0,1:T(8,128)(2,1)S(1)}, bf16[128,1,128]{2,0,1:T(8,128)(2,1)S(1)}, u32[]{:S(2)}, u32[]{:S(2)}) collective-permute-start(bf16[128,1,128]{2,0,1:T(8,128)(2,1)S(1)} %bitcast.382), channel_id=1, source_target_pairs={{0,320},{8,328},{16,336},{24,344},{32,352},{40,360},{48,368},{56,3... | collective-permute-start | bytes 98312 | tf_op jit(solution)/shard_map/ppermute | solution.py:19
  43.7 17.8 %collective-permute-start.7 = (bf16[128,1,128]{2,0,1:T(8,128)(2,1)S(1)}, bf16[128,1,128]{2,0,1:T(8,128)(2,1)S(1)}, u32[]{:S(2)}, u32[]{:S(2)}) collective-permute-start(bf16[128,1,128]{2,0,1:T(8,128)(2,1)S(1)} %bitcast.383), channel_id=1, source_target_pairs={{0,256},{8,264},{16,272},{24,280},{32,288},{40,296},{48,304},{56,3... | collective-permute-start | bytes 98312 | tf_op jit(solution)/shard_map/ppermute | solution.py:19
  45.0 27.1 %collective-permute-start.5 = (bf16[128,1,128]{2,0,1:T(8,128)(2,1)S(1)}, bf16[128,1,128]{2,0,1:T(8,128)(2,1)S(1)}, u32[]{:S(2)}, u32[]{:S(2)}) collective-permute-start(bf16[128,1,128]{2,0,1:T(8,128)(2,1)S(1)} %bitcast.384), channel_id=1, source_target_pairs={{0,192},{8,200},{16,208},{24,216},{32,224},{40,232},{48,240},{56,2... | collective-permute-start | bytes 98312 | tf_op jit(solution)/shard_map/ppermute | solution.py:19
  47.2 26.2 %collective-permute-start.3 = (bf16[128,1,128]{2,0,1:T(8,128)(2,1)S(1)}, bf16[128,1,128]{2,0,1:T(8,128)(2,1)S(1)}, u32[]{:S(2)}, u32[]{:S(2)}) collective-permute-start(bf16[128,1,128]{2,0,1:T(8,128)(2,1)S(1)} %bitcast.385), channel_id=1, source_target_pairs={{0,128},{8,136},{16,144},{24,152},{32,160},{40,168},{48,176},{56,1... | collective-permute-start | bytes 98312 | tf_op jit(solution)/shard_map/ppermute | solution.py:19
  48.5 27.8 %collective-permute-start.1 = (bf16[128,1,128]{2,0,1:T(8,128)(2,1)S(1)}, bf16[128,1,128]{2,0,1:T(8,128)(2,1)S(1)}, u32[]{:S(2)}, u32[]{:S(2)}) collective-permute-start(bf16[128,1,128]{2,0,1:T(8,128)(2,1)S(1)} %bitcast.386), channel_id=1, source_target_pairs={{0,64},{8,72},{16,80},{24,88},{32,96},{40,104},{48,112},{56,120},{... | collective-permute-start | bytes 98312 | tf_op jit(solution)/shard_map/ppermute | solution.py:19
  59.9 17.7 %collective-permute-start.6 = (bf16[128,1,128]{0,2,1:T(8,128)(2,1)S(1)}, bf16[128,1,128]{0,2,1:T(8,128)(2,1)S(1)}, u32[]{:S(2)}, u32[]{:S(2)}) collective-permute-start(bf16[128,1,128]{0,2,1:T(8,128)(2,1)S(1)} %pad_maximum_fusion.1), channel_id=1, source_target_pairs={{0,256},{8,264},{16,272},{24,280},{32,288},{40,296},{48,304},{56,3... | collective-permute-start | bytes 98312 | tf_op jit(solution)/shard_map/ppermute | solution.py:19
  61.5 17.4 %collective-permute-start.4 = (bf16[128,1,128]{0,2,1:T(8,128)(2,1)S(1)}, bf16[128,1,128]{0,2,1:T(8,128)(2,1)S(1)}, u32[]{:S(2)}, u32[]{:S(2)}) collective-permute-start(bf16[128,1,128]{0,2,1:T(8,128)(2,1)S(1)} %pad_maximum_fusion.1), channel_id=1, source_target_pairs={{0,192},{8,200},{16,208},{24,216},{32,224},{40,232},{48,240},{56,2... | collective-permute-start | bytes 98312 | tf_op jit(solution)/shard_map/ppermute | solution.py:19
  72.1 8.1 %collective-permute-start.2 = (bf16[128,1,128]{0,2,1:T(8,128)(2,1)S(1)}, bf16[128,1,128]{0,2,1:T(8,128)(2,1)S(1)}, u32[]{:S(2)}, u32[]{:S(2)}) collective-permute-start(bf16[128,1,128]{0,2,1:T(8,128)(2,1)S(1)} %pad_maximum_fusion.1), channel_id=1, source_target_pairs={{0,128},{8,136},{16,144},{24,152},{32,160},{40,168},{48,176},{56,1... | collective-permute-start | bytes 98312 | tf_op jit(solution)/shard_map/ppermute | solution.py:19
  73.4 8.1 %collective-permute-start = (bf16[128,1,128]{0,2,1:T(8,128)(2,1)S(1)}, bf16[128,1,128]{0,2,1:T(8,128)(2,1)S(1)}, u32[]{:S(2)}, u32[]{:S(2)}) collective-permute-start(bf16[128,1,128]{0,2,1:T(8,128)(2,1)S(1)} %pad_maximum_fusion.1), channel_id=1, source_target_pairs={{0,64},{8,72},{16,80},{24,88},{32,96},{40,104},{48,112},{56,120},{... | collective-permute-start | bytes 98312 | tf_op jit(solution)/shard_map/ppermute | solution.py:19
  76.3 7.6 %collective-permute-start.13 = (bf16[128,1,128]{2,0,1:T(8,128)(2,1)S(1)}, bf16[128,1,128]{2,0,1:T(8,128)(2,1)S(1)}, u32[]{:S(2)}, u32[]{:S(2)}) collective-permute-start(bf16[128,1,128]{2,0,1:T(8,128)(2,1)S(1)} %bitcast.387), channel_id=1, source_target_pairs={{0,448},{8,456},{16,464},{24,472},{32,480},{40,488},{48,496},{56,5... | collective-permute-start | bytes 98312 | tf_op jit(solution)/shard_map/ppermute | solution.py:19
  77.6 6.2 %collective-permute-start.11 = (bf16[128,1,128]{2,0,1:T(8,128)(2,1)S(1)}, bf16[128,1,128]{2,0,1:T(8,128)(2,1)S(1)}, u32[]{:S(2)}, u32[]{:S(2)}) collective-permute-start(bf16[128,1,128]{2,0,1:T(8,128)(2,1)S(1)} %bitcast.388), channel_id=1, source_target_pairs={{0,384},{8,392},{16,400},{24,408},{32,416},{40,424},{48,432},{56,4... | collective-permute-start | bytes 98312 | tf_op jit(solution)/shard_map/ppermute | solution.py:19
  78.9 5.0 %collective-permute-start.12 = (bf16[128,1,128]{0,2,1:T(8,128)(2,1)S(1)}, bf16[128,1,128]{0,2,1:T(8,128)(2,1)S(1)}, u32[]{:S(2)}, u32[]{:S(2)}) collective-permute-start(bf16[128,1,128]{0,2,1:T(8,128)(2,1)S(1)} %pad_maximum_fusion.1), channel_id=1, source_target_pairs={{0,448},{8,456},{16,464},{24,472},{32,480},{40,488},{48,496},{56,5... | collective-permute-start | bytes 98312 | tf_op jit(solution)/shard_map/ppermute | solution.py:19
  80.2 3.6 collective-permute-start.10
  81.5 2.3 collective-permute-start.8
  301.1 53.7 %copy-start.2 = (bf16[128,256]{1,0:T(8,128)(2,1)S(1)}, bf16[128,256]{1,0:T(8,128)(2,1)}, u32[]{:S(2)}) copy-start(bf16[128,256]{1,0:T(8,128)(2,1)} %param.29) | copy-start | bytes 196612
Sparse Core Ops, SparseCore 0:
  10.3 148.5 all-gather.2
  161.9 139.1 all-gather.4
  303.9 50.8 reduce-scatter.1
where the time goes:
time: 364 us; the launch traced here: 363 us
  waiting for transfers between devices  270 us (74%)
  starting transfers between devices  43.5 us (12%)
  blocking collectives  20 us (5%)
  between operations  14.9 us (4%)
  matrix products  6.4 us (2%)
  other arithmetic  4.23 us (1%)
    all_gather x1, waiting for transfers between devices, per_device(): values_piece = lax.all_gather(cache_values, 'seq', axis=1, tiled=True)  142 us
    all_gather x1, waiting for transfers between devices, per_device(): keys_piece = lax.all_gather(cache_keys, 'seq', axis=1, tiled=True)  75 us
    reduce_scatter x1, waiting for transfers between devices, per_device(): lax.psum_scatter(partial_out.astype(jnp.bfloat16), 'tp', scatter_dimensio...  52.4 us
    ppermute x14, starting transfers between devices, shifted(): return lax.ppermute(value, axis, pairs)  43.4 us
    all_gather x1, blocking collectives, per_device(): gathered = lax.all_gather(hidden_in, 'tp', axis=1, tiled=True)  20 us
  transfers between devices with their start and end apart: 17, of which 3 were waited for; matrix products, arithmetic and copies ran while one was open for 3% of the time, Pallas kernels for 0%

commit v1 on v0

--- a/solution.py
+++ b/solution.py
@@ -124,15 +124,13 @@
             lambda state_in: state_in,
             state_now,
         )
-    keys_piece = lax.all_gather(cache_keys, "seq", axis=1, tiled=True)
-    values_piece = lax.all_gather(cache_values, "seq", axis=1, tiled=True)
-    row_count = keys_piece.shape[1]
-    keys_block = lax.dynamic_index_in_dim(keys_piece, group_id, 0, keepdims=False).reshape(
-        row_count, kv_local, head_dim
-    )
-    values_block = lax.dynamic_index_in_dim(values_piece, group_id, 0, keepdims=False).reshape(
-        row_count, kv_local, head_dim
-    )
+    peer_groups = group_of[jnp.arange(seq_size, dtype=jnp.int32) % req_count]
+    cache_both = jnp.stack([cache_keys, cache_values], 1)
+    outgoing = cache_both[peer_groups]
+    incoming = lax.all_to_all(outgoing, "seq", 0, 0, tiled=True)
+    row_count = seq_size * cache_keys.shape[1]
+    keys_block = incoming[:, 0].reshape(row_count, kv_local, head_dim)
+    values_block = incoming[:, 1].reshape(row_count, kv_local, head_dim)
     visible = (jnp.arange(row_count, dtype=jnp.int32) < length)[None, :]
     state_now = lax.cond(
         jnp.int32(0) < length,
@@ -147,9 +145,10 @@
         .reshape(tok_rows, heads_local * head_dim)
     )
     partial_out = jnp.dot(mixed, w_out, preferred_element_type=jnp.float32)
-    summed = lax.psum_scatter(
-        partial_out.astype(jnp.bfloat16), "tp", scatter_dimension=1, tiled=True
-    ).astype(jnp.float32)
+    tp_size = lax.axis_size("tp")
+    pieces = partial_out.astype(jnp.bfloat16).reshape(tok_rows, tp_size, -1)
+    arrived = lax.all_to_all(pieces, "tp", 1, 1, tiled=True)
+    summed = jnp.sum(arrived.astype(jnp.float32), 1)
     return (hidden_in.astype(jnp.float32) + summed).astype(jnp.bfloat16)
 
 

time: 364 us -> 290 us (0.80)
  the two profiles are of different devices: /device:TPU:1 before, /device:TPU:38 now
where the time goes in v1:
time: 290 us; the launch traced here: 289 us
  waiting for transfers between devices  177 us (61%)
  starting transfers between devices  48.9 us (17%)
  blocking collectives  28.3 us (10%)
  matrix products  14.4 us (5%)
  other arithmetic  10.2 us (4%)
  local copies, waits for them, and re-layouts  8.34 us (3%)
    ppermute x14, waiting for transfers between devices, shifted(): return lax.ppermute(value, axis, pairs)  177 us
    ppermute x14, starting transfers between devices, shifted(): return lax.ppermute(value, axis, pairs)  30.2 us
    all_to_all x1, starting transfers between devices, per_device(): incoming = lax.all_to_all(outgoing, 'seq', 0, 0, tiled=True)  18.7 us
    all_to_all x1, blocking collectives, per_device(): arrived = lax.all_to_all(pieces, 'tp', 1, 1, tiled=True)  14.7 us
    all_gather x1, blocking collectives, per_device(): gathered = lax.all_gather(hidden_in, 'tp', axis=1, tiled=True)  13.6 us
    dot_general x8, matrix products, attend(): jnp.einsum('tcgd,kcd->tcgk', queries, keys_block, preferred_element_type=...  7.27 us
  transfers between devices with their start and end apart: 15, of which 3 were waited for; matrix products, arithmetic and copies ran while one was open for 3% of the time, Pallas kernels for 0%

profile of v1, /device:TPU:38, one launch (start us, length us, event | category | flops | bytes accessed | tf_op | source)
XLA Modules:
  0.0 289.4 jit_solution(7387092435480790350)
XLA Ops:
  0.0 1.6 fusion.145
  1.6 4.9 %fusion.127 = s32[64]{0:T(128)S(1)} fusion(s32[]{:T(128)} %bitcast.147, s32[]{:T(128)} %bitcast.148, s32[]{:T(128)} %bitcast.149, s32[]{:T(128)} %bitcast.150, s32[]{:T(128)} %bitcast.151, s32[]{:T(128)} %bitcast.153, s32[]{:T(128)} %bitcast.152, s32[]{:T(128)} %bitcast.146), kind=kLoop, calls=%fused_computation.204 | loop fusion | flops 1664 | bytes 288 | tf_op jit(solution)/shard_map/select_n | solution.py:129
  7.5 3.0 %gather_fusion = bf16[64,2,128,128]{3,2,1,0:T(8,128)(2,1)} fusion(bf16[2,2,128,128]{3,2,1,0:T(8,128)(2,1)S(1)} %pad_maximum_fusion, s32[1024]{0:T(1024)S(1)} %pad_clamp_fusion), kind=kCustom, calls=%fused_computation | custom fusion | bytes 8388864 | tf_op jit(solution)/shard_map/gather | solution.py:129
  10.6 18.7 %all-to-all-start = ((bf16[64,2,128,128]{3,2,1,0:T(8,128)(2,1)}), bf16[64,2,128,128]{3,2,1,0:T(8,128)(2,1)}, u32[]{:S(2)}, u32[]{:S(2)}) async-start(bf16[64,2,128,128]{3,2,1,0:T(8,128)(2,1)} %gather_fusion), calls=%async_computation | async-start | bytes 8388608 | tf_op jit(solution)/shard_map/all_to_all | solution.py:130
  29.3 13.6 %all_gather.3 = bf16[128,2048]{1,0:T(8,128)(2,1)S(1)} all-gather(bf16[128,256]{1,0:T(8,128)(2,1)S(1)} %copy-done.1), channel_id=1, replica_groups=mesh['seq'=64,'tp'=8] {'tp'}, dimensions={1}, use_global_device_ids=true | all-gather | bytes 589824 | tf_op jit(solution)/shard_map/all_gather | solution.py:82
  43.1 1.4 convolution_convert_fusion.1
  44.5 1.3 collective-permute-start.9
  45.8 1.3 collective-permute-start.7
  47.1 1.3 collective-permute-start.5
  48.4 1.3 collective-permute-start.3
  49.7 11.2 %collective-permute-start.1 = (bf16[128,1,128]{2,0,1:T(8,128)(2,1)S(1)}, bf16[128,1,128]{2,0,1:T(8,128)(2,1)S(1)}, u32[]{:S(2)}, u32[]{:S(2)}) collective-permute-start(bf16[128,1,128]{2,0,1:T(8,128)(2,1)S(1)} %bitcast.427), channel_id=1, source_target_pairs={{0,64},{8,72},{16,80},{24,88},{32,96},{40,104},{48,112},{56,120},{... | collective-permute-start | bytes 98312 | tf_op jit(solution)/shard_map/ppermute | solution.py:19
  63.0 1.5 multiply_reduce_fusion.1
  66.2 156.3 %collective-permute-done.9 = bf16[128,1,128]{2,0,1:T(8,128)(2,1)S(1)} collective-permute-done((bf16[128,1,128]{2,0,1:T(8,128)(2,1)S(1)}, bf16[128,1,128]{2,0,1:T(8,128)(2,1)S(1)}, u32[]{:S(2)}, u32[]{:S(2)}) %collective-permute-start.9) | collective-permute-done | bytes 32800 | tf_op jit(solution)/shard_map/ppermute | solution.py:19
  223.8 1.3 collective-permute-start.4
  225.1 1.3 collective-permute-start.2
  226.4 4.7 %collective-permute-start = (bf16[128,1,128]{0,2,1:T(8,128)(2,1)S(1)}, bf16[128,1,128]{0,2,1:T(8,128)(2,1)S(1)}, u32[]{:S(2)}, u32[]{:S(2)}) collective-permute-start(bf16[128,1,128]{0,2,1:T(8,128)(2,1)S(1)} %pad_maximum_fusion.2), channel_id=1, source_target_pairs={{0,64},{8,72},{16,80},{24,88},{32,96},{40,104},{48,112},{56,120},{... | collective-permute-start | bytes 98312 | tf_op jit(solution)/shard_map/ppermute | solution.py:19
  233.1 7.7 %collective-permute-done.4 = bf16[128,1,128]{0,2,1:T(8,128)(2,1)S(1)} collective-permute-done((bf16[128,1,128]{0,2,1:T(8,128)(2,1)S(1)}, bf16[128,1,128]{0,2,1:T(8,128)(2,1)S(1)}, u32[]{:S(2)}, u32[]{:S(2)}) %collective-permute-start.4) | collective-permute-done | bytes 32800 | tf_op jit(solution)/shard_map/ppermute | solution.py:19
  242.8 1.3 collective-permute-start.8
  247.2 13.3 %collective-permute-done.8 = bf16[128,1,128]{0,2,1:T(8,128)(2,1)S(1)} collective-permute-done((bf16[128,1,128]{0,2,1:T(8,128)(2,1)S(1)}, bf16[128,1,128]{0,2,1:T(8,128)(2,1)S(1)}, u32[]{:S(2)}, u32[]{:S(2)}) %collective-permute-start.8) | collective-permute-done | bytes 32800 | tf_op jit(solution)/shard_map/ppermute | solution.py:19
  261.7 12.0 %conditional.15 = (f32[128,1,2]{0,2,1:T(2,128)S(1)}, f32[128,1,2,128]{0,3,2,1:T(8,128)S(1)}) conditional(s32[]{:T(128)} %convert_element_type.104, (f32[128,1,2]{0,2,1:T(2,128)S(1)}, f32[128,1,2,128]{3,0,2,1:T(8,128)S(1)}) %tuple.63, (s32[]{:T(128)}, s32[8192]{0:T(1024)S(1)}, bf16[64,2,128,128]{3,2,1,0:T(8,128)(2,1)}, ...), branch_computations={%region_33.34_spmd, %region_34.37_spmd} | conditional | flops 1088496640 | bytes 38402068 | solution.py:135
  262.4 2.6 fusion.136
  265.0 5.7 %fusion.137 = (f32[128,2]{0,1:T(2,128)S(1)}, f32[128,1,2,8192]{0,3,2,1:T(8,128)S(1)}) fusion(bf16[8192,128,1]{1,0,2:T(8,128)(2,1)S(1)} %bitcast.411, bf16[128,1,2,128]{3,0,2,1:T(8,128)(2,1)S(1)} %get-tuple-element.203, pred[8192]{0:T(1024)(128)(4,1)S(1)} %broadcast_compare_fusion), kind=kOutput, calls=%fused_computation.215 | convolution fusion | flops 543162112 | bytes 10560512 | tf_op jit(solution)/shard_map/cond/branch_1_fun/tcgd,kcd->tcgk/dot_general | solution.py:42
  270.7 1.7 fusion.89
  274.1 14.7 %all_to_all.10 = bf16[128,8,256]{2,0,1:T(8,128)(2,1)S(1)} all-to-all(bf16[128,8,256]{2,0,1:T(8,128)(2,1)S(1)} %bitcast.414), channel_id=1, replica_groups=mesh['seq'=64,'tp'=8] {'tp'}, dimensions={1} | all-to-all | bytes 1048576 | tf_op jit(solution)/shard_map/all_to_all | solution.py:150
  (115 shorter events, 18.9 us)
Async XLA Ops:
  0.0 273.7 %copy-start = (bf16[256,2048]{1,0:T(8,128)(2,1)S(1)}, bf16[256,2048]{1,0:T(8,128)(2,1)}, u32[]{:S(2)}) copy-start(bf16[256,2048]{1,0:T(8,128)(2,1)} %param.35) | copy-start | bytes 3145732
  10.6 18.7 %copy-start.1 = (bf16[128,256]{1,0:T(8,128)(2,1)S(1)}, bf16[128,256]{1,0:T(8,128)(2,1)}, u32[]{:S(2)}) copy-start(bf16[128,256]{1,0:T(8,128)(2,1)} %param.29) | copy-start | bytes 196612
  10.6 32.6 %copy-start.5 = (f32[2048]{0:T(1024)S(1)}, f32[2048]{0:T(1024)}, u32[]{:S(2)}) copy-start(f32[2048]{0:T(1024)} %param.30) | copy-start | bytes 24580
  10.6 50.5 %copy-start.4 = (bf16[2048,256]{1,0:T(8,128)(2,1)S(1)}, bf16[2048,256]{1,0:T(8,128)(2,1)}, u32[]{:S(2)}) copy-start(bf16[2048,256]{1,0:T(8,128)(2,1)} %param.31) | copy-start | bytes 3145732
  10.6 251.1 %all-to-all-start = ((bf16[64,2,128,128]{3,2,1,0:T(8,128)(2,1)}), bf16[64,2,128,128]{3,2,1,0:T(8,128)(2,1)}, u32[]{:S(2)}, u32[]{:S(2)}) async-start(bf16[64,2,128,128]{3,2,1,0:T(8,128)(2,1)} %gather_fusion), calls=%async_computation | async-start | bytes 8388608 | tf_op jit(solution)/shard_map/all_to_all | solution.py:130
  29.2 32.5 %copy-start.7 = (s32[8]{0:T(128)S(1)}, s32[8]{0:T(128)}, u32[]{:S(2)}) copy-start(s32[8]{0:T(128)} %param.40) | copy-start | bytes 100
  29.3 35.3 %copy-start.2 = (f32[128]{0:T(128)S(1)}, f32[128]{0:T(128)}, u32[]{:S(2)}) copy-start(f32[128]{0:T(128)} %param.37) | copy-start | bytes 1540
  29.3 35.9 %copy-start.3 = (f32[128]{0:T(128)S(1)}, f32[128]{0:T(128)}, u32[]{:S(2)}) copy-start(f32[128]{0:T(128)} %param.36) | copy-start | bytes 1540
  29.3 36.6 %copy-start.6 = (bf16[2048,2]{0,1:T(2,128)(2,1)S(1)}, bf16[2048,2]{0,1:T(2,128)(2,1)}, u32[]{:S(2)}) copy-start(bf16[2048,2]{0,1:T(2,128)(2,1)} %param.34) | copy-start | bytes 24580
  44.5 178.0 %collective-permute-start.9 = (bf16[128,1,128]{2,0,1:T(8,128)(2,1)S(1)}, bf16[128,1,128]{2,0,1:T(8,128)(2,1)S(1)}, u32[]{:S(2)}, u32[]{:S(2)}) collective-permute-start(bf16[128,1,128]{2,0,1:T(8,128)(2,1)S(1)} %bitcast.423), channel_id=1, source_target_pairs={{0,320},{8,328},{16,336},{24,344},{32,352},{40,360},{48,368},{56,3... | collective-permute-start | bytes 98312 | tf_op jit(solution)/shard_map/ppermute | solution.py:19
  45.8 177.9 %collective-permute-start.7 = (bf16[128,1,128]{2,0,1:T(8,128)(2,1)S(1)}, bf16[128,1,128]{2,0,1:T(8,128)(2,1)S(1)}, u32[]{:S(2)}, u32[]{:S(2)}) collective-permute-start(bf16[128,1,128]{2,0,1:T(8,128)(2,1)S(1)} %bitcast.424), channel_id=1, source_target_pairs={{0,256},{8,264},{16,272},{24,280},{32,288},{40,296},{48,304},{56,3... | collective-permute-start | bytes 98312 | tf_op jit(solution)/shard_map/ppermute | solution.py:19
  47.1 178.0 %collective-permute-start.5 = (bf16[128,1,128]{2,0,1:T(8,128)(2,1)S(1)}, bf16[128,1,128]{2,0,1:T(8,128)(2,1)S(1)}, u32[]{:S(2)}, u32[]{:S(2)}) collective-permute-start(bf16[128,1,128]{2,0,1:T(8,128)(2,1)S(1)} %bitcast.425), channel_id=1, source_target_pairs={{0,192},{8,200},{16,208},{24,216},{32,224},{40,232},{48,240},{56,2... | collective-permute-start | bytes 98312 | tf_op jit(solution)/shard_map/ppermute | solution.py:19
  48.4 178.0 %collective-permute-start.3 = (bf16[128,1,128]{2,0,1:T(8,128)(2,1)S(1)}, bf16[128,1,128]{2,0,1:T(8,128)(2,1)S(1)}, u32[]{:S(2)}, u32[]{:S(2)}) collective-permute-start(bf16[128,1,128]{2,0,1:T(8,128)(2,1)S(1)} %bitcast.426), channel_id=1, source_target_pairs={{0,128},{8,136},{16,144},{24,152},{32,160},{40,168},{48,176},{56,1... | collective-permute-start | bytes 98312 | tf_op jit(solution)/shard_map/ppermute | solution.py:19
  49.7 181.4 %collective-permute-start.1 = (bf16[128,1,128]{2,0,1:T(8,128)(2,1)S(1)}, bf16[128,1,128]{2,0,1:T(8,128)(2,1)S(1)}, u32[]{:S(2)}, u32[]{:S(2)}) collective-permute-start(bf16[128,1,128]{2,0,1:T(8,128)(2,1)S(1)} %bitcast.427), channel_id=1, source_target_pairs={{0,64},{8,72},{16,80},{24,88},{32,96},{40,104},{48,112},{56,120},{... | collective-permute-start | bytes 98312 | tf_op jit(solution)/shard_map/ppermute | solution.py:19
  222.5 9.3 %collective-permute-start.6 = (bf16[128,1,128]{0,2,1:T(8,128)(2,1)S(1)}, bf16[128,1,128]{0,2,1:T(8,128)(2,1)S(1)}, u32[]{:S(2)}, u32[]{:S(2)}) collective-permute-start(bf16[128,1,128]{0,2,1:T(8,128)(2,1)S(1)} %pad_maximum_fusion.2), channel_id=1, source_target_pairs={{0,256},{8,264},{16,272},{24,280},{32,288},{40,296},{48,304},{56,3... | collective-permute-start | bytes 98312 | tf_op jit(solution)/shard_map/ppermute | solution.py:19
  223.8 17.1 %collective-permute-start.4 = (bf16[128,1,128]{0,2,1:T(8,128)(2,1)S(1)}, bf16[128,1,128]{0,2,1:T(8,128)(2,1)S(1)}, u32[]{:S(2)}, u32[]{:S(2)}) collective-permute-start(bf16[128,1,128]{0,2,1:T(8,128)(2,1)S(1)} %pad_maximum_fusion.2), channel_id=1, source_target_pairs={{0,192},{8,200},{16,208},{24,216},{32,224},{40,232},{48,240},{56,2... | collective-permute-start | bytes 98312 | tf_op jit(solution)/shard_map/ppermute | solution.py:19
  225.1 16.4 %collective-permute-start.2 = (bf16[128,1,128]{0,2,1:T(8,128)(2,1)S(1)}, bf16[128,1,128]{0,2,1:T(8,128)(2,1)S(1)}, u32[]{:S(2)}, u32[]{:S(2)}) collective-permute-start(bf16[128,1,128]{0,2,1:T(8,128)(2,1)S(1)} %pad_maximum_fusion.2), channel_id=1, source_target_pairs={{0,128},{8,136},{16,144},{24,152},{32,160},{40,168},{48,176},{56,1... | collective-permute-start | bytes 98312 | tf_op jit(solution)/shard_map/ppermute | solution.py:19
  226.4 16.4 %collective-permute-start = (bf16[128,1,128]{0,2,1:T(8,128)(2,1)S(1)}, bf16[128,1,128]{0,2,1:T(8,128)(2,1)S(1)}, u32[]{:S(2)}, u32[]{:S(2)}) collective-permute-start(bf16[128,1,128]{0,2,1:T(8,128)(2,1)S(1)} %pad_maximum_fusion.2), channel_id=1, source_target_pairs={{0,64},{8,72},{16,80},{24,88},{32,96},{40,104},{48,112},{56,120},{... | collective-permute-start | bytes 98312 | tf_op jit(solution)/shard_map/ppermute | solution.py:19
  231.2 30.4 %collective-permute-start.13 = (bf16[128,1,128]{2,0,1:T(8,128)(2,1)S(1)}, bf16[128,1,128]{2,0,1:T(8,128)(2,1)S(1)}, u32[]{:S(2)}, u32[]{:S(2)}) collective-permute-start(bf16[128,1,128]{2,0,1:T(8,128)(2,1)S(1)} %bitcast.428), channel_id=1, source_target_pairs={{0,448},{8,456},{16,464},{24,472},{32,480},{40,488},{48,496},{56,5... | collective-permute-start | bytes 98312 | tf_op jit(solution)/shard_map/ppermute | solution.py:19
  231.8 29.2 %collective-permute-start.11 = (bf16[128,1,128]{2,0,1:T(8,128)(2,1)S(1)}, bf16[128,1,128]{2,0,1:T(8,128)(2,1)S(1)}, u32[]{:S(2)}, u32[]{:S(2)}) collective-permute-start(bf16[128,1,128]{2,0,1:T(8,128)(2,1)S(1)} %bitcast.429), channel_id=1, source_target_pairs={{0,384},{8,392},{16,400},{24,408},{32,416},{40,424},{48,432},{56,4... | collective-permute-start | bytes 98312 | tf_op jit(solution)/shard_map/ppermute | solution.py:19
  240.8 20.8 %collective-permute-start.12 = (bf16[128,1,128]{0,2,1:T(8,128)(2,1)S(1)}, bf16[128,1,128]{0,2,1:T(8,128)(2,1)S(1)}, u32[]{:S(2)}, u32[]{:S(2)}) collective-permute-start(bf16[128,1,128]{0,2,1:T(8,128)(2,1)S(1)} %pad_maximum_fusion.2), channel_id=1, source_target_pairs={{0,448},{8,456},{16,464},{24,472},{32,480},{40,488},{48,496},{56,5... | collective-permute-start | bytes 98312 | tf_op jit(solution)/shard_map/ppermute | solution.py:19
  241.5 19.5 %collective-permute-start.10 = (bf16[128,1,128]{0,2,1:T(8,128)(2,1)S(1)}, bf16[128,1,128]{0,2,1:T(8,128)(2,1)S(1)}, u32[]{:S(2)}, u32[]{:S(2)}) collective-permute-start(bf16[128,1,128]{0,2,1:T(8,128)(2,1)S(1)} %pad_maximum_fusion.2), channel_id=1, source_target_pairs={{0,384},{8,392},{16,400},{24,408},{32,416},{40,424},{48,432},{56,4... | collective-permute-start | bytes 98312 | tf_op jit(solution)/shard_map/ppermute | solution.py:19
  242.8 17.7 %collective-permute-start.8 = (bf16[128,1,128]{0,2,1:T(8,128)(2,1)S(1)}, bf16[128,1,128]{0,2,1:T(8,128)(2,1)S(1)}, u32[]{:S(2)}, u32[]{:S(2)}) collective-permute-start(bf16[128,1,128]{0,2,1:T(8,128)(2,1)S(1)} %pad_maximum_fusion.2), channel_id=1, source_target_pairs={{0,320},{8,328},{16,336},{24,344},{32,352},{40,360},{48,368},{56,3... | collective-permute-start | bytes 98312 | tf_op jit(solution)/shard_map/ppermute | solution.py:19

commit v2 on v1

--- a/solution.py
+++ b/solution.py
@@ -3,7 +3,7 @@
 import jax
 import jax.numpy as jnp
 from jax import lax
-from jax.sharding import PartitionSpec as P
+from jax.sharding import Mesh, PartitionSpec as P
 
 SPAN = 1024
 
@@ -77,18 +77,31 @@
     heads_local = w_query.shape[1] // head_dim
     group_size = heads_local // kv_local
     per_request = SPAN // tok_rows
-    seq_size = lax.axis_size("seq")
-    req_count = seq_size // per_request
+    ring_x = lax.axis_size("sx")
+    ring_z = lax.axis_size("sz")
+    req_count = ring_x * ring_z // per_request
+    pair = ring_z // req_count
+    x_index = lax.axis_index("sx")
+    z_index = lax.axis_index("sz")
+    seq_index = x_index * ring_z + z_index
+    request = seq_index % req_count
+    local_part = seq_index // req_count
+    parity = z_index // req_count
+    length = cached_len[request]
+
+    peer_groups = group_of[jnp.arange(ring_z, dtype=jnp.int32) % req_count]
+    cache_both = jnp.stack([cache_keys, cache_values], 1)
+    incoming = lax.all_to_all(cache_both[peer_groups], "sz", 0, 0, tiled=True)
+    cache_rows = ring_z * cache_keys.shape[1]
+    keys_cache = incoming[:, 0].reshape(cache_rows, kv_local, head_dim)
+    values_cache = incoming[:, 1].reshape(cache_rows, kv_local, head_dim)
+    cache_pos = x_index * cache_rows + jnp.arange(cache_rows, dtype=jnp.int32)
+
     gathered = lax.all_gather(hidden_in, "tp", axis=1, tiled=True)
     widened = gathered.astype(jnp.float32)
     normed = (
         widened * lax.rsqrt(jnp.mean(widened * widened, -1, keepdims=True) + norm_eps) * norm_gain
     ).astype(jnp.bfloat16)
-    seq_index = lax.axis_index("seq")
-    local_part = seq_index // req_count
-    request = seq_index % req_count
-    length = cached_len[request]
-    group_id = group_of[request]
     positions = length + local_part * tok_rows + jnp.arange(tok_rows, dtype=jnp.int32)
     query_raw = jnp.dot(normed, w_query, preferred_element_type=jnp.float32).reshape(
         tok_rows, kv_local, group_size, head_dim
@@ -106,41 +119,48 @@
     gates = jax.nn.sigmoid(jnp.dot(normed, w_headgate, preferred_element_type=jnp.float32)).reshape(
         tok_rows, kv_local, group_size
     )
-    state_now = (
-        jnp.full((tok_rows, kv_local, group_size), masked_score, jnp.float32),
-        jnp.zeros((tok_rows, kv_local, group_size), jnp.float32),
-        jnp.zeros((tok_rows, kv_local, group_size, head_dim), jnp.float32),
-    )
+
+    partner_pairs = [(z, (z + req_count) % ring_z) for z in range(ring_z)]
+    partner_keys, partner_values = lax.ppermute((keys_new, values_new), "sz", partner_pairs)
+    partner_part = x_index * pair + (pair - 1 - parity)
+    all_queries = lax.all_gather(queries, "sx", axis=0, tiled=True)
+    query_tok = (
+        (jnp.arange(ring_x, dtype=jnp.int32) * pair + parity)[:, None] * tok_rows
+        + jnp.arange(tok_rows, dtype=jnp.int32)[None, :]
+    ).reshape(-1)
     row_ids = jnp.arange(tok_rows, dtype=jnp.int32)
-    state_now = attend(
-        state_now, queries, keys_new, values_new, row_ids[None, :] <= row_ids[:, None]
-    )
-    all_seen = jnp.ones((1, tok_rows), bool)
-    for distance in range(1, per_request):
-        earlier_keys, earlier_values = shifted((keys_new, values_new), "seq", distance * req_count)
-        state_now = lax.cond(
-            local_part >= distance,
-            lambda state_in: attend(state_in, queries, earlier_keys, earlier_values, all_seen),
-            lambda state_in: state_in,
-            state_now,
-        )
-    peer_groups = group_of[jnp.arange(seq_size, dtype=jnp.int32) % req_count]
-    cache_both = jnp.stack([cache_keys, cache_values], 1)
-    outgoing = cache_both[peer_groups]
-    incoming = lax.all_to_all(outgoing, "seq", 0, 0, tiled=True)
-    row_count = seq_size * cache_keys.shape[1]
-    keys_block = incoming[:, 0].reshape(row_count, kv_local, head_dim)
-    values_block = incoming[:, 1].reshape(row_count, kv_local, head_dim)
-    visible = (jnp.arange(row_count, dtype=jnp.int32) < length)[None, :]
-    state_now = lax.cond(
-        jnp.int32(0) < length,
-        lambda state_old: attend(state_old, queries, keys_block, values_block, visible),
-        lambda state_old: state_old,
-        state_now,
-    )
-    running_max, running_sum, running_acc = state_now
+    key_tok = jnp.concatenate([local_part * tok_rows + row_ids, partner_part * tok_rows + row_ids])
+    keys_all = jnp.concatenate([keys_cache, keys_new, partner_keys], 0)
+    values_all = jnp.concatenate([values_cache, values_new, partner_values], 0)
+    query_count = query_tok.shape[0]
+    visible = jnp.concatenate(
+        [
+            jnp.broadcast_to((cache_pos < length)[None, :], (query_count, cache_rows)),
+            key_tok[None, :] <= query_tok[:, None],
+        ],
+        1,
+    )
+    scores = jnp.einsum(
+        "tcgd,kcd->tcgk", all_queries, keys_all, preferred_element_type=jnp.float32
+    ) * head_dim ** (-0.5)
+    seen = visible[:, None, None, :]
+    scores = jnp.where(seen, scores, masked_score)
+    top = jnp.max(scores, -1)
+    expo = jnp.where(seen, jnp.exp(scores - top[..., None]), 0.0)
+    total = jnp.sum(expo, -1)
+    acc = jnp.einsum(
+        "tcgk,kcd->tcgd", expo.astype(jnp.bfloat16), values_all, preferred_element_type=jnp.float32
+    )
+    stats = jnp.stack([top, total], -1).reshape(ring_x, tok_rows, kv_local, group_size, 2)
+    acc = acc.reshape(ring_x, tok_rows, kv_local, group_size, head_dim)
+    stats_in = lax.all_to_all(stats, "sx", 0, 0, tiled=True)
+    acc_in = lax.all_to_all(acc, "sx", 0, 0, tiled=True)
+    best = jnp.max(stats_in[..., 0], 0)
+    factor = jnp.exp(stats_in[..., 0] - best[None])
+    total = jnp.sum(stats_in[..., 1] * factor, 0)
+    summed_acc = jnp.sum(acc_in * factor[..., None], 0)
     mixed = (
-        (running_acc / running_sum[..., None] * gates[..., None])
+        (summed_acc / total[..., None] * gates[..., None])
         .astype(jnp.bfloat16)
         .reshape(tok_rows, heads_local * head_dim)
     )
@@ -153,8 +173,15 @@
 
 
 def solution(mesh):
+    seq_size = mesh.shape["seq"]
+    tp_size = mesh.shape["tp"]
+    req_count = seq_size // (SPAN // 128)
+    ring_z = 2 * req_count
+    ring_x = seq_size // ring_z
+    split_mesh = Mesh(mesh.devices.reshape(ring_x, ring_z, tp_size), ("sx", "sz", "tp"))
+    seq = ("sx", "sz")
     in_specs = (
-        P("seq", "tp"),
+        P(seq, "tp"),
         P(),
         P(None, "tp"),
         P(None, "tp"),
@@ -163,12 +190,12 @@
         P("tp", None),
         P(),
         P(),
-        P(None, "seq", "tp"),
-        P(None, "seq", "tp"),
-        P(),
-        P(),
-    )
-    out_specs = P("seq", "tp")
+        P(None, seq, "tp"),
+        P(None, seq, "tp"),
+        P(),
+        P(),
+    )
+    out_specs = P(seq, "tp")
     return jax.shard_map(
-        per_device, mesh=mesh, in_specs=in_specs, out_specs=out_specs, check_vma=False
-    )
+        per_device, mesh=split_mesh, in_specs=in_specs, out_specs=out_specs, check_vma=False
+    )

time: 290 us -> 156 us (0.54)
  the two profiles are of different devices: /device:TPU:38 before, /device:TPU:1 now
where the time goes in v2:
time: 156 us; the launch traced here: 155 us
  blocking collectives  48.2 us (31%)
  starting transfers between devices  35.6 us (23%)
  waiting for transfers between devices  24.7 us (16%)
  matrix products  17.6 us (11%)
  local copies, waits for them, and re-layouts  14 us (9%)
  other arithmetic  13.5 us (9%)
    ppermute x2, starting transfers between devices, per_device(): lax.ppermute((keys_new, values_new), 'sz', partner_pairs)  22.5 us
    all_gather x1, blocking collectives, per_device(): gathered = lax.all_gather(hidden_in, 'tp', axis=1, tiled=True)  20.2 us
    ppermute x2, waiting for transfers between devices, per_device(): lax.ppermute((keys_new, values_new), 'sz', partner_pairs)  17.8 us
    all_to_all x1, blocking collectives, per_device(): arrived = lax.all_to_all(pieces, 'tp', 1, 1, tiled=True)  17.2 us
    all_gather x1, blocking collectives, per_device(): all_queries = lax.all_gather(queries, 'sx', axis=0, tiled=True)  10.9 us
    all_to_all x1, waiting for transfers between devices, per_device(): acc_in = lax.all_to_all(acc, 'sx', 0, 0, tiled=True)  6.88 us
    dot_general x1, matrix products, per_device(): jnp.einsum('tcgd,kcd->tcgk', all_queries, keys_all, preferred_element_typ...  6.72 us
    reduce_sum x1, other arithmetic, per_device(): total = jnp.sum(expo, -1)  6.14 us
  transfers between devices with their start and end apart: 5, of which 2 were waited for; matrix products, arithmetic and copies ran while one was open for 17% of the time, Pallas kernels for 0%

profile of v2, /device:TPU:1, one launch (start us, length us, event | category | flops | bytes accessed | tf_op | source)
XLA Modules:
  0.0 154.6 jit_solution(10557558886728345072)
XLA Ops:
  0.0 20.2 %all_gather.6 = bf16[128,2048]{1,0:T(8,128)(2,1)S(1)} all-gather(bf16[128,256]{1,0:T(8,128)(2,1)} %param.13), channel_id=1, replica_groups=mesh['sx'=4,'sz'=16,'tp'=8] {'tp'}, dimensions={1}, use_global_device_ids=true | all-gather | bytes 589824 | tf_op jit(solution)/shard_map/all_gather | solution.py:100
  20.4 2.0 %fusion.10 = bf16[128,1,128]{2,0,1:T(8,128)(2,1)} fusion(bf16[2048,128]{1,0:T(8,128)(2,1)} %param.17, bf16[128,2048]{1,0:T(8,128)(2,1)S(1)} %all_gather.6, f32[2048]{0:T(1024)} %param.14, f32[128]{0:T(128)S(1)} %add_rsqrt_fusion.2), kind=kOutput, calls=%fused_computation.16 | convolution fusion | flops 68173824 | bytes 1090048 | tf_op jit(solution)/shard_map/dot_general | solution.py:115
  22.4 10.6 %collective-permute-start = (bf16[128,1,128]{2,0,1:T(8,128)(2,1)}, bf16[128,1,128]{2,0,1:T(8,128)(2,1)}, u32[]{:S(2)}, u32[]{:S(2)}) collective-permute-start(bf16[128,1,128]{2,0,1:T(8,128)(2,1)} %fusion.10), channel_id=1, source_target_pairs={{0,64},{8,72},{16,80},{24,88},{32,96},{40,104},{48,112},{56,120},{... | collective-permute-start | bytes 98312 | tf_op jit(solution)/shard_map/ppermute | solution.py:124
  33.0 1.3 gather_fusion
  35.3 1.7 %gather_fusion.1 = bf16[16,2,128,128]{3,2,1,0:T(8,128)(2,1)} fusion(bf16[2,2,128,128]{3,2,0,1:T(8,128)(2,1)S(1)} %pad_maximum_fusion, s32[1024]{0:T(1024)S(1)} %pad_clamp_fusion), kind=kCustom, calls=%fused_computation.1 | custom fusion | bytes 2097216 | tf_op jit(solution)/shard_map/gather | solution.py:94
  36.9 4.9 %all-to-all-start = ((bf16[16,2,128,128]{3,2,1,0:T(8,128)(2,1)}), bf16[16,2,128,128]{3,2,1,0:T(8,128)(2,1)S(1)}, u32[]{:S(2)}, u32[]{:S(2)}) async-start(bf16[16,2,128,128]{3,2,1,0:T(8,128)(2,1)} %gather_fusion.1), calls=%async_computation | async-start | bytes 2097152 | tf_op jit(solution)/shard_map/all_to_all | solution.py:94
  43.6 1.5 multiply_reduce_fusion.2
  46.7 11.9 %collective-permute-start.1 = (bf16[128,1,128]{0,2,1:T(8,128)(2,1)}, bf16[128,1,128]{0,2,1:T(8,128)(2,1)}, u32[]{:S(2)}, u32[]{:S(2)}) collective-permute-start(bf16[128,1,128]{0,2,1:T(8,128)(2,1)} %pad_maximum_fusion.2), channel_id=1, source_target_pairs={{0,64},{8,72},{16,80},{24,88},{32,96},{40,104},{48,112},{56,120},{... | collective-permute-start | bytes 98312 | tf_op jit(solution)/shard_map/ppermute | solution.py:124
  58.7 1.6 %fusion.49 = f32[128,256]{1,0:T(8,128)S(1)} fusion(bf16[2048,256]{1,0:T(8,128)(2,1)} %param.15, bf16[128,2048]{1,0:T(8,128)(2,1)S(1)} %all_gather.6, f32[2048]{0:T(1024)} %param.14, f32[128]{0:T(128)S(1)} %add_rsqrt_fusion.2), kind=kOutput, calls=%fused_computation.98 | convolution fusion | flops 135266304 | bytes 1712640 | tf_op jit(solution)/shard_map/dot_general | solution.py:106
  62.5 2.2 %pad_add_fusion = pred[512,2304]{0,1:T(8,128)(4,1)S(1)} fusion(pred[512,256]{0,1:T(8,128)(4,1)S(1)} %broadcast_compare_fusion, pred[2304]{0:T(1024)(128)(4,1)S(1)} %pad.9.clone), kind=kLoop, calls=%fused_computation.9 | loop fusion | flops 1179648 | bytes 1313024 | tf_op jit(solution)/shard_map/concatenate | solution.py:136
  64.7 10.9 %all_gather.7 = bf16[512,1,2,128]{3,0,2,1:T(8,128)(2,1)S(1)} all-gather(bf16[128,1,2,128]{3,0,2,1:T(8,128)(2,1)S(1)} %pad_maximum_fusion.1), channel_id=1, replica_groups=mesh['sx'=4,'sz'=16,'tp'=8] {'sx'}, dimensions={0}, use_global_device_ids=true | all-gather | bytes 327680 | tf_op jit(solution)/shard_map/all_gather | solution.py:126
  75.7 1.5 copy.58
  77.1 1.5 copy.60
  78.6 1.5 copy.59
  80.0 17.8 %collective-permute-done.1 = bf16[128,1,128]{0,2,1:T(8,128)(2,1)} collective-permute-done((bf16[128,1,128]{0,2,1:T(8,128)(2,1)}, bf16[128,1,128]{0,2,1:T(8,128)(2,1)}, u32[]{:S(2)}, u32[]{:S(2)}) %collective-permute-start.1) | collective-permute-done | bytes 32800 | tf_op jit(solution)/shard_map/ppermute | solution.py:124
  97.8 1.5 copy.61
  100.3 1.2 copy.72
  101.6 6.7 %fusion = (f32[512,2]{0,1:T(2,128)S(1)}, f32[2304,512,2]{1,0,2:T(8,128)}) fusion(pred[512,2304]{0,1:T(8,128)(4,1)S(1)} %pad_add_fusion, bf16[512,1,2,128]{3,0,2,1:T(8,128)(2,1)S(1)} %all_gather.7, bf16[128,1,128]{2,0,1:T(8,128)(2,1)} %copy.61, bf16[128,1,128]{2,0,1:T(8,128)(2,1)} %copy.60, bf16[2048,1,128]{2,0,1:T(8,128)(2,1)} %bitcast.102), kind=kOutput, calls=%fused_computation.4 | convolution fusion | flops 612826112 | bytes 11472896 | tf_op jit(solution)/shard_map/tcgd,kcd->tcgk/dot_general | solution.py:143
  108.4 6.1 %fusion.1 = f32[512,2]{0,1:T(2,128)S(1)} fusion(f32[2304,512,2]{1,0,2:T(8,128)} %get-tuple-element.16, f32[512,2]{0,1:T(2,128)S(1)} %get-tuple-element.15, pred[512,2304]{0,1:T(8,128)(4,1)S(1)} %pad_add_fusion), kind=kLoop, calls=%fused_computation.5 | loop fusion | flops 11795456 | bytes 10625024 | tf_op jit(solution)/shard_map/reduce_sum | solution.py:150
  115.1 4.0 %all-to-all-start.2 = ((f32[4,128,1,2,2]{1,3,4,2,0:T(2,128)}), f32[4,128,1,2,2]{1,3,4,2,0:T(2,128)S(1)}, u32[]{:S(2)}, u32[]{:S(2)}) async-start(f32[4,128,1,2,2]{1,3,4,2,0:T(2,128)} %copy.66), calls=%async_computation.2 | async-start | bytes 16384 | tf_op jit(solution)/shard_map/all_to_all | solution.py:156
  119.1 5.1 %fusion.7 = f32[1,2,16,4,8,128]{5,4,3,2,1,0:T(8,128)S(1)} fusion(f32[2304,512,2]{1,0,2:T(8,128)} %get-tuple-element.16, f32[512,2]{0,1:T(2,128)S(1)} %get-tuple-element.15, pred[512,2304]{0,1:T(8,128)(4,1)S(1)} %pad_add_fusion, bf16[128,1,128]{0,2,1:T(8,128)(2,1)S(1)} %copy-done.3, bf16[128,1,128]{0,2,1:T(8,128)(2,1)S(1)} %copy-done.2, ...), kind=kOutput, calls=%fused_computation.14 | convolution fusion | flops 617545728 | bytes 11735040 | tf_op jit(solution)/shard_map/tcgk,kcd->tcgd/dot_general | solution.py:151
  125.1 4.2 %all-to-all-start.1 = ((f32[4,128,1,2,128]{1,4,3,2,0:T(8,128)}), f32[4,128,1,2,128]{1,4,3,2,0:T(8,128)S(1)}, u32[]{:S(2)}, u32[]{:S(2)}) async-start(f32[4,128,1,2,128]{1,4,3,2,0:T(8,128)} %bitcast.98), calls=%async_computation.1 | async-start | bytes 1048576 | tf_op jit(solution)/shard_map/all_to_all | solution.py:157
  129.3 6.9 %all-to-all-done.1 = f32[4,128,1,2,128]{1,4,3,2,0:T(8,128)S(1)} async-done(((f32[4,128,1,2,128]{1,4,3,2,0:T(8,128)}), f32[4,128,1,2,128]{1,4,3,2,0:T(8,128)S(1)}, u32[]{:S(2)}, u32[]{:S(2)}) %all-to-all-start.1) | async-done | bytes 524320 | tf_op jit(solution)/shard_map/all_to_all | solution.py:157
  136.7 17.2 %all_to_all.20 = bf16[128,8,256]{2,0,1:T(8,128)(2,1)S(1)} all-to-all(bf16[128,8,256]{2,0,1:T(8,128)(2,1)S(1)} %bitcast.100), channel_id=1, replica_groups=mesh['sx'=4,'sz'=16,'tp'=8] {'tp'}, dimensions={1} | all-to-all | bytes 1048576 | tf_op jit(solution)/shard_map/all_to_all | solution.py:170
  (62 shorter events, 9.7 us)
Async XLA Ops:
  0.0 136.3 %copy-start = (bf16[256,2048]{1,0:T(8,128)(2,1)S(1)}, bf16[256,2048]{1,0:T(8,128)(2,1)}, u32[]{:S(2)}) copy-start(bf16[256,2048]{1,0:T(8,128)(2,1)} %param.19) | copy-start | bytes 3145732
  0.0 62.2 %copy-start.5 = (f32[2048]{0:T(1024)S(1)}, f32[2048]{0:T(1024)}, u32[]{:S(2)}) copy-start(f32[2048]{0:T(1024)} %param.14) | copy-start | bytes 24580
  0.0 61.6 %copy-start.4 = (f32[128]{0:T(128)S(1)}, f32[128]{0:T(128)}, u32[]{:S(2)}) copy-start(f32[128]{0:T(128)} %param.20) | copy-start | bytes 1540
  0.0 62.2 %copy-start.6 = (bf16[2048,2]{0,1:T(2,128)(2,1)S(1)}, bf16[2048,2]{0,1:T(2,128)(2,1)}, u32[]{:S(2)}) copy-start(bf16[2048,2]{0,1:T(2,128)(2,1)} %param.18) | copy-start | bytes 24580
  22.4 56.2 %collective-permute-start = (bf16[128,1,128]{2,0,1:T(8,128)(2,1)}, bf16[128,1,128]{2,0,1:T(8,128)(2,1)}, u32[]{:S(2)}, u32[]{:S(2)}) collective-permute-start(bf16[128,1,128]{2,0,1:T(8,128)(2,1)} %fusion.10), channel_id=1, source_target_pairs={{0,64},{8,72},{16,80},{24,88},{32,96},{40,104},{48,112},{56,120},{... | collective-permute-start | bytes 98312 | tf_op jit(solution)/shard_map/ppermute | solution.py:124
  36.9 62.4 %all-to-all-start = ((bf16[16,2,128,128]{3,2,1,0:T(8,128)(2,1)}), bf16[16,2,128,128]{3,2,1,0:T(8,128)(2,1)S(1)}, u32[]{:S(2)}, u32[]{:S(2)}) async-start(bf16[16,2,128,128]{3,2,1,0:T(8,128)(2,1)} %gather_fusion.1), calls=%async_computation | async-start | bytes 2097152 | tf_op jit(solution)/shard_map/all_to_all | solution.py:94
  46.7 51.1 %collective-permute-start.1 = (bf16[128,1,128]{0,2,1:T(8,128)(2,1)}, bf16[128,1,128]{0,2,1:T(8,128)(2,1)}, u32[]{:S(2)}, u32[]{:S(2)}) collective-permute-start(bf16[128,1,128]{0,2,1:T(8,128)(2,1)} %pad_maximum_fusion.2), channel_id=1, source_target_pairs={{0,64},{8,72},{16,80},{24,88},{32,96},{40,104},{48,112},{56,120},{... | collective-permute-start | bytes 98312 | tf_op jit(solution)/shard_map/ppermute | solution.py:124
  101.6 17.5 %copy-start.2 = (bf16[128,1,128]{0,2,1:T(8,128)(2,1)S(1)}, bf16[128,1,128]{0,2,1:T(8,128)(2,1)}, u32[]{:S(2)}) copy-start(bf16[128,1,128]{0,2,1:T(8,128)(2,1)} %copy.58) | copy-start | bytes 98308
  101.6 17.5 %copy-start.3 = (bf16[128,1,128]{0,2,1:T(8,128)(2,1)S(1)}, bf16[128,1,128]{0,2,1:T(8,128)(2,1)}, u32[]{:S(2)}) copy-start(bf16[128,1,128]{0,2,1:T(8,128)(2,1)} %copy.59) | copy-start | bytes 98308
  115.1 9.9 %all-to-all-start.2 = ((f32[4,128,1,2,2]{1,3,4,2,0:T(2,128)}), f32[4,128,1,2,2]{1,3,4,2,0:T(2,128)S(1)}, u32[]{:S(2)}, u32[]{:S(2)}) async-start(f32[4,128,1,2,2]{1,3,4,2,0:T(2,128)} %copy.66), calls=%async_computation.2 | async-start | bytes 16384 | tf_op jit(solution)/shard_map/all_to_all | solution.py:156
  119.1 34.8 %copy-start.1 = (bf16[128,256]{1,0:T(8,128)(2,1)S(1)}, bf16[128,256]{1,0:T(8,128)(2,1)}, u32[]{:S(2)}) copy-start(bf16[128,256]{1,0:T(8,128)(2,1)} %param.13) | copy-start | bytes 196612
  125.1 11.2 %all-to-all-start.1 = ((f32[4,128,1,2,128]{1,4,3,2,0:T(8,128)}), f32[4,128,1,2,128]{1,4,3,2,0:T(8,128)S(1)}, u32[]{:S(2)}, u32[]{:S(2)}) async-start(f32[4,128,1,2,128]{1,4,3,2,0:T(8,128)} %bitcast.98), calls=%async_computation.1 | async-start | bytes 1048576 | tf_op jit(solution)/shard_map/all_to_all | solution.py:157

commit v3 on v2

--- a/solution.py
+++ b/solution.py
@@ -3,6 +3,8 @@
 import jax
 import jax.numpy as jnp
 from jax import lax
+from jax.experimental import pallas as pl
+from jax.experimental.pallas import tpu as pltpu
 from jax.sharding import Mesh, PartitionSpec as P
 
 SPAN = 1024
@@ -54,6 +56,68 @@
         preferred_element_type=jnp.float32,
     )
     return (new_max, new_sum, running_acc * rescale[..., None] + update)
+
+
+def attention_kernel(
+    scalars, q_ref, qtok_ref, kc_ref, vc_ref, kn_ref, vn_ref, ktok_ref, acc_ref, top_ref, total_ref
+):
+    scale = q_ref.shape[-1] ** (-0.5)
+    dims = (((1,), (1,)), ((), ()))
+    q = q_ref[...]
+    cache_scores = lax.dot_general(q, kc_ref[...], dims, preferred_element_type=jnp.float32) * scale
+    cache_pos = scalars[1] + lax.broadcasted_iota(jnp.int32, (1, kc_ref.shape[0]), 1)
+    cache_seen = cache_pos < scalars[0]
+    cache_scores = jnp.where(cache_seen, cache_scores, masked_score)
+    new_scores = lax.dot_general(q, kn_ref[...], dims, preferred_element_type=jnp.float32) * scale
+    new_seen = ktok_ref[...] <= qtok_ref[...]
+    new_scores = jnp.where(new_seen, new_scores, masked_score)
+    top = jnp.maximum(
+        jnp.max(cache_scores, 1, keepdims=True), jnp.max(new_scores, 1, keepdims=True)
+    )
+    cache_expo = jnp.where(cache_seen, jnp.exp(cache_scores - top), 0.0)
+    new_expo = jnp.where(new_seen, jnp.exp(new_scores - top), 0.0)
+    total_ref[...] = jnp.sum(cache_expo, 1, keepdims=True) + jnp.sum(new_expo, 1, keepdims=True)
+    top_ref[...] = top
+    acc_ref[...] = jnp.dot(
+        cache_expo.astype(jnp.bfloat16), vc_ref[...], preferred_element_type=jnp.float32
+    ) + jnp.dot(new_expo.astype(jnp.bfloat16), vn_ref[...], preferred_element_type=jnp.float32)
+
+
+def attention(scalars, q_rows, q_tok, keys_cache, values_cache, keys_new, values_new, key_tok):
+    rows, width = q_rows.shape
+    cache_rows = keys_cache.shape[0]
+    new_rows = keys_new.shape[0]
+    block = 256
+    full = lambda shape: pl.BlockSpec(shape, lambda i, s: (0, 0))
+    row_block = lambda cols: pl.BlockSpec((block, cols), lambda i, s: (i, 0))
+    flops = 4 * rows * (cache_rows + new_rows) * width
+    return pl.pallas_call(
+        attention_kernel,
+        out_shape=(
+            jax.ShapeDtypeStruct((rows, width), jnp.float32),
+            jax.ShapeDtypeStruct((rows, 1), jnp.float32),
+            jax.ShapeDtypeStruct((rows, 1), jnp.float32),
+        ),
+        grid_spec=pltpu.PrefetchScalarGridSpec(
+            num_scalar_prefetch=1,
+            grid=(rows // block,),
+            in_specs=[
+                row_block(width),
+                row_block(1),
+                full((cache_rows, width)),
+                full((cache_rows, width)),
+                full((new_rows, width)),
+                full((new_rows, width)),
+                full((1, new_rows)),
+            ],
+            out_specs=[row_block(width), row_block(1), row_block(1)],
+        ),
+        cost_estimate=pl.CostEstimate(
+            flops=flops,
+            transcendentals=rows * (cache_rows + new_rows),
+            bytes_accessed=2 * (rows + 2 * cache_rows + 2 * new_rows) * width + 4 * rows * width,
+        ),
+    )(scalars, q_rows, q_tok, keys_cache, values_cache, keys_new, values_new, key_tok)
 
 
 def per_device(
@@ -121,7 +185,7 @@
     )
 
     partner_pairs = [(z, (z + req_count) % ring_z) for z in range(ring_z)]
-    partner_keys, partner_values = lax.ppermute((keys_new, values_new), "sz", partner_pairs)
+    partner_kv = lax.ppermute(jnp.stack([keys_new, values_new]), "sz", partner_pairs)
     partner_part = x_index * pair + (pair - 1 - parity)
     all_queries = lax.all_gather(queries, "sx", axis=0, tiled=True)
     query_tok = (
@@ -130,28 +194,21 @@
     ).reshape(-1)
     row_ids = jnp.arange(tok_rows, dtype=jnp.int32)
     key_tok = jnp.concatenate([local_part * tok_rows + row_ids, partner_part * tok_rows + row_ids])
-    keys_all = jnp.concatenate([keys_cache, keys_new, partner_keys], 0)
-    values_all = jnp.concatenate([values_cache, values_new, partner_values], 0)
+    keys_two = jnp.concatenate([keys_new, partner_kv[0]], 0).reshape(-1, head_dim)
+    values_two = jnp.concatenate([values_new, partner_kv[1]], 0).reshape(-1, head_dim)
     query_count = query_tok.shape[0]
-    visible = jnp.concatenate(
-        [
-            jnp.broadcast_to((cache_pos < length)[None, :], (query_count, cache_rows)),
-            key_tok[None, :] <= query_tok[:, None],
-        ],
-        1,
-    )
-    scores = jnp.einsum(
-        "tcgd,kcd->tcgk", all_queries, keys_all, preferred_element_type=jnp.float32
-    ) * head_dim ** (-0.5)
-    seen = visible[:, None, None, :]
-    scores = jnp.where(seen, scores, masked_score)
-    top = jnp.max(scores, -1)
-    expo = jnp.where(seen, jnp.exp(scores - top[..., None]), 0.0)
-    total = jnp.sum(expo, -1)
-    acc = jnp.einsum(
-        "tcgk,kcd->tcgd", expo.astype(jnp.bfloat16), values_all, preferred_element_type=jnp.float32
-    )
-    stats = jnp.stack([top, total], -1).reshape(ring_x, tok_rows, kv_local, group_size, 2)
+    scalars = jnp.stack([length, x_index * cache_rows]).astype(jnp.int32)
+    acc, top, total = attention(
+        scalars,
+        all_queries.reshape(-1, head_dim),
+        jnp.repeat(query_tok, heads_local)[:, None],
+        keys_cache.reshape(cache_rows, head_dim),
+        values_cache.reshape(cache_rows, head_dim),
+        keys_two,
+        values_two,
+        key_tok[None, :],
+    )
+    stats = jnp.concatenate([top, total], -1).reshape(ring_x, tok_rows, kv_local, group_size, 2)
     acc = acc.reshape(ring_x, tok_rows, kv_local, group_size, head_dim)
     stats_in = lax.all_to_all(stats, "sx", 0, 0, tiled=True)
     acc_in = lax.all_to_all(acc, "sx", 0, 0, tiled=True)

time: 156 us -> 131 us (0.84)
  matrix products: 17.6 us -> 2.97 us
  Pallas kernels: 0 us -> 8.74 us
  waiting for transfers between devices: 24.7 us -> 17.7 us
  other arithmetic: 13.5 us -> 6.57 us
  local copies, waits for them, and re-layouts: 14 us -> 11.5 us
  blocking collectives: 48.2 us -> 45.9 us
    dot_general x2 -> x0, matrix products: 11.8 us -> none  [the longest x1 6.72 us: per_device(): jnp.einsum('tcgd,kcd->tcgk', all_queries, keys_all, preferred_element_typ...]
    all_to_all x1, starting transfers between devices: 4.86 us -> 15.9 us  [per_device(): incoming = lax.all_to_all(cache_both[peer_groups], 'sz', 0, 0, tiled=True)]
    ppermute x2 -> x1, waiting for transfers between devices: 17.8 us -> 7.44 us  [per_device(): lax.ppermute(jnp.stack([keys_new, values_new]), 'sz', partner_pairs)]
    ppermute x2 -> x1, starting transfers between devices: 22.5 us -> 12.3 us  [per_device(): lax.ppermute(jnp.stack([keys_new, values_new]), 'sz', partner_pairs)]
    pallas_call x0 -> x1, Pallas kernels: none -> 8.74 us  [attention(): pl.pallas_call(attention_kernel, out_shape=(jax.ShapeDtypeStruct((rows, w...]
    reduce_sum x1 -> x0, other arithmetic: 6.14 us -> none  [per_device(): total = jnp.sum(expo, -1)]
    all_gather x1, blocking collectives: 20.2 us -> 14.6 us  [per_device(): gathered = lax.all_gather(hidden_in, 'tp', axis=1, tiled=True)]
    all_to_all x1, waiting for transfers between devices: 0.01 us -> 3.72 us  [per_device(): stats_in = lax.all_to_all(stats, 'sx', 0, 0, tiled=True)]
  transfers between devices with their start and end apart: 5 -> 4, of which waited for: 2 -> 3; matrix products, arithmetic and copies ran while one was open for 17% -> 7% of each run, Pallas kernels for 0% -> 0%
where the time goes in v3:
time: 131 us; the launch traced here: 130 us
  blocking collectives  45.9 us (35%)
  starting transfers between devices  35.8 us (27%)
  waiting for transfers between devices  17.7 us (14%)
  local copies, waits for them, and re-layouts  11.5 us (9%)
  Pallas kernels  8.74 us (7%)
  other arithmetic  6.57 us (5%)
  matrix products  2.97 us (2%)
    all_to_all x1, blocking collectives, per_device(): arrived = lax.all_to_all(pieces, 'tp', 1, 1, tiled=True)  20.4 us
    all_to_all x1, starting transfers between devices, per_device(): incoming = lax.all_to_all(cache_both[peer_groups], 'sz', 0, 0, tiled=True)  15.9 us
    all_gather x1, blocking collectives, per_device(): gathered = lax.all_gather(hidden_in, 'tp', axis=1, tiled=True)  14.6 us
    ppermute x1, starting transfers between devices, per_device(): lax.ppermute(jnp.stack([keys_new, values_new]), 'sz', partner_pairs)  12.3 us
    all_gather x1, blocking collectives, per_device(): all_queries = lax.all_gather(queries, 'sx', axis=0, tiled=True)  11 us
    pallas_call x1, Pallas kernels, attention(): pl.pallas_call(attention_kernel, out_shape=(jax.ShapeDtypeStruct((rows, w...  8.74 us
    ppermute x1, waiting for transfers between devices, per_device(): lax.ppermute(jnp.stack([keys_new, values_new]), 'sz', partner_pairs)  7.44 us
    all_to_all x1, waiting for transfers between devices, per_device(): acc_in = lax.all_to_all(acc, 'sx', 0, 0, tiled=True)  6.57 us
  transfers between devices with their start and end apart: 4, of which 3 were waited for; matrix products, arithmetic and copies ran while one was open for 7% of the time, Pallas kernels for 0%

profile of v3, /device:TPU:1, one launch (start us, length us, event | category | flops | bytes accessed | tf_op | source)
XLA Modules:
  0.0 130.3 jit_solution(13067169355494212180)
XLA Ops:
  0.0 0.7 copy-done.1
  0.8 0.7 gather_fusion
  1.6 1.6 %gather_fusion.1 = bf16[16,2,128,128]{3,2,1,0:T(8,128)(2,1)} fusion(bf16[2,2,128,128]{3,2,0,1:T(8,128)(2,1)S(1)} %pad_maximum_fusion, s32[1024]{0:T(1024)S(1)} %pad_clamp_fusion), kind=kCustom, calls=%fused_computation.1 | custom fusion | bytes 2097216 | tf_op jit(solution)/shard_map/gather | solution.py:158
  3.3 15.9 %all-to-all-start = ((bf16[16,2,128,128]{3,2,1,0:T(8,128)(2,1)}), bf16[16,2,128,128]{3,2,1,0:T(8,128)(2,1)S(1)}, u32[]{:S(2)}, u32[]{:S(2)}) async-start(bf16[16,2,128,128]{3,2,1,0:T(8,128)(2,1)} %gather_fusion.1), calls=%async_computation | async-start | bytes 2097152 | tf_op jit(solution)/shard_map/all_to_all | solution.py:158
  19.2 14.6 %all_gather.6 = bf16[128,2048]{1,0:T(8,128)(2,1)S(1)} all-gather(bf16[128,256]{1,0:T(8,128)(2,1)S(1)} %copy-done.3), channel_id=1, replica_groups=mesh['sx'=4,'sz'=16,'tp'=8] {'tp'}, dimensions={1}, use_global_device_ids=true | all-gather | bytes 589824 | tf_op jit(solution)/shard_map/all_gather | solution.py:164
  35.7 0.6 dynamic_slice.3
  38.5 12.3 %collective-permute-start = (bf16[2,128,1,128]{3,1,2,0:T(8,128)(2,1)S(1)}, bf16[2,128,1,128]{3,1,2,0:T(8,128)(2,1)S(1)}, u32[]{:S(2)}, u32[]{:S(2)}) collective-permute-start(bf16[2,128,1,128]{3,1,2,0:T(8,128)(2,1)S(1)} %pad_maximum_fusion.2), channel_id=1, source_target_pairs={{0,64},{8,72},{16,80},{24,88},{32,96},{40,104},{48,112},{56,120},{... | collective-permute-start | bytes 196616 | tf_op jit(solution)/shard_map/ppermute | solution.py:188
  51.1 1.0 broadcast_in_dim_reshape.5.qtok_ref
  52.0 1.6 %fusion.26 = f32[128,256]{1,0:T(8,128)S(1)} fusion(bf16[2048,256]{1,0:T(8,128)(2,1)} %param.15, bf16[128,2048]{1,0:T(8,128)(2,1)S(1)} %all_gather.6, f32[2048]{0:T(1024)S(1)} %copy-done.10, f32[128]{0:T(128)S(1)} %add_rsqrt_fusion.2), kind=kOutput, calls=%fused_computation.72 | convolution fusion | flops 135266304 | bytes 1712640 | tf_op jit(solution)/shard_map/dot_general | solution.py:170
  53.7 1.3 %pad_add_fusion.1.scalars = s32[2]{0:T(128)} fusion(s32[1]{0:T(128)} %bitcast, s32[1]{0:T(128)} %dynamic_slice.3), kind=kLoop, calls=%fused_computation.62 | loop fusion | flops 2 | bytes 16 | tf_op jit(solution)/shard_map/stack | solution.py:200
  57.2 11.0 %all_gather.7 = bf16[512,1,2,128]{3,2,1,0:T(2,128)(2,1)} all-gather(bf16[128,1,2,128]{3,2,1,0:T(2,128)(2,1)S(1)} %pad_maximum_fusion.1), channel_id=1, replica_groups=mesh['sx'=4,'sz'=16,'tp'=8] {'sx'}, dimensions={0}, use_global_device_ids=true | all-gather | bytes 327680 | tf_op jit(solution)/shard_map/all_gather | solution.py:190
  68.3 7.4 %collective-permute-done = bf16[2,128,1,128]{3,1,2,0:T(8,128)(2,1)S(1)} collective-permute-done((bf16[2,128,1,128]{3,1,2,0:T(8,128)(2,1)S(1)}, bf16[2,128,1,128]{3,1,2,0:T(8,128)(2,1)S(1)}, u32[]{:S(2)}, u32[]{:S(2)}) %collective-permute-start) | collective-permute-done | bytes 65568 | tf_op jit(solution)/shard_map/ppermute | solution.py:188
  75.7 0.7 maximum_bitcast_fusion
  76.4 1.1 fusion.28
  77.5 8.7 %shard_map.127 = (f32[1024,128]{1,0:T(8,128)}, f32[1024,1]{1,0:T(8,128)}, f32[1024,1]{1,0:T(8,128)}) custom-call(s32[2]{0:T(128)} %pad_add_fusion.1.scalars, bf16[1024,128]{1,0:T(8,128)(2,1)} %bitcast.71, s32[1024,1]{1,0:T(8,128)} %broadcast_in_dim_reshape.5.qtok_ref, bf16[2048,128]{1,0:T(8,128)(2,1)} %bitcast.67, bf16[2048,128]{1,0:T(8,128)(2,1)} %bitcast.66, ...), custom_call_target="tpu_custom_call" | custom-call | flops 1207959552 | bytes 1966080 | tf_op jit(solution)/shard_map/pallas_call | solution.py:94
  86.3 1.3 copy.67
  88.3 0.8 copy.69
  89.0 4.1 %all-to-all-start.2 = ((f32[4,128,1,2,2]{1,3,4,2,0:T(2,128)}), f32[4,128,1,2,2]{1,3,4,2,0:T(2,128)S(1)}, u32[]{:S(2)}, u32[]{:S(2)}) async-start(f32[4,128,1,2,2]{1,3,4,2,0:T(2,128)} %copy.69), calls=%async_computation.2 | async-start | bytes 16384 | tf_op jit(solution)/shard_map/all_to_all | solution.py:213
  93.6 3.7 %all-to-all-done.2 = f32[4,128,1,2,2]{1,3,4,2,0:T(2,128)S(1)} async-done(((f32[4,128,1,2,2]{1,3,4,2,0:T(2,128)}), f32[4,128,1,2,2]{1,3,4,2,0:T(2,128)S(1)}, u32[]{:S(2)}, u32[]{:S(2)}) %all-to-all-start.2) | async-done | bytes 8224 | tf_op jit(solution)/shard_map/all_to_all | solution.py:213
  97.4 3.5 %all-to-all-start.1 = ((f32[4,128,1,2,128]{4,3,1,2,0:T(2,128)}), f32[4,128,1,2,128]{4,3,1,2,0:T(2,128)S(1)}, u32[]{:S(2)}, u32[]{:S(2)}) async-start(f32[4,128,1,2,128]{4,3,1,2,0:T(2,128)} %bitcast.23), calls=%async_computation.1 | async-start | bytes 1048576 | tf_op jit(solution)/shard_map/all_to_all | solution.py:214
  101.2 6.6 %all-to-all-done.1 = f32[4,128,1,2,128]{4,3,1,2,0:T(2,128)S(1)} async-done(((f32[4,128,1,2,128]{4,3,1,2,0:T(2,128)}), f32[4,128,1,2,128]{4,3,1,2,0:T(2,128)S(1)}, u32[]{:S(2)}, u32[]{:S(2)}) %all-to-all-start.1) | async-done | bytes 524320 | tf_op jit(solution)/shard_map/all_to_all | solution.py:214
  107.7 0.8 multiply_reduce_fusion
  109.2 20.4 %all_to_all.20 = bf16[128,8,256]{2,0,1:T(8,128)(2,1)S(1)} all-to-all(bf16[128,8,256]{2,0,1:T(8,128)(2,1)S(1)} %bitcast.65), channel_id=1, replica_groups=mesh['sx'=4,'sz'=16,'tp'=8] {'tp'}, dimensions={1} | all-to-all | bytes 1048576 | tf_op jit(solution)/shard_map/all_to_all | solution.py:227
  129.7 0.6 add_convert_fusion
  (69 shorter events, 8.2 us)
Async XLA Ops:
  0.0 108.9 %copy-start = (bf16[256,2048]{1,0:T(8,128)(2,1)S(1)}, bf16[256,2048]{1,0:T(8,128)(2,1)}, u32[]{:S(2)}) copy-start(bf16[256,2048]{1,0:T(8,128)(2,1)} %param.19) | copy-start | bytes 3145732
  0.0 0.7 copy-start.1
  0.8 0.8 copy-start.4
  0.8 0.9 copy-start.5
  3.3 15.9 %copy-start.3 = (bf16[128,256]{1,0:T(8,128)(2,1)S(1)}, bf16[128,256]{1,0:T(8,128)(2,1)}, u32[]{:S(2)}) copy-start(bf16[128,256]{1,0:T(8,128)(2,1)} %param.13) | copy-start | bytes 196612
  3.3 73.1 %all-to-all-start = ((bf16[16,2,128,128]{3,2,1,0:T(8,128)(2,1)}), bf16[16,2,128,128]{3,2,1,0:T(8,128)(2,1)S(1)}, u32[]{:S(2)}, u32[]{:S(2)}) async-start(bf16[16,2,128,128]{3,2,1,0:T(8,128)(2,1)} %gather_fusion.1), calls=%async_computation | async-start | bytes 2097152 | tf_op jit(solution)/shard_map/all_to_all | solution.py:158
  19.2 14.8 %copy-start.8 = (bf16[2048,128]{1,0:T(8,128)(2,1)S(1)}, bf16[2048,128]{1,0:T(8,128)(2,1)}, u32[]{:S(2)}) copy-start(bf16[2048,128]{1,0:T(8,128)(2,1)} %param.16) | copy-start | bytes 1572868
  33.7 0.7 copy-start.10
  34.4 3.6 %copy-start.9 = (bf16[2048,128]{1,0:T(8,128)(2,1)S(1)}, bf16[2048,128]{1,0:T(8,128)(2,1)}, u32[]{:S(2)}) copy-start(bf16[2048,128]{1,0:T(8,128)(2,1)} %param.17) | copy-start | bytes 1572868
  35.0 0.7 copy-start.12
  37.0 0.7 copy-start.6
  38.5 37.2 %collective-permute-start = (bf16[2,128,1,128]{3,1,2,0:T(8,128)(2,1)S(1)}, bf16[2,128,1,128]{3,1,2,0:T(8,128)(2,1)S(1)}, u32[]{:S(2)}, u32[]{:S(2)}) collective-permute-start(bf16[2,128,1,128]{3,1,2,0:T(8,128)(2,1)S(1)} %pad_maximum_fusion.2), channel_id=1, source_target_pairs={{0,64},{8,72},{16,80},{24,88},{32,96},{40,104},{48,112},{56,120},{... | collective-permute-start | bytes 196616 | tf_op jit(solution)/shard_map/ppermute | solution.py:188
  55.9 0.7 copy-start.7
  86.2 1.3 copy-start.2
  89.0 4.2 %copy-start.11 = (bf16[2048,2]{0,1:T(2,128)(2,1)S(1)}, bf16[2048,2]{0,1:T(2,128)(2,1)}, u32[]{:S(2)}) copy-start(bf16[2048,2]{0,1:T(2,128)(2,1)} %param.18) | copy-start | bytes 24580
  89.0 8.3 %all-to-all-start.2 = ((f32[4,128,1,2,2]{1,3,4,2,0:T(2,128)}), f32[4,128,1,2,2]{1,3,4,2,0:T(2,128)S(1)}, u32[]{:S(2)}, u32[]{:S(2)}) async-start(f32[4,128,1,2,2]{1,3,4,2,0:T(2,128)} %copy.69), calls=%async_computation.2 | async-start | bytes 16384 | tf_op jit(solution)/shard_map/all_to_all | solution.py:213
  97.4 10.4 %all-to-all-start.1 = ((f32[4,128,1,2,128]{4,3,1,2,0:T(2,128)}), f32[4,128,1,2,128]{4,3,1,2,0:T(2,128)S(1)}, u32[]{:S(2)}, u32[]{:S(2)}) async-start(f32[4,128,1,2,128]{4,3,1,2,0:T(2,128)} %bitcast.23), calls=%async_computation.1 | async-start | bytes 1048576 | tf_op jit(solution)/shard_map/all_to_all | solution.py:214

commit v4 on v3

--- a/solution.py
+++ b/solution.py
@@ -208,10 +208,12 @@
         values_two,
         key_tok[None, :],
     )
-    stats = jnp.concatenate([top, total], -1).reshape(ring_x, tok_rows, kv_local, group_size, 2)
-    acc = acc.reshape(ring_x, tok_rows, kv_local, group_size, head_dim)
-    stats_in = lax.all_to_all(stats, "sx", 0, 0, tiled=True)
-    acc_in = lax.all_to_all(acc, "sx", 0, 0, tiled=True)
+    slot_rows = tok_rows * heads_local
+    stats = jnp.concatenate([top, total], -1).reshape(ring_x, -1, head_dim)
+    packed = jnp.concatenate([acc.reshape(ring_x, slot_rows, head_dim), stats], 1)
+    packed_in = lax.all_to_all(packed, "sx", 0, 0, tiled=True)
+    acc_in = packed_in[:, :slot_rows].reshape(ring_x, tok_rows, kv_local, group_size, head_dim)
+    stats_in = packed_in[:, slot_rows:].reshape(ring_x, tok_rows, kv_local, group_size, 2)
     best = jnp.max(stats_in[..., 0], 0)
     factor = jnp.exp(stats_in[..., 0] - best[None])
     total = jnp.sum(stats_in[..., 1] * factor, 0)

time: 131 us -> 126 us (0.962); the launches traced: 130 us -> 123 us
  waiting for transfers between devices: 17.7 us -> 14.1 us
  starting transfers between devices: 35.8 us -> 32.3 us
    all_to_all x2 -> x1, waiting for transfers between devices: 10.3 us -> 6.57 us  [per_device(): packed_in = lax.all_to_all(packed, 'sx', 0, 0, tiled=True)]
    all_to_all x2 -> x1, starting transfers between devices: 7.62 us -> 4.15 us  [per_device(): packed_in = lax.all_to_all(packed, 'sx', 0, 0, tiled=True)]
    unnamed x26 -> x28, local copies, waits for them, and re-layouts: 3.06 us -> 3.57 us
  transfers between devices with their start and end apart: 4 -> 3, of which waited for: 3 -> 2; matrix products, arithmetic and copies ran while one was open for 7% -> 8% of each run, Pallas kernels for 0% -> 0%
where the time goes in v4:
time: 126 us; the launch traced here: 123 us
  blocking collectives  44.8 us (36%)
  starting transfers between devices  32.3 us (26%)
  waiting for transfers between devices  14.1 us (11%)
  local copies, waits for them, and re-layouts  11.7 us (9%)
  Pallas kernels  8.75 us (7%)
  other arithmetic  7.67 us (6%)
  matrix products  2.98 us (2%)
    all_to_all x1, blocking collectives, per_device(): arrived = lax.all_to_all(pieces, 'tp', 1, 1, tiled=True)  19.2 us
    all_to_all x1, starting transfers between devices, per_device(): incoming = lax.all_to_all(cache_both[peer_groups], 'sz', 0, 0, tiled=True)  15.9 us
    all_gather x1, blocking collectives, per_device(): gathered = lax.all_gather(hidden_in, 'tp', axis=1, tiled=True)  14.6 us
    ppermute x1, starting transfers between devices, per_device(): lax.ppermute(jnp.stack([keys_new, values_new]), 'sz', partner_pairs)  12.3 us
    all_gather x1, blocking collectives, per_device(): all_queries = lax.all_gather(queries, 'sx', axis=0, tiled=True)  11 us
    pallas_call x1, Pallas kernels, attention(): pl.pallas_call(attention_kernel, out_shape=(jax.ShapeDtypeStruct((rows, w...  8.75 us
    ppermute x1, waiting for transfers between devices, per_device(): lax.ppermute(jnp.stack([keys_new, values_new]), 'sz', partner_pairs)  7.54 us
    all_to_all x1, waiting for transfers between devices, per_device(): packed_in = lax.all_to_all(packed, 'sx', 0, 0, tiled=True)  6.57 us
  transfers between devices with their start and end apart: 3, of which 2 were waited for; matrix products, arithmetic and copies ran while one was open for 8% of the time, Pallas kernels for 0%

profile of v4, /device:TPU:1, one launch (start us, length us, event | category | flops | bytes accessed | tf_op | source)
XLA Modules:
  0.0 123.3 jit_solution(17679973265825655709)
XLA Ops:
  0.0 0.7 copy-done.1
  0.8 0.7 gather_fusion
  1.6 1.6 %gather_fusion.1 = bf16[16,2,128,128]{3,2,1,0:T(8,128)(2,1)} fusion(bf16[2,2,128,128]{3,2,0,1:T(8,128)(2,1)S(1)} %pad_maximum_fusion.1, s32[1024]{0:T(1024)S(1)} %pad_clamp_fusion), kind=kCustom, calls=%fused_computation.1 | custom fusion | bytes 2097216 | tf_op jit(solution)/shard_map/gather | solution.py:158
  3.3 15.9 %all-to-all-start = ((bf16[16,2,128,128]{3,2,1,0:T(8,128)(2,1)}), bf16[16,2,128,128]{3,2,1,0:T(8,128)(2,1)S(1)}, u32[]{:S(2)}, u32[]{:S(2)}) async-start(bf16[16,2,128,128]{3,2,1,0:T(8,128)(2,1)} %gather_fusion.1), calls=%async_computation | async-start | bytes 2097152 | tf_op jit(solution)/shard_map/all_to_all | solution.py:158
  19.2 14.6 %all_gather.6 = bf16[128,2048]{1,0:T(8,128)(2,1)S(1)} all-gather(bf16[128,256]{1,0:T(8,128)(2,1)S(1)} %copy-done.4), channel_id=1, replica_groups=mesh['sx'=4,'sz'=16,'tp'=8] {'tp'}, dimensions={1}, use_global_device_ids=true | all-gather | bytes 589824 | tf_op jit(solution)/shard_map/all_gather | solution.py:164
  35.0 0.6 copy-done.13
  35.7 0.6 dynamic_slice.3
  37.0 0.6 copy-done.7
  38.6 12.3 %collective-permute-start = (bf16[2,128,1,128]{3,1,2,0:T(8,128)(2,1)S(1)}, bf16[2,128,1,128]{3,1,2,0:T(8,128)(2,1)S(1)}, u32[]{:S(2)}, u32[]{:S(2)}) collective-permute-start(bf16[2,128,1,128]{3,1,2,0:T(8,128)(2,1)S(1)} %pad_maximum_fusion.3), channel_id=1, source_target_pairs={{0,64},{8,72},{16,80},{24,88},{32,96},{40,104},{48,112},{56,120},{... | collective-permute-start | bytes 196616 | tf_op jit(solution)/shard_map/ppermute | solution.py:188
  51.1 1.0 broadcast_in_dim_reshape.5.qtok_ref
  52.0 1.6 %fusion.24 = f32[128,256]{1,0:T(8,128)S(1)} fusion(bf16[2048,256]{1,0:T(8,128)(2,1)} %param.15, bf16[128,2048]{1,0:T(8,128)(2,1)S(1)} %all_gather.6, f32[2048]{0:T(1024)S(1)} %copy-done.12, f32[128]{0:T(128)S(1)} %add_rsqrt_fusion.2), kind=kOutput, calls=%fused_computation.71 | convolution fusion | flops 135266304 | bytes 1712640 | tf_op jit(solution)/shard_map/dot_general | solution.py:170
  53.7 1.3 %pad_add_fusion.1.scalars = s32[2]{0:T(128)} fusion(s32[1]{0:T(128)} %bitcast, s32[1]{0:T(128)} %dynamic_slice.3), kind=kLoop, calls=%fused_computation.61 | loop fusion | flops 2 | bytes 16 | tf_op jit(solution)/shard_map/stack | solution.py:200
  57.1 11.0 %all_gather.7 = bf16[512,1,2,128]{3,2,1,0:T(2,128)(2,1)} all-gather(bf16[128,1,2,128]{3,2,1,0:T(2,128)(2,1)S(1)} %pad_maximum_fusion.2), channel_id=1, replica_groups=mesh['sx'=4,'sz'=16,'tp'=8] {'sx'}, dimensions={0}, use_global_device_ids=true | all-gather | bytes 327680 | tf_op jit(solution)/shard_map/all_gather | solution.py:190
  68.2 7.5 %collective-permute-done = bf16[2,128,1,128]{3,1,2,0:T(8,128)(2,1)S(1)} collective-permute-done((bf16[2,128,1,128]{3,1,2,0:T(8,128)(2,1)S(1)}, bf16[2,128,1,128]{3,1,2,0:T(8,128)(2,1)S(1)}, u32[]{:S(2)}, u32[]{:S(2)}) %collective-permute-start) | collective-permute-done | bytes 65568 | tf_op jit(solution)/shard_map/ppermute | solution.py:188
  75.7 0.7 maximum_bitcast_fusion
  76.4 1.1 fusion.26
  77.5 8.7 %shard_map.127 = (f32[1024,128]{1,0:T(8,128)}, f32[1024,1]{1,0:T(8,128)}, f32[1024,1]{1,0:T(8,128)}) custom-call(s32[2]{0:T(128)} %pad_add_fusion.1.scalars, bf16[1024,128]{1,0:T(8,128)(2,1)} %bitcast.74, s32[1024,1]{1,0:T(8,128)} %broadcast_in_dim_reshape.5.qtok_ref, bf16[2048,128]{1,0:T(8,128)(2,1)} %bitcast.69, bf16[2048,128]{1,0:T(8,128)(2,1)} %bitcast.68, ...), custom_call_target="tpu_custom_call" | custom-call | flops 1207959552 | bytes 1966080 | tf_op jit(solution)/shard_map/pallas_call | solution.py:94
  86.3 1.3 %copy.69 = f32[1024,1]{0,1:T(1,128)S(1)} copy(f32[1024,1]{1,0:T(8,128)} %get-tuple-element.9) | data formatting | bytes 8192 | tf_op jit(solution)/shard_map/pallas_call | solution.py:94
  88.8 0.8 pad_maximum_fusion
  89.7 4.1 %all-to-all-start.1 = ((f32[4,260,128]{2,1,0:T(8,128)}), f32[4,260,128]{2,1,0:T(8,128)S(1)}, u32[]{:S(2)}, u32[]{:S(2)}) async-start(f32[4,260,128]{2,1,0:T(8,128)} %pad_maximum_fusion), calls=%async_computation.1 | async-start | bytes 1081344 | tf_op jit(solution)/shard_map/all_to_all | solution.py:214
  94.3 6.6 %all-to-all-done.1 = f32[4,260,128]{2,1,0:T(8,128)S(1)} async-done(((f32[4,260,128]{2,1,0:T(8,128)}), f32[4,260,128]{2,1,0:T(8,128)S(1)}, u32[]{:S(2)}, u32[]{:S(2)}) %all-to-all-start.1) | async-done | bytes 532512 | tf_op jit(solution)/shard_map/all_to_all | solution.py:214
  101.0 0.6 fusion.27
  103.4 19.2 %all_to_all.15 = bf16[128,8,256]{2,0,1:T(8,128)(2,1)S(1)} all-to-all(bf16[128,8,256]{2,0,1:T(8,128)(2,1)S(1)} %bitcast.60), channel_id=1, replica_groups=mesh['sx'=4,'sz'=16,'tp'=8] {'tp'}, dimensions={1} | all-to-all | bytes 1048576 | tf_op jit(solution)/shard_map/all_to_all | solution.py:229
  122.7 0.6 add_convert_fusion
  (73 shorter events, 8.4 us)
Async XLA Ops:
  0.0 103.0 %copy-start = (bf16[256,2048]{1,0:T(8,128)(2,1)S(1)}, bf16[256,2048]{1,0:T(8,128)(2,1)}, u32[]{:S(2)}) copy-start(bf16[256,2048]{1,0:T(8,128)(2,1)} %param.19) | copy-start | bytes 3145732
  0.0 0.7 copy-start.1
  0.8 0.8 copy-start.5
  0.8 0.9 copy-start.6
  3.3 15.9 %copy-start.4 = (bf16[128,256]{1,0:T(8,128)(2,1)S(1)}, bf16[128,256]{1,0:T(8,128)(2,1)}, u32[]{:S(2)}) copy-start(bf16[128,256]{1,0:T(8,128)(2,1)} %param.13) | copy-start | bytes 196612
  3.3 73.1 %all-to-all-start = ((bf16[16,2,128,128]{3,2,1,0:T(8,128)(2,1)}), bf16[16,2,128,128]{3,2,1,0:T(8,128)(2,1)S(1)}, u32[]{:S(2)}, u32[]{:S(2)}) async-start(bf16[16,2,128,128]{3,2,1,0:T(8,128)(2,1)} %gather_fusion.1), calls=%async_computation | async-start | bytes 2097152 | tf_op jit(solution)/shard_map/all_to_all | solution.py:158
  19.2 14.8 %copy-start.9 = (bf16[2048,128]{1,0:T(8,128)(2,1)S(1)}, bf16[2048,128]{1,0:T(8,128)(2,1)}, u32[]{:S(2)}) copy-start(bf16[2048,128]{1,0:T(8,128)(2,1)} %param.16) | copy-start | bytes 1572868
  33.8 0.7 copy-start.12
  34.5 3.6 %copy-start.10 = (bf16[2048,128]{1,0:T(8,128)(2,1)S(1)}, bf16[2048,128]{1,0:T(8,128)(2,1)}, u32[]{:S(2)}) copy-start(bf16[2048,128]{1,0:T(8,128)(2,1)} %param.17) | copy-start | bytes 1572868
  35.0 0.7 copy-start.13
  37.0 0.7 copy-start.7
  38.6 37.1 %collective-permute-start = (bf16[2,128,1,128]{3,1,2,0:T(8,128)(2,1)S(1)}, bf16[2,128,1,128]{3,1,2,0:T(8,128)(2,1)S(1)}, u32[]{:S(2)}, u32[]{:S(2)}) collective-permute-start(bf16[2,128,1,128]{3,1,2,0:T(8,128)(2,1)S(1)} %pad_maximum_fusion.3), channel_id=1, source_target_pairs={{0,64},{8,72},{16,80},{24,88},{32,96},{40,104},{48,112},{56,120},{... | collective-permute-start | bytes 196616 | tf_op jit(solution)/shard_map/ppermute | solution.py:188
  55.8 0.7 copy-start.8
  86.3 1.3 %copy-start.3 = (f32[1024,1]{1,0:T(8,128)S(1)}, f32[1024,1]{1,0:T(8,128)}, u32[]{:S(2)}) copy-start(f32[1024,1]{1,0:T(8,128)} %get-tuple-element.10) | copy-start | bytes 12292
  87.8 1.0 copy-start.2
  89.7 4.2 %copy-start.11 = (bf16[2048,2]{0,1:T(2,128)(2,1)S(1)}, bf16[2048,2]{0,1:T(2,128)(2,1)}, u32[]{:S(2)}) copy-start(bf16[2048,2]{0,1:T(2,128)(2,1)} %param.18) | copy-start | bytes 24580
  89.7 11.2 %all-to-all-start.1 = ((f32[4,260,128]{2,1,0:T(8,128)}), f32[4,260,128]{2,1,0:T(8,128)S(1)}, u32[]{:S(2)}, u32[]{:S(2)}) async-start(f32[4,260,128]{2,1,0:T(8,128)} %pad_maximum_fusion), calls=%async_computation.1 | async-start | bytes 1081344 | tf_op jit(solution)/shard_map/all_to_all | solution.py:214

commit v5 on v4

--- a/solution.py
+++ b/solution.py
@@ -187,7 +187,12 @@
     partner_pairs = [(z, (z + req_count) % ring_z) for z in range(ring_z)]
     partner_kv = lax.ppermute(jnp.stack([keys_new, values_new]), "sz", partner_pairs)
     partner_part = x_index * pair + (pair - 1 - parity)
-    all_queries = lax.all_gather(queries, "sx", axis=0, tiled=True)
+    shifted_queries = [queries] + [
+        lax.ppermute(queries, "sx", [(i, (i + step) % ring_x) for i in range(ring_x)])
+        for step in range(1, ring_x)
+    ]
+    source_step = (x_index - jnp.arange(ring_x, dtype=jnp.int32)) % ring_x
+    all_queries = jnp.take(jnp.stack(shifted_queries), source_step, axis=0)
     query_tok = (
         (jnp.arange(ring_x, dtype=jnp.int32) * pair + parity)[:, None] * tok_rows
         + jnp.arange(tok_rows, dtype=jnp.int32)[None, :]

time: 126 us -> 127 us (level)
  blocking collectives: 44.8 us -> 30.9 us
  starting transfers between devices: 32.3 us -> 41.7 us
  other arithmetic: 7.67 us -> 10.5 us
  local copies, waits for them, and re-layouts: 11.7 us -> 13.7 us
  waiting for transfers between devices: 14.1 us -> 15.6 us
    all_gather x1 -> x0, blocking collectives: 11 us -> none  [per_device(): all_queries = lax.all_gather(queries, 'sx', axis=0, tiled=True)]
    ppermute x0 -> x3, starting transfers between devices: none -> 9.33 us  [per_device(): lax.ppermute(queries, 'sx', [(i, (i + step) % ring_x) for i in range(ring...]
    all_to_all x1, blocking collectives: 19.2 us -> 16.4 us  [per_device(): arrived = lax.all_to_all(pieces, 'tp', 1, 1, tiled=True)]
    unnamed x28 -> x30, local copies, waits for them, and re-layouts: 3.57 us -> 4.19 us
  transfers between devices with their start and end apart: 3 -> 6, of which waited for: 2 -> 2; matrix products, arithmetic and copies ran while one was open for 8% -> 11% of each run, Pallas kernels for 0% -> 0%
where the time goes in v5:
time: 127 us; the launch traced here: 125 us
  starting transfers between devices  41.7 us (33%)
  blocking collectives  30.9 us (24%)
  waiting for transfers between devices  15.6 us (12%)
  local copies, waits for them, and re-layouts  13.7 us (11%)
  other arithmetic  10.5 us (8%)
  Pallas kernels  8.74 us (7%)
  matrix products  2.81 us (2%)
    all_to_all x1, blocking collectives, per_device(): arrived = lax.all_to_all(pieces, 'tp', 1, 1, tiled=True)  16.4 us
    all_to_all x1, starting transfers between devices, per_device(): incoming = lax.all_to_all(cache_both[peer_groups], 'sz', 0, 0, tiled=True)  15.9 us
    all_gather x1, blocking collectives, per_device(): gathered = lax.all_gather(hidden_in, 'tp', axis=1, tiled=True)  14.6 us
    ppermute x1, starting transfers between devices, per_device(): lax.ppermute(jnp.stack([keys_new, values_new]), 'sz', partner_pairs)  12.3 us
    ppermute x3, starting transfers between devices, per_device(): lax.ppermute(queries, 'sx', [(i, (i + step) % ring_x) for i in range(ring...  9.33 us
    pallas_call x1, Pallas kernels, attention(): pl.pallas_call(attention_kernel, out_shape=(jax.ShapeDtypeStruct((rows, w...  8.74 us
    ppermute x1, waiting for transfers between devices, per_device(): lax.ppermute(jnp.stack([keys_new, values_new]), 'sz', partner_pairs)  8.36 us
    all_to_all x1, waiting for transfers between devices, per_device(): packed_in = lax.all_to_all(packed, 'sx', 0, 0, tiled=True)  7.23 us
  transfers between devices with their start and end apart: 6, of which 2 were waited for; matrix products, arithmetic and copies ran while one was open for 11% of the time, Pallas kernels for 0%

profile of v5, /device:TPU:1, one launch (start us, length us, event | category | flops | bytes accessed | tf_op | source)
XLA Modules:
  0.0 125.1 jit_solution(7637021818303119523)
XLA Ops:
  0.0 0.7 copy-done.1
  1.6 1.7 %gather_fusion.2 = bf16[16,2,128,128]{3,2,1,0:T(8,128)(2,1)} fusion(bf16[2,2,128,128]{3,2,0,1:T(8,128)(2,1)S(1)} %pad_maximum_fusion.1, s32[1024]{0:T(1024)S(1)} %pad_clamp_fusion), kind=kCustom, calls=%fused_computation.2 | custom fusion | bytes 2097216 | tf_op jit(solution)/shard_map/gather | solution.py:158
  3.3 15.9 %all-to-all-start = ((bf16[16,2,128,128]{3,2,1,0:T(8,128)(2,1)}), bf16[16,2,128,128]{3,2,1,0:T(8,128)(2,1)S(1)}, u32[]{:S(2)}, u32[]{:S(2)}) async-start(bf16[16,2,128,128]{3,2,1,0:T(8,128)(2,1)} %gather_fusion.2), calls=%async_computation | async-start | bytes 2097152 | tf_op jit(solution)/shard_map/all_to_all | solution.py:158
  19.2 14.6 %all_gather.3 = bf16[128,2048]{1,0:T(8,128)(2,1)S(1)} all-gather(bf16[128,256]{1,0:T(8,128)(2,1)S(1)} %copy-done.4), channel_id=1, replica_groups=mesh['sx'=4,'sz'=16,'tp'=8] {'tp'}, dimensions={1}, use_global_device_ids=true | all-gather | bytes 589824 | tf_op jit(solution)/shard_map/all_gather | solution.py:164
  38.6 4.4 %collective-permute-start.2 = (bf16[128,1,2,128]{3,2,0,1:T(2,128)(2,1)S(1)}, bf16[128,1,2,128]{3,2,0,1:T(2,128)(2,1)S(1)}, u32[]{:S(2)}, u32[]{:S(2)}) collective-permute-start(bf16[128,1,2,128]{3,2,0,1:T(2,128)(2,1)S(1)} %pad_maximum_fusion.2), channel_id=1, source_target_pairs={{0,384},{128,0},{256,128},{384,256},{1,385},{129,1},{257,129},{385... | collective-permute-start | bytes 196616 | tf_op jit(solution)/shard_map/ppermute | solution.py:191
  43.0 2.4 %collective-permute-start.1 = (bf16[128,1,2,128]{3,2,0,1:T(2,128)(2,1)S(1)}, bf16[128,1,2,128]{3,2,0,1:T(2,128)(2,1)S(1)}, u32[]{:S(2)}, u32[]{:S(2)}) collective-permute-start(bf16[128,1,2,128]{3,2,0,1:T(2,128)(2,1)S(1)} %pad_maximum_fusion.2), channel_id=1, source_target_pairs={{0,256},{128,384},{256,0},{384,128},{1,257},{129,385},{257,1},{385... | collective-permute-start | bytes 196616 | tf_op jit(solution)/shard_map/ppermute | solution.py:191
  45.4 2.5 %collective-permute-start = (bf16[128,1,2,128]{3,2,0,1:T(2,128)(2,1)S(1)}, bf16[128,1,2,128]{3,2,0,1:T(2,128)(2,1)S(1)}, u32[]{:S(2)}, u32[]{:S(2)}) collective-permute-start(bf16[128,1,2,128]{3,2,0,1:T(2,128)(2,1)S(1)} %pad_maximum_fusion.2), channel_id=1, source_target_pairs={{0,128},{128,256},{256,384},{384,0},{1,129},{129,257},{257,385},{3... | collective-permute-start | bytes 196616 | tf_op jit(solution)/shard_map/ppermute | solution.py:191
  49.5 1.4 %convolution_convert_fusion.1 = bf16[128,128]{1,0:T(8,128)(2,1)S(1)} fusion(bf16[2048,128]{1,0:T(8,128)(2,1)} %param.17, bf16[128,2048]{1,0:T(8,128)(2,1)S(1)} %all_gather.3, f32[2048]{0:T(1024)S(1)} %copy-done.13, f32[128]{0:T(128)S(1)} %add_rsqrt_fusion.2), kind=kOutput, calls=%fused_computation.6 | convolution fusion | flops 68173824 | bytes 1090048 | tf_op jit(solution)/shard_map/dot_general | solution.py:179
  50.9 0.7 pad_maximum_fusion.3
  51.6 12.3 %collective-permute-start.3 = (bf16[2,128,1,128]{3,1,2,0:T(8,128)(2,1)}, bf16[2,128,1,128]{3,1,2,0:T(8,128)(2,1)S(1)}, u32[]{:S(2)}, u32[]{:S(2)}) collective-permute-start(bf16[2,128,1,128]{3,1,2,0:T(8,128)(2,1)} %pad_maximum_fusion.3), channel_id=1, source_target_pairs={{0,64},{8,72},{16,80},{24,88},{32,96},{40,104},{48,112},{56,120},{... | collective-permute-start | bytes 196616 | tf_op jit(solution)/shard_map/ppermute | solution.py:188
  64.4 1.0 broadcast_in_dim_reshape.5.qtok_ref
  66.0 1.3 %pad_add_fusion.1.scalars = s32[2]{0:T(128)} fusion(s32[1]{0:T(128)} %bitcast, s32[1]{0:T(128)} %dynamic_slice.3), kind=kLoop, calls=%fused_computation.76 | loop fusion | flops 2 | bytes 16 | tf_op jit(solution)/shard_map/stack | solution.py:205
  68.0 1.2 maximum_bitcast_fusion
  69.2 1.1 gather_fusion
  70.3 8.4 %collective-permute-done.3 = bf16[2,128,1,128]{3,1,2,0:T(8,128)(2,1)S(1)} collective-permute-done((bf16[2,128,1,128]{3,1,2,0:T(8,128)(2,1)}, bf16[2,128,1,128]{3,1,2,0:T(8,128)(2,1)S(1)}, u32[]{:S(2)}, u32[]{:S(2)}) %collective-permute-start.3) | collective-permute-done | bytes 65568 | tf_op jit(solution)/shard_map/ppermute | solution.py:188
  78.6 0.7 maximum_bitcast_fusion.1
  79.4 0.9 broadcast_select_fusion.q_ref
  80.3 1.1 fusion.28
  81.4 8.7 %shard_map.127 = (f32[1024,128]{1,0:T(8,128)}, f32[1024,1]{1,0:T(8,128)}, f32[1024,1]{1,0:T(8,128)}) custom-call(s32[2]{0:T(128)} %pad_add_fusion.1.scalars, bf16[1024,128]{1,0:T(8,128)(2,1)} %broadcast_select_fusion.q_ref, s32[1024,1]{1,0:T(8,128)} %broadcast_in_dim_reshape.5.qtok_ref, bf16[2048,128]{1,0:T(8,128)(2,1)} %bitcast.81, ...), custom_call_target="tpu_custom_call" | custom-call | flops 1207959552 | bytes 1966080 | tf_op jit(solution)/shard_map/pallas_call | solution.py:94
  90.1 1.3 %copy.65 = f32[1024,1]{0,1:T(1,128)S(1)} copy(f32[1024,1]{1,0:T(8,128)} %get-tuple-element.9) | data formatting | bytes 8192 | tf_op jit(solution)/shard_map/pallas_call | solution.py:94
  92.7 0.8 pad_maximum_fusion
  93.5 4.2 %all-to-all-start.1 = ((f32[4,260,128]{2,1,0:T(8,128)}), f32[4,260,128]{2,1,0:T(8,128)S(1)}, u32[]{:S(2)}, u32[]{:S(2)}) async-start(f32[4,260,128]{2,1,0:T(8,128)} %pad_maximum_fusion), calls=%async_computation.1 | async-start | bytes 1081344 | tf_op jit(solution)/shard_map/all_to_all | solution.py:219
  98.2 7.2 %all-to-all-done.1 = f32[4,260,128]{2,1,0:T(8,128)S(1)} async-done(((f32[4,260,128]{2,1,0:T(8,128)}), f32[4,260,128]{2,1,0:T(8,128)S(1)}, u32[]{:S(2)}, u32[]{:S(2)}) %all-to-all-start.1) | async-done | bytes 532512 | tf_op jit(solution)/shard_map/all_to_all | solution.py:219
  108.0 16.4 %all_to_all.15 = bf16[128,8,256]{2,0,1:T(8,128)(2,1)S(1)} all-to-all(bf16[128,8,256]{2,0,1:T(8,128)(2,1)S(1)} %bitcast.69), channel_id=1, replica_groups=mesh['sx'=4,'sz'=16,'tp'=8] {'tp'}, dimensions={1} | all-to-all | bytes 1048576 | tf_op jit(solution)/shard_map/all_to_all | solution.py:234
  (88 shorter events, 13.1 us)
Async XLA Ops:
  0.0 107.6 %copy-start = (bf16[256,2048]{1,0:T(8,128)(2,1)S(1)}, bf16[256,2048]{1,0:T(8,128)(2,1)}, u32[]{:S(2)}) copy-start(bf16[256,2048]{1,0:T(8,128)(2,1)} %param.19) | copy-start | bytes 3145732
  0.0 0.7 copy-start.1
  0.8 0.8 copy-start.6
  0.8 0.9 copy-start.7
  3.3 15.9 %copy-start.4 = (bf16[128,256]{1,0:T(8,128)(2,1)S(1)}, bf16[128,256]{1,0:T(8,128)(2,1)}, u32[]{:S(2)}) copy-start(bf16[128,256]{1,0:T(8,128)(2,1)} %param.13) | copy-start | bytes 196612
  3.3 77.0 %all-to-all-start = ((bf16[16,2,128,128]{3,2,1,0:T(8,128)(2,1)}), bf16[16,2,128,128]{3,2,1,0:T(8,128)(2,1)S(1)}, u32[]{:S(2)}, u32[]{:S(2)}) async-start(bf16[16,2,128,128]{3,2,1,0:T(8,128)(2,1)} %gather_fusion.2), calls=%async_computation | async-start | bytes 2097152 | tf_op jit(solution)/shard_map/all_to_all | solution.py:158
  19.2 14.8 %copy-start.10 = (bf16[2048,256]{1,0:T(8,128)(2,1)S(1)}, bf16[2048,256]{1,0:T(8,128)(2,1)}, u32[]{:S(2)}) copy-start(bf16[2048,256]{1,0:T(8,128)(2,1)} %param.15) | copy-start | bytes 3145732
  33.8 0.7 copy-start.13
  35.2 0.7 copy-start.14
  37.2 0.7 copy-start.8
  37.9 10.0 %copy-start.11 = (bf16[2048,128]{1,0:T(8,128)(2,1)S(1)}, bf16[2048,128]{1,0:T(8,128)(2,1)}, u32[]{:S(2)}) copy-start(bf16[2048,128]{1,0:T(8,128)(2,1)} %param.16) | copy-start | bytes 1572868
  38.6 28.8 %collective-permute-start.2 = (bf16[128,1,2,128]{3,2,0,1:T(2,128)(2,1)S(1)}, bf16[128,1,2,128]{3,2,0,1:T(2,128)(2,1)S(1)}, u32[]{:S(2)}, u32[]{:S(2)}) collective-permute-start(bf16[128,1,2,128]{3,2,0,1:T(2,128)(2,1)S(1)} %pad_maximum_fusion.2), channel_id=1, source_target_pairs={{0,384},{128,0},{256,128},{384,256},{1,385},{129,1},{257,129},{385... | collective-permute-start | bytes 196616 | tf_op jit(solution)/shard_map/ppermute | solution.py:191
  43.0 24.4 %collective-permute-start.1 = (bf16[128,1,2,128]{3,2,0,1:T(2,128)(2,1)S(1)}, bf16[128,1,2,128]{3,2,0,1:T(2,128)(2,1)S(1)}, u32[]{:S(2)}, u32[]{:S(2)}) collective-permute-start(bf16[128,1,2,128]{3,2,0,1:T(2,128)(2,1)S(1)} %pad_maximum_fusion.2), channel_id=1, source_target_pairs={{0,256},{128,384},{256,0},{384,128},{1,257},{129,385},{257,1},{385... | collective-permute-start | bytes 196616 | tf_op jit(solution)/shard_map/ppermute | solution.py:191
  45.4 22.0 %collective-permute-start = (bf16[128,1,2,128]{3,2,0,1:T(2,128)(2,1)S(1)}, bf16[128,1,2,128]{3,2,0,1:T(2,128)(2,1)S(1)}, u32[]{:S(2)}, u32[]{:S(2)}) collective-permute-start(bf16[128,1,2,128]{3,2,0,1:T(2,128)(2,1)S(1)} %pad_maximum_fusion.2), channel_id=1, source_target_pairs={{0,128},{128,256},{256,384},{384,0},{1,129},{129,257},{257,385},{3... | collective-permute-start | bytes 196616 | tf_op jit(solution)/shard_map/ppermute | solution.py:191
  48.4 0.7 copy-start.9
  51.6 27.0 %collective-permute-start.3 = (bf16[2,128,1,128]{3,1,2,0:T(8,128)(2,1)}, bf16[2,128,1,128]{3,1,2,0:T(8,128)(2,1)S(1)}, u32[]{:S(2)}, u32[]{:S(2)}) collective-permute-start(bf16[2,128,1,128]{3,1,2,0:T(8,128)(2,1)} %pad_maximum_fusion.3), channel_id=1, source_target_pairs={{0,64},{8,72},{16,80},{24,88},{32,96},{40,104},{48,112},{56,120},{... | collective-permute-start | bytes 196616 | tf_op jit(solution)/shard_map/ppermute | solution.py:188
  67.4 0.6 copy-start.5
  90.1 1.3 %copy-start.3 = (f32[1024,1]{1,0:T(8,128)S(1)}, f32[1024,1]{1,0:T(8,128)}, u32[]{:S(2)}) copy-start(f32[1024,1]{1,0:T(8,128)} %get-tuple-element.10) | copy-start | bytes 12292
  91.6 1.0 copy-start.2
  93.5 4.2 %copy-start.12 = (bf16[2048,2]{0,1:T(2,128)(2,1)S(1)}, bf16[2048,2]{0,1:T(2,128)(2,1)}, u32[]{:S(2)}) copy-start(bf16[2048,2]{0,1:T(2,128)(2,1)} %param.18) | copy-start | bytes 24580
  93.5 11.9 %all-to-all-start.1 = ((f32[4,260,128]{2,1,0:T(8,128)}), f32[4,260,128]{2,1,0:T(8,128)S(1)}, u32[]{:S(2)}, u32[]{:S(2)}) async-start(f32[4,260,128]{2,1,0:T(8,128)} %pad_maximum_fusion), calls=%async_computation.1 | async-start | bytes 1081344 | tf_op jit(solution)/shard_map/all_to_all | solution.py:219

commit v6 on v5

--- a/solution.py
+++ b/solution.py
@@ -161,32 +161,36 @@
     values_cache = incoming[:, 1].reshape(cache_rows, kv_local, head_dim)
     cache_pos = x_index * cache_rows + jnp.arange(cache_rows, dtype=jnp.int32)
 
-    gathered = lax.all_gather(hidden_in, "tp", axis=1, tiled=True)
+    partner_pairs = [(z, (z + req_count) % ring_z) for z in range(ring_z)]
+    partner_hidden = lax.ppermute(hidden_in, "sz", partner_pairs)
+    partner_part = x_index * pair + (pair - 1 - parity)
+    both_hidden = jnp.concatenate([hidden_in, partner_hidden], 0)
+    gathered = lax.all_gather(both_hidden, "tp", axis=1, tiled=True)
     widened = gathered.astype(jnp.float32)
     normed = (
         widened * lax.rsqrt(jnp.mean(widened * widened, -1, keepdims=True) + norm_eps) * norm_gain
     ).astype(jnp.bfloat16)
-    positions = length + local_part * tok_rows + jnp.arange(tok_rows, dtype=jnp.int32)
-    query_raw = jnp.dot(normed, w_query, preferred_element_type=jnp.float32).reshape(
+    row_ids = jnp.arange(tok_rows, dtype=jnp.int32)
+    key_tok = jnp.concatenate([local_part * tok_rows + row_ids, partner_part * tok_rows + row_ids])
+    positions = length + key_tok
+    own_normed = normed[:tok_rows]
+    query_raw = jnp.dot(own_normed, w_query, preferred_element_type=jnp.float32).reshape(
         tok_rows, kv_local, group_size, head_dim
     )
-    queries = rotate(head_norm(query_raw, q_gain), positions).astype(jnp.bfloat16)
+    queries = rotate(head_norm(query_raw, q_gain), positions[:tok_rows]).astype(jnp.bfloat16)
     key_raw = jnp.dot(normed, w_key, preferred_element_type=jnp.float32).reshape(
-        tok_rows, kv_local, head_dim
-    )
-    keys_new = rotate(head_norm(key_raw, k_gain), positions).astype(jnp.bfloat16)
-    values_new = (
+        2 * tok_rows, kv_local, head_dim
+    )
+    keys_two = rotate(head_norm(key_raw, k_gain), positions).astype(jnp.bfloat16).reshape(-1, head_dim)
+    values_two = (
         jnp.dot(normed, w_value, preferred_element_type=jnp.float32)
         .astype(jnp.bfloat16)
-        .reshape(tok_rows, kv_local, head_dim)
-    )
-    gates = jax.nn.sigmoid(jnp.dot(normed, w_headgate, preferred_element_type=jnp.float32)).reshape(
-        tok_rows, kv_local, group_size
-    )
-
-    partner_pairs = [(z, (z + req_count) % ring_z) for z in range(ring_z)]
-    partner_kv = lax.ppermute(jnp.stack([keys_new, values_new]), "sz", partner_pairs)
-    partner_part = x_index * pair + (pair - 1 - parity)
+        .reshape(-1, head_dim)
+    )
+    gates = jax.nn.sigmoid(
+        jnp.dot(own_normed, w_headgate, preferred_element_type=jnp.float32)
+    ).reshape(tok_rows, kv_local, group_size)
+
     shifted_queries = [queries] + [
         lax.ppermute(queries, "sx", [(i, (i + step) % ring_x) for i in range(ring_x)])
         for step in range(1, ring_x)
@@ -197,10 +201,6 @@
         (jnp.arange(ring_x, dtype=jnp.int32) * pair + parity)[:, None] * tok_rows
         + jnp.arange(tok_rows, dtype=jnp.int32)[None, :]
     ).reshape(-1)
-    row_ids = jnp.arange(tok_rows, dtype=jnp.int32)
-    key_tok = jnp.concatenate([local_part * tok_rows + row_ids, partner_part * tok_rows + row_ids])
-    keys_two = jnp.concatenate([keys_new, partner_kv[0]], 0).reshape(-1, head_dim)
-    values_two = jnp.concatenate([values_new, partner_kv[1]], 0).reshape(-1, head_dim)
     query_count = query_tok.shape[0]
     scalars = jnp.stack([length, x_index * cache_rows]).astype(jnp.int32)
     acc, top, total = attention(

time: 127 us -> 142 us (1.12)
  between operations: 1.15 us -> 13.9 us
  blocking collectives: 30.9 us -> 19.4 us
  waiting for transfers between devices: 15.6 us -> 24.1 us
  other arithmetic: 10.5 us -> 17.6 us
    all_gather x0 -> x1, waiting for transfers between devices: none -> 16.8 us  [per_device(): gathered = lax.all_gather(both_hidden, 'tp', axis=1, tiled=True)]
    all_gather x1 -> x0, blocking collectives: 14.6 us -> none  [per_device(): gathered = lax.all_gather(hidden_in, 'tp', axis=1, tiled=True)]
    ppermute x1, waiting for transfers between devices: 8.36 us -> 0.72 us  [per_device(): partner_hidden = lax.ppermute(hidden_in, 'sz', partner_pairs)]
    ppermute x1, starting transfers between devices: 12.3 us -> 16.4 us  [per_device(): partner_hidden = lax.ppermute(hidden_in, 'sz', partner_pairs)]
    all_to_all x1, starting transfers between devices: 15.9 us -> 11.8 us  [per_device(): incoming = lax.all_to_all(cache_both[peer_groups], 'sz', 0, 0, tiled=True)]
    unnamed x30 -> x22, local copies, waits for them, and re-layouts: 4.19 us -> 0.95 us
    all_to_all x1, blocking collectives: 16.4 us -> 19.4 us  [per_device(): arrived = lax.all_to_all(pieces, 'tp', 1, 1, tiled=True)]
    concatenate x1 -> x3, other arithmetic: 0.18 us -> 2.71 us  [rotate(): jnp.concatenate([first * cosine - second * sine, second * cosine + first...]
  transfers between devices with their start and end apart: 6 -> 7, of which waited for: 2 -> 3; matrix products, arithmetic and copies ran while one was open for 11% -> 16% of each run, Pallas kernels for 0% -> 0%
where the time goes in v6:
time: 142 us; the launch traced here: 141 us
  starting transfers between devices  40.9 us (29%)
  waiting for transfers between devices  24.1 us (17%)
  blocking collectives  19.4 us (14%)
  other arithmetic  17.6 us (12%)
  between operations  13.9 us (10%)
  local copies, waits for them, and re-layouts  12.7 us (9%)
  Pallas kernels  8.73 us (6%)
  matrix products  3.46 us (2%)
    all_to_all x1, blocking collectives, per_device(): arrived = lax.all_to_all(pieces, 'tp', 1, 1, tiled=True)  19.4 us
    all_gather x1, waiting for transfers between devices, per_device(): gathered = lax.all_gather(both_hidden, 'tp', axis=1, tiled=True)  16.8 us
    ppermute x1, starting transfers between devices, per_device(): partner_hidden = lax.ppermute(hidden_in, 'sz', partner_pairs)  16.4 us
    all_to_all x1, starting transfers between devices, per_device(): incoming = lax.all_to_all(cache_both[peer_groups], 'sz', 0, 0, tiled=True)  11.8 us
    ppermute x3, starting transfers between devices, per_device(): lax.ppermute(queries, 'sx', [(i, (i + step) % ring_x) for i in range(ring...  9.26 us
    pallas_call x1, Pallas kernels, attention(): pl.pallas_call(attention_kernel, out_shape=(jax.ShapeDtypeStruct((rows, w...  8.73 us
    all_to_all x1, waiting for transfers between devices, per_device(): packed_in = lax.all_to_all(packed, 'sx', 0, 0, tiled=True)  6.6 us
    all_to_all x1, starting transfers between devices, per_device(): packed_in = lax.all_to_all(packed, 'sx', 0, 0, tiled=True)  3.47 us
  transfers between devices with their start and end apart: 7, of which 3 were waited for; matrix products, arithmetic and copies ran while one was open for 16% of the time, Pallas kernels for 0%

profile of v6, /device:TPU:1, one launch (start us, length us, event | category | flops | bytes accessed | tf_op | source)
XLA Modules:
  0.0 140.8 jit_solution(4629069107602098353)
XLA Ops:
  6.5 16.4 %collective-permute-start = (bf16[128,256]{1,0:T(8,128)(2,1)}, bf16[128,256]{1,0:T(8,128)(2,1)S(1)}, u32[]{:S(2)}, u32[]{:S(2)}) collective-permute-start(bf16[128,256]{1,0:T(8,128)(2,1)} %param.13), channel_id=1, source_target_pairs={{0,64},{8,72},{16,80},{24,88},{32,96},{40,104},{48,112},{56,120},{... | collective-permute-start | bytes 196616 | tf_op jit(solution)/shard_map/ppermute | solution.py:165
  23.0 1.3 gather_fusion.1
  25.0 1.5 %pad_maximum_fusion.1 = bf16[256,256]{1,0:T(8,128)(2,1)} fusion(bf16[128,256]{1,0:T(8,128)(2,1)S(1)} %collective-permute-done, bf16[128,256]{1,0:T(8,128)(2,1)} %param.13), kind=kLoop, calls=%fused_computation.37 | loop fusion | flops 262144 | bytes 262144 | tf_op jit(solution)/shard_map/concatenate | solution.py:167
  27.4 1.7 %gather_fusion.2 = bf16[16,2,128,128]{3,2,1,0:T(8,128)(2,1)} fusion(bf16[2,2,128,128]{3,2,0,1:T(8,128)(2,1)S(1)} %pad_maximum_fusion.2, s32[1024]{0:T(1024)S(1)} %pad_clamp_fusion), kind=kCustom, calls=%fused_computation.2 | custom fusion | bytes 2097216 | tf_op jit(solution)/shard_map/gather | solution.py:158
  29.1 11.8 %all-to-all-start = ((bf16[16,2,128,128]{3,2,1,0:T(8,128)(2,1)}), bf16[16,2,128,128]{3,2,1,0:T(8,128)(2,1)S(1)}, u32[]{:S(2)}, u32[]{:S(2)}) async-start(bf16[16,2,128,128]{3,2,1,0:T(8,128)(2,1)} %gather_fusion.2), calls=%async_computation | async-start | bytes 2097152 | tf_op jit(solution)/shard_map/all_to_all | solution.py:158
  41.6 1.2 fusion.27
  43.2 1.3 pad_add_fusion.1.scalars
  45.9 16.8 %all-gather.2.cloned.1.call-done = bf16[256,2048]{1,0:T(8,128)(2,1)} async-done(((bf16[256,256]{1,0:T(8,128)(2,1)}), bf16[256,2048]{1,0:T(8,128)(2,1)}) %all-gather.2.cloned.1.call-update) | async-done | bytes 1048592 | tf_op jit(solution)/shard_map/all_gather | solution.py:168
  62.7 1.6 %fusion = f32[256]{0:T(256)S(1)} fusion(bf16[256,2048]{1,0:T(8,128)(2,1)} %all-gather.2.cloned.1.call-done), kind=kLoop, calls=%fused_computation.6 | loop fusion | flops 1572608 | bytes 1049600 | tf_op jit(solution)/shard_map/reduce_sum | solution.py:171
  67.5 4.3 %collective-permute-start.3 = (bf16[128,1,2,128]{3,2,0,1:T(2,128)(2,1)}, bf16[128,1,2,128]{3,2,0,1:T(2,128)(2,1)}, u32[]{:S(2)}, u32[]{:S(2)}) collective-permute-start(bf16[128,1,2,128]{3,2,0,1:T(2,128)(2,1)} %pad_maximum_fusion.3), channel_id=1, source_target_pairs={{0,384},{128,0},{256,128},{384,256},{1,385},{129,1},{257,129},{385... | collective-permute-start | bytes 196616 | tf_op jit(solution)/shard_map/ppermute | solution.py:195
  71.8 2.5 %collective-permute-start.2 = (bf16[128,1,2,128]{3,2,0,1:T(2,128)(2,1)}, bf16[128,1,2,128]{3,2,0,1:T(2,128)(2,1)}, u32[]{:S(2)}, u32[]{:S(2)}) collective-permute-start(bf16[128,1,2,128]{3,2,0,1:T(2,128)(2,1)} %pad_maximum_fusion.3), channel_id=1, source_target_pairs={{0,256},{128,384},{256,0},{384,128},{1,257},{129,385},{257,1},{385... | collective-permute-start | bytes 196616 | tf_op jit(solution)/shard_map/ppermute | solution.py:195
  74.3 2.5 %collective-permute-start.1 = (bf16[128,1,2,128]{3,2,0,1:T(2,128)(2,1)}, bf16[128,1,2,128]{3,2,0,1:T(2,128)(2,1)}, u32[]{:S(2)}, u32[]{:S(2)}) collective-permute-start(bf16[128,1,2,128]{3,2,0,1:T(2,128)(2,1)} %pad_maximum_fusion.3), channel_id=1, source_target_pairs={{0,128},{128,256},{256,384},{384,0},{1,129},{129,257},{257,385},{3... | collective-permute-start | bytes 196616 | tf_op jit(solution)/shard_map/ppermute | solution.py:195
  78.2 1.2 fusion.21
  79.4 2.1 %convolution_convert_fusion.1.vn_ref = bf16[256,128]{1,0:T(8,128)(2,1)} fusion(bf16[256,2048]{1,0:T(8,128)(2,1)S(1)} %fusion.2, bf16[2048,128]{1,0:T(8,128)(2,1)} %param.17), kind=kOutput, calls=%fused_computation.9 | convolution fusion | flops 134250496 | bytes 1638400 | tf_op jit(solution)/shard_map/dot_general | solution.py:186
  82.2 1.3 maximum_bitcast_fusion
  83.4 1.8 %gather_fusion = bf16[4,128,2,128]{3,2,1,0:T(2,128)(2,1)} fusion(bf16[4,128,2,128]{3,2,1,0:T(2,128)(2,1)S(1)} %maximum_bitcast_fusion, s32[1024]{0:T(1024)S(1)} %pad_clamp_fusion.2), kind=kCustom, calls=%fused_computation | custom fusion | bytes 524304 | tf_op jit(solution)/shard_map/jit(_take)/gather | solution.py:199
  85.2 1.9 %broadcast_select_fusion.q_ref = bf16[1024,128]{1,0:T(8,128)(2,1)} fusion(bf16[1024,128]{1,0:T(8,128)(2,1)} %bitcast.67, pred[1024]{0:T(1024)(128)(4,1)S(1)} %broadcast_in_dim.19), kind=kLoop, calls=%fused_computation.23 | loop fusion | flops 131072 | bytes 525312 | tf_op jit(solution)/shard_map/jit(_take)/select_n | solution.py:199
  87.0 1.1 fusion.28
  88.1 8.7 %shard_map.127 = (f32[1024,128]{1,0:T(8,128)}, f32[1024,1]{1,0:T(8,128)}, f32[1024,1]{1,0:T(8,128)}) custom-call(s32[2]{0:T(128)} %pad_add_fusion.1.scalars, bf16[1024,128]{1,0:T(8,128)(2,1)} %broadcast_select_fusion.q_ref, s32[1024,1]{1,0:T(8,128)} %broadcast_in_dim_reshape.5.qtok_ref, bf16[2048,128]{1,0:T(8,128)(2,1)} %bitcast.75, ...), custom_call_target="tpu_custom_call" | custom-call | flops 1207959552 | bytes 1966080 | tf_op jit(solution)/shard_map/pallas_call | solution.py:94
  96.9 1.3 copy.65
  98.1 1.2 copy.66
  100.8 3.5 %all-to-all-start.1 = ((f32[4,260,128]{2,1,0:T(8,128)}), f32[4,260,128]{2,1,0:T(8,128)S(1)}, u32[]{:S(2)}, u32[]{:S(2)}) async-start(f32[4,260,128]{2,1,0:T(8,128)} %pad_maximum_fusion), calls=%async_computation.1 | async-start | bytes 1081344 | tf_op jit(solution)/shard_map/all_to_all | solution.py:219
  104.6 6.6 %all-to-all-done.1 = f32[4,260,128]{2,1,0:T(8,128)S(1)} async-done(((f32[4,260,128]{2,1,0:T(8,128)}), f32[4,260,128]{2,1,0:T(8,128)S(1)}, u32[]{:S(2)}, u32[]{:S(2)}) %all-to-all-start.1) | async-done | bytes 532512 | tf_op jit(solution)/shard_map/all_to_all | solution.py:219
  113.8 19.4 %all_to_all.15 = bf16[128,8,256]{2,0,1:T(8,128)(2,1)S(1)} all-to-all(bf16[128,8,256]{2,0,1:T(8,128)(2,1)S(1)} %bitcast.63), channel_id=1, replica_groups=mesh['sx'=4,'sz'=16,'tp'=8] {'tp'}, dimensions={1} | all-to-all | bytes 1048576 | tf_op jit(solution)/shard_map/all_to_all | solution.py:234
  (82 shorter events, 14.2 us)
Async XLA Ops:
  6.5 106.9 %copy-start = (bf16[256,2048]{1,0:T(8,128)(2,1)S(1)}, bf16[256,2048]{1,0:T(8,128)(2,1)}, u32[]{:S(2)}) copy-start(bf16[256,2048]{1,0:T(8,128)(2,1)} %param.19) | copy-start | bytes 3145732
  6.5 56.1 %all-gather.2.cloned.1.call-start = ((), (), s32[]{:S(2)}) async-start(), calls=%async_computation.3 | async-start | bytes 1179648 | tf_op jit(solution)/shard_map/all_gather | solution.py:168
  6.5 18.5 %collective-permute-start = (bf16[128,256]{1,0:T(8,128)(2,1)}, bf16[128,256]{1,0:T(8,128)(2,1)S(1)}, u32[]{:S(2)}, u32[]{:S(2)}) collective-permute-start(bf16[128,256]{1,0:T(8,128)(2,1)} %param.13), channel_id=1, source_target_pairs={{0,64},{8,72},{16,80},{24,88},{32,96},{40,104},{48,112},{56,120},{... | collective-permute-start | bytes 196616 | tf_op jit(solution)/shard_map/ppermute | solution.py:165
  29.1 11.8 %copy-start.10 = (s32[8]{0:T(128)S(1)}, s32[8]{0:T(128)}, u32[]{:S(2)}) copy-start(s32[8]{0:T(128)} %param.24) | copy-start | bytes 100
  29.1 57.9 %all-to-all-start = ((bf16[16,2,128,128]{3,2,1,0:T(8,128)(2,1)}), bf16[16,2,128,128]{3,2,1,0:T(8,128)(2,1)S(1)}, u32[]{:S(2)}, u32[]{:S(2)}) async-start(bf16[16,2,128,128]{3,2,1,0:T(8,128)(2,1)} %gather_fusion.2), calls=%async_computation | async-start | bytes 2097152 | tf_op jit(solution)/shard_map/all_to_all | solution.py:158
  41.5 3.3 %copy-start.7 = (f32[64]{0:T(128)}, f32[64]{0:T(128)S(1)}, u32[]{:S(2)}) copy-start(f32[64]{0:T(128)S(1)} %multiply_exponential_fusion) | copy-start | bytes 772
  44.7 19.5 %copy-start.6 = (f32[2048]{0:T(1024)S(1)}, f32[2048]{0:T(1024)}, u32[]{:S(2)}) copy-start(f32[2048]{0:T(1024)} %param.14) | copy-start | bytes 24580
  62.7 1.6 %copy-start.1 = (bf16[256,2048]{1,0:T(8,128)(2,1)S(1)}, bf16[256,2048]{1,0:T(8,128)(2,1)}, u32[]{:S(2)}) copy-start(bf16[256,2048]{1,0:T(8,128)(2,1)} %all-gather.2.cloned.1.call-done) | copy-start | bytes 3145732
  64.3 1.2 copy-start.2
  65.5 0.7 copy-start.8
  65.9 10.9 %copy-start.3 = (bf16[2048,128]{1,0:T(8,128)(2,1)S(1)}, bf16[2048,128]{1,0:T(8,128)(2,1)}, u32[]{:S(2)}) copy-start(bf16[2048,128]{1,0:T(8,128)(2,1)} %param.16) | copy-start | bytes 1572868
  67.5 14.7 %collective-permute-start.3 = (bf16[128,1,2,128]{3,2,0,1:T(2,128)(2,1)}, bf16[128,1,2,128]{3,2,0,1:T(2,128)(2,1)}, u32[]{:S(2)}, u32[]{:S(2)}) collective-permute-start(bf16[128,1,2,128]{3,2,0,1:T(2,128)(2,1)} %pad_maximum_fusion.3), channel_id=1, source_target_pairs={{0,384},{128,0},{256,128},{384,256},{1,385},{129,1},{257,129},{385... | collective-permute-start | bytes 196616 | tf_op jit(solution)/shard_map/ppermute | solution.py:195
  71.8 10.4 %collective-permute-start.2 = (bf16[128,1,2,128]{3,2,0,1:T(2,128)(2,1)}, bf16[128,1,2,128]{3,2,0,1:T(2,128)(2,1)}, u32[]{:S(2)}, u32[]{:S(2)}) collective-permute-start(bf16[128,1,2,128]{3,2,0,1:T(2,128)(2,1)} %pad_maximum_fusion.3), channel_id=1, source_target_pairs={{0,256},{128,384},{256,0},{384,128},{1,257},{129,385},{257,1},{385... | collective-permute-start | bytes 196616 | tf_op jit(solution)/shard_map/ppermute | solution.py:195
  74.3 7.9 %collective-permute-start.1 = (bf16[128,1,2,128]{3,2,0,1:T(2,128)(2,1)}, bf16[128,1,2,128]{3,2,0,1:T(2,128)(2,1)}, u32[]{:S(2)}, u32[]{:S(2)}) collective-permute-start(bf16[128,1,2,128]{3,2,0,1:T(2,128)(2,1)} %pad_maximum_fusion.3), channel_id=1, source_target_pairs={{0,128},{128,256},{256,384},{384,0},{1,129},{129,257},{257,385},{3... | collective-permute-start | bytes 196616 | tf_op jit(solution)/shard_map/ppermute | solution.py:195
  96.9 3.1 %copy-start.4 = (f32[1024,128]{1,0:T(8,128)S(1)}, f32[1024,128]{1,0:T(8,128)}, u32[]{:S(2)}) copy-start(f32[1024,128]{1,0:T(8,128)} %get-tuple-element.8) | copy-start | bytes 1572868
  99.9 4.3 %copy-start.9 = (bf16[2048,2]{0,1:T(2,128)(2,1)S(1)}, bf16[2048,2]{0,1:T(2,128)(2,1)}, u32[]{:S(2)}) copy-start(bf16[2048,2]{0,1:T(2,128)(2,1)} %param.18) | copy-start | bytes 24580
  100.8 10.5 %all-to-all-start.1 = ((f32[4,260,128]{2,1,0:T(8,128)}), f32[4,260,128]{2,1,0:T(8,128)S(1)}, u32[]{:S(2)}, u32[]{:S(2)}) async-start(f32[4,260,128]{2,1,0:T(8,128)} %pad_maximum_fusion), calls=%async_computation.1 | async-start | bytes 1081344 | tf_op jit(solution)/shard_map/all_to_all | solution.py:219
  113.8 19.5 %copy-start.5 = (bf16[128,256]{1,0:T(8,128)(2,1)S(1)}, bf16[128,256]{1,0:T(8,128)(2,1)}, u32[]{:S(2)}) copy-start(bf16[128,256]{1,0:T(8,128)(2,1)} %param.13) | copy-start | bytes 196612
Sparse Core Ops, SparseCore 0:
  26.6 35.9 all-gather.1

commit v7 on v4

--- a/solution.py
+++ b/solution.py
@@ -64,23 +64,48 @@
     scale = q_ref.shape[-1] ** (-0.5)
     dims = (((1,), (1,)), ((), ()))
     q = q_ref[...]
-    cache_scores = lax.dot_general(q, kc_ref[...], dims, preferred_element_type=jnp.float32) * scale
-    cache_pos = scalars[1] + lax.broadcasted_iota(jnp.int32, (1, kc_ref.shape[0]), 1)
-    cache_seen = cache_pos < scalars[0]
-    cache_scores = jnp.where(cache_seen, cache_scores, masked_score)
     new_scores = lax.dot_general(q, kn_ref[...], dims, preferred_element_type=jnp.float32) * scale
     new_seen = ktok_ref[...] <= qtok_ref[...]
     new_scores = jnp.where(new_seen, new_scores, masked_score)
-    top = jnp.maximum(
-        jnp.max(cache_scores, 1, keepdims=True), jnp.max(new_scores, 1, keepdims=True)
-    )
-    cache_expo = jnp.where(cache_seen, jnp.exp(cache_scores - top), 0.0)
-    new_expo = jnp.where(new_seen, jnp.exp(new_scores - top), 0.0)
-    total_ref[...] = jnp.sum(cache_expo, 1, keepdims=True) + jnp.sum(new_expo, 1, keepdims=True)
-    top_ref[...] = top
-    acc_ref[...] = jnp.dot(
-        cache_expo.astype(jnp.bfloat16), vc_ref[...], preferred_element_type=jnp.float32
-    ) + jnp.dot(new_expo.astype(jnp.bfloat16), vn_ref[...], preferred_element_type=jnp.float32)
+    new_top = jnp.max(new_scores, 1, keepdims=True)
+    cache_rows = kc_ref.shape[0]
+    length, start = scalars[0], scalars[1]
+
+    def finish(top, cache_total, cache_acc):
+        new_expo = jnp.where(new_seen, jnp.exp(new_scores - top), 0.0)
+        total_ref[...] = cache_total + jnp.sum(new_expo, 1, keepdims=True)
+        top_ref[...] = top
+        acc_ref[...] = cache_acc + jnp.dot(
+            new_expo.astype(jnp.bfloat16), vn_ref[...], preferred_element_type=jnp.float32
+        )
+
+    def cache_part(masked):
+        cache_scores = (
+            lax.dot_general(q, kc_ref[...], dims, preferred_element_type=jnp.float32) * scale
+        )
+        if masked:
+            cache_seen = start + lax.broadcasted_iota(jnp.int32, (1, cache_rows), 1) < length
+            cache_scores = jnp.where(cache_seen, cache_scores, masked_score)
+        top = jnp.maximum(jnp.max(cache_scores, 1, keepdims=True), new_top)
+        cache_expo = jnp.exp(cache_scores - top)
+        if masked:
+            cache_expo = jnp.where(cache_seen, cache_expo, 0.0)
+        cache_acc = jnp.dot(
+            cache_expo.astype(jnp.bfloat16), vc_ref[...], preferred_element_type=jnp.float32
+        )
+        finish(top, jnp.sum(cache_expo, 1, keepdims=True), cache_acc)
+
+    @pl.when(length >= start + cache_rows)
+    def _():
+        cache_part(False)
+
+    @pl.when(jnp.logical_and(length > start, length < start + cache_rows))
+    def _():
+        cache_part(True)
+
+    @pl.when(length <= start)
+    def _():
+        finish(new_top, jnp.zeros_like(new_top), jnp.zeros(acc_ref.shape, jnp.float32))
 
 
 def attention(scalars, q_rows, q_tok, keys_cache, values_cache, keys_new, values_new, key_tok):

time: 126 us -> 126 us (level)
  the two profiles are of different devices: /device:TPU:1 before, /device:TPU:32 now
where the time goes in v7:
time: 126 us
  blocking collectives  41.7 us (33%)
  starting transfers between devices  31 us (25%)
  waiting for transfers between devices  20.1 us (16%)
  local copies, waits for them, and re-layouts  11.7 us (9%)
  Pallas kernels  9.3 us (7%)
  other arithmetic  7.67 us (6%)
  matrix products  2.97 us (2%)
    all_to_all x1, starting transfers between devices, per_device(): incoming = lax.all_to_all(cache_both[peer_groups], 'sz', 0, 0, tiled=True)  15.3 us
    all_to_all x1, blocking collectives, per_device(): arrived = lax.all_to_all(pieces, 'tp', 1, 1, tiled=True)  14.7 us
    all_gather x1, blocking collectives, per_device(): gathered = lax.all_gather(hidden_in, 'tp', axis=1, tiled=True)  13.8 us
    all_gather x1, blocking collectives, per_device(): all_queries = lax.all_gather(queries, 'sx', axis=0, tiled=True)  13.3 us
    ppermute x1, starting transfers between devices, per_device(): lax.ppermute(jnp.stack([keys_new, values_new]), 'sz', partner_pairs)  11.2 us
    ppermute x1, waiting for transfers between devices, per_device(): lax.ppermute(jnp.stack([keys_new, values_new]), 'sz', partner_pairs)  10.7 us
    all_to_all x1, waiting for transfers between devices, per_device(): packed_in = lax.all_to_all(packed, 'sx', 0, 0, tiled=True)  9.38 us
    pallas_call x1, Pallas kernels, attention(): pl.pallas_call(attention_kernel, out_shape=(jax.ShapeDtypeStruct((rows, w...  9.3 us
  transfers between devices with their start and end apart: 3, of which 2 were waited for; matrix products, arithmetic and copies ran while one was open for 7% of the time, Pallas kernels for 0%

profile of v7, /device:TPU:32, one launch (start us, length us, event | category | flops | bytes accessed | tf_op | source)
XLA Modules:
  0.0 125.5 jit_solution(5524383515409967093)
XLA Ops:
  0.0 0.7 copy-done.1
  0.8 0.7 gather_fusion
  1.6 1.6 %gather_fusion.1 = bf16[16,2,128,128]{3,2,1,0:T(8,128)(2,1)} fusion(bf16[2,2,128,128]{3,2,0,1:T(8,128)(2,1)S(1)} %pad_maximum_fusion.1, s32[1024]{0:T(1024)S(1)} %pad_clamp_fusion), kind=kCustom, calls=%fused_computation.1 | custom fusion | bytes 2097216 | tf_op jit(solution)/shard_map/gather | solution.py:183
  3.3 15.3 %all-to-all-start = ((bf16[16,2,128,128]{3,2,1,0:T(8,128)(2,1)}), bf16[16,2,128,128]{3,2,1,0:T(8,128)(2,1)S(1)}, u32[]{:S(2)}, u32[]{:S(2)}) async-start(bf16[16,2,128,128]{3,2,1,0:T(8,128)(2,1)} %gather_fusion.1), calls=%async_computation | async-start | bytes 2097152 | tf_op jit(solution)/shard_map/all_to_all | solution.py:183
  18.7 13.8 %all_gather.6 = bf16[128,2048]{1,0:T(8,128)(2,1)S(1)} all-gather(bf16[128,256]{1,0:T(8,128)(2,1)S(1)} %copy-done.4), channel_id=1, replica_groups=mesh['sx'=4,'sz'=16,'tp'=8] {'tp'}, dimensions={1}, use_global_device_ids=true | all-gather | bytes 589824 | tf_op jit(solution)/shard_map/all_gather | solution.py:189
  33.7 0.6 copy-done.13
  34.3 0.6 dynamic_slice.3
  35.7 0.6 copy-done.7
  37.2 11.2 %collective-permute-start = (bf16[2,128,1,128]{3,1,2,0:T(8,128)(2,1)S(1)}, bf16[2,128,1,128]{3,1,2,0:T(8,128)(2,1)S(1)}, u32[]{:S(2)}, u32[]{:S(2)}) collective-permute-start(bf16[2,128,1,128]{3,1,2,0:T(8,128)(2,1)S(1)} %pad_maximum_fusion.3), channel_id=1, source_target_pairs={{0,64},{8,72},{16,80},{24,88},{32,96},{40,104},{48,112},{56,120},{... | collective-permute-start | bytes 196616 | tf_op jit(solution)/shard_map/ppermute | solution.py:213
  48.7 1.0 broadcast_in_dim_reshape.5.qtok_ref
  49.6 1.6 %fusion.24 = f32[128,256]{1,0:T(8,128)S(1)} fusion(bf16[2048,256]{1,0:T(8,128)(2,1)} %param.15, bf16[128,2048]{1,0:T(8,128)(2,1)S(1)} %all_gather.6, f32[2048]{0:T(1024)S(1)} %copy-done.12, f32[128]{0:T(128)S(1)} %add_rsqrt_fusion.2), kind=kOutput, calls=%fused_computation.71 | convolution fusion | flops 135266304 | bytes 1712640 | tf_op jit(solution)/shard_map/dot_general | solution.py:195
  51.3 1.3 %pad_add_fusion.1.scalars = s32[2]{0:T(128)} fusion(s32[1]{0:T(128)} %bitcast, s32[1]{0:T(128)} %dynamic_slice.3), kind=kLoop, calls=%fused_computation.61 | loop fusion | flops 2 | bytes 16 | tf_op jit(solution)/shard_map/stack | solution.py:225
  54.7 13.3 %all_gather.7 = bf16[512,1,2,128]{3,2,1,0:T(2,128)(2,1)} all-gather(bf16[128,1,2,128]{3,2,1,0:T(2,128)(2,1)S(1)} %pad_maximum_fusion.2), channel_id=1, replica_groups=mesh['sx'=4,'sz'=16,'tp'=8] {'sx'}, dimensions={0}, use_global_device_ids=true | all-gather | bytes 327680 | tf_op jit(solution)/shard_map/all_gather | solution.py:215
  68.1 10.7 %collective-permute-done = bf16[2,128,1,128]{3,1,2,0:T(8,128)(2,1)S(1)} collective-permute-done((bf16[2,128,1,128]{3,1,2,0:T(8,128)(2,1)S(1)}, bf16[2,128,1,128]{3,1,2,0:T(8,128)(2,1)S(1)}, u32[]{:S(2)}, u32[]{:S(2)}) %collective-permute-start) | collective-permute-done | bytes 65568 | tf_op jit(solution)/shard_map/ppermute | solution.py:213
  78.8 0.7 maximum_bitcast_fusion
  79.5 1.1 fusion.26
  80.6 9.3 %shard_map.127 = (f32[1024,128]{1,0:T(8,128)}, f32[1024,1]{1,0:T(8,128)}, f32[1024,1]{1,0:T(8,128)}) custom-call(s32[2]{0:T(128)} %pad_add_fusion.1.scalars, bf16[1024,128]{1,0:T(8,128)(2,1)} %bitcast.74, s32[1024,1]{1,0:T(8,128)} %broadcast_in_dim_reshape.5.qtok_ref, bf16[2048,128]{1,0:T(8,128)(2,1)} %bitcast.69, bf16[2048,128]{1,0:T(8,128)(2,1)} %bitcast.68, ...), custom_call_target="tpu_custom_call" | custom-call | flops 1207959552 | bytes 1966080 | tf_op jit(solution)/shard_map/pallas_call | solution.py:119
  89.9 1.3 %copy.69 = f32[1024,1]{0,1:T(1,128)S(1)} copy(f32[1024,1]{1,0:T(8,128)} %get-tuple-element.9) | data formatting | bytes 8192 | tf_op jit(solution)/shard_map/pallas_call | solution.py:119
  92.5 0.8 pad_maximum_fusion
  93.3 4.4 %all-to-all-start.1 = ((f32[4,260,128]{2,1,0:T(8,128)}), f32[4,260,128]{2,1,0:T(8,128)S(1)}, u32[]{:S(2)}, u32[]{:S(2)}) async-start(f32[4,260,128]{2,1,0:T(8,128)} %pad_maximum_fusion), calls=%async_computation.1 | async-start | bytes 1081344 | tf_op jit(solution)/shard_map/all_to_all | solution.py:239
  98.2 9.4 %all-to-all-done.1 = f32[4,260,128]{2,1,0:T(8,128)S(1)} async-done(((f32[4,260,128]{2,1,0:T(8,128)}), f32[4,260,128]{2,1,0:T(8,128)S(1)}, u32[]{:S(2)}, u32[]{:S(2)}) %all-to-all-start.1) | async-done | bytes 532512 | tf_op jit(solution)/shard_map/all_to_all | solution.py:239
  107.7 0.6 fusion.27
  110.1 14.7 %all_to_all.15 = bf16[128,8,256]{2,0,1:T(8,128)(2,1)S(1)} all-to-all(bf16[128,8,256]{2,0,1:T(8,128)(2,1)S(1)} %bitcast.60), channel_id=1, replica_groups=mesh['sx'=4,'sz'=16,'tp'=8] {'tp'}, dimensions={1} | all-to-all | bytes 1048576 | tf_op jit(solution)/shard_map/all_to_all | solution.py:254
  124.9 0.6 add_convert_fusion
  (73 shorter events, 8.4 us)
Async XLA Ops:
  0.0 109.8 %copy-start = (bf16[256,2048]{1,0:T(8,128)(2,1)S(1)}, bf16[256,2048]{1,0:T(8,128)(2,1)}, u32[]{:S(2)}) copy-start(bf16[256,2048]{1,0:T(8,128)(2,1)} %param.19) | copy-start | bytes 3145732
  0.0 0.7 copy-start.1
  0.8 0.8 copy-start.5
  0.8 0.9 copy-start.6
  3.3 15.3 %copy-start.4 = (bf16[128,256]{1,0:T(8,128)(2,1)S(1)}, bf16[128,256]{1,0:T(8,128)(2,1)}, u32[]{:S(2)}) copy-start(bf16[128,256]{1,0:T(8,128)(2,1)} %param.13) | copy-start | bytes 196612
  3.3 76.2 %all-to-all-start = ((bf16[16,2,128,128]{3,2,1,0:T(8,128)(2,1)}), bf16[16,2,128,128]{3,2,1,0:T(8,128)(2,1)S(1)}, u32[]{:S(2)}, u32[]{:S(2)}) async-start(bf16[16,2,128,128]{3,2,1,0:T(8,128)(2,1)} %gather_fusion.1), calls=%async_computation | async-start | bytes 2097152 | tf_op jit(solution)/shard_map/all_to_all | solution.py:183
  18.6 14.0 %copy-start.9 = (bf16[2048,128]{1,0:T(8,128)(2,1)S(1)}, bf16[2048,128]{1,0:T(8,128)(2,1)}, u32[]{:S(2)}) copy-start(bf16[2048,128]{1,0:T(8,128)(2,1)} %param.16) | copy-start | bytes 1572868
  32.4 0.7 copy-start.12
  33.1 3.6 %copy-start.10 = (bf16[2048,128]{1,0:T(8,128)(2,1)S(1)}, bf16[2048,128]{1,0:T(8,128)(2,1)}, u32[]{:S(2)}) copy-start(bf16[2048,128]{1,0:T(8,128)(2,1)} %param.17) | copy-start | bytes 1572868
  33.7 0.7 copy-start.13
  35.7 0.7 copy-start.7
  37.2 41.6 %collective-permute-start = (bf16[2,128,1,128]{3,1,2,0:T(8,128)(2,1)S(1)}, bf16[2,128,1,128]{3,1,2,0:T(8,128)(2,1)S(1)}, u32[]{:S(2)}, u32[]{:S(2)}) collective-permute-start(bf16[2,128,1,128]{3,1,2,0:T(8,128)(2,1)S(1)} %pad_maximum_fusion.3), channel_id=1, source_target_pairs={{0,64},{8,72},{16,80},{24,88},{32,96},{40,104},{48,112},{56,120},{... | collective-permute-start | bytes 196616 | tf_op jit(solution)/shard_map/ppermute | solution.py:213
  53.4 0.7 copy-start.8
  89.9 1.3 %copy-start.3 = (f32[1024,1]{1,0:T(8,128)S(1)}, f32[1024,1]{1,0:T(8,128)}, u32[]{:S(2)}) copy-start(f32[1024,1]{1,0:T(8,128)} %get-tuple-element.10) | copy-start | bytes 12292
  91.4 1.0 copy-start.2
  93.3 4.4 %copy-start.11 = (bf16[2048,2]{0,1:T(2,128)(2,1)S(1)}, bf16[2048,2]{0,1:T(2,128)(2,1)}, u32[]{:S(2)}) copy-start(bf16[2048,2]{0,1:T(2,128)(2,1)} %param.18) | copy-start | bytes 24580
  93.3 14.3 %all-to-all-start.1 = ((f32[4,260,128]{2,1,0:T(8,128)}), f32[4,260,128]{2,1,0:T(8,128)S(1)}, u32[]{:S(2)}, u32[]{:S(2)}) async-start(f32[4,260,128]{2,1,0:T(8,128)} %pad_maximum_fusion), calls=%async_computation.1 | async-start | bytes 1081344 | tf_op jit(solution)/shard_map/all_to_all | solution.py:239

commit v8 on v7

--- a/solution.py
+++ b/solution.py
@@ -57,6 +57,13 @@
     )
     return (new_max, new_sum, running_acc * rescale[..., None] + update)
 
+
+def split_three(value):
+    high = lax.reduce_precision(value, exponent_bits=8, mantissa_bits=7)
+    rest = value - high
+    middle = lax.reduce_precision(rest, exponent_bits=8, mantissa_bits=7)
+    low = rest - middle
+    return [part.astype(jnp.bfloat16) for part in (high, middle, low)]
 
 def attention_kernel(
     scalars, q_ref, qtok_ref, kc_ref, vc_ref, kn_ref, vn_ref, ktok_ref, acc_ref, top_ref, total_ref
@@ -234,11 +241,20 @@
         key_tok[None, :],
     )
     slot_rows = tok_rows * heads_local
-    stats = jnp.concatenate([top, total], -1).reshape(ring_x, -1, head_dim)
-    packed = jnp.concatenate([acc.reshape(ring_x, slot_rows, head_dim), stats], 1)
-    packed_in = lax.all_to_all(packed, "sx", 0, 0, tiled=True)
+    pieces = [split_three(top), split_three(total)]
+    stats = jnp.concatenate(pieces[0] + pieces[1], -1).reshape(ring_x, -1, head_dim)
+    acc_half = acc.astype(jnp.bfloat16).reshape(ring_x, slot_rows, head_dim)
+    packed_in = lax.all_to_all(jnp.concatenate([acc_half, stats], 1), "sx", 0, 0, tiled=True)
+    packed_in = packed_in.astype(jnp.float32)
     acc_in = packed_in[:, :slot_rows].reshape(ring_x, tok_rows, kv_local, group_size, head_dim)
-    stats_in = packed_in[:, slot_rows:].reshape(ring_x, tok_rows, kv_local, group_size, 2)
+    stats_in = packed_in[:, slot_rows:].reshape(ring_x, tok_rows, kv_local, group_size, 6)
+    stats_in = jnp.stack(
+        [
+            stats_in[..., 0] + stats_in[..., 1] + stats_in[..., 2],
+            stats_in[..., 3] + stats_in[..., 4] + stats_in[..., 5],
+        ],
+        -1,
+    )
     best = jnp.max(stats_in[..., 0], 0)
     factor = jnp.exp(stats_in[..., 0] - best[None])
     total = jnp.sum(stats_in[..., 1] * factor, 0)

time: 126 us -> 131 us (1.040)
  the two profiles are of different devices: /device:TPU:32 before, /device:TPU:1 now
where the time goes in v8:
time: 131 us; the launch traced here: 130 us
  blocking collectives  44.8 us (34%)
  starting transfers between devices  32.7 us (25%)
  local copies, waits for them, and re-layouts  15.5 us (12%)
  waiting for transfers between devices  12 us (9%)
  other arithmetic  11.2 us (9%)
  Pallas kernels  9.32 us (7%)
  matrix products  4.02 us (3%)
    all_to_all x1, blocking collectives, per_device(): arrived = lax.all_to_all(pieces, 'tp', 1, 1, tiled=True)  19.2 us
    all_to_all x1, starting transfers between devices, per_device(): incoming = lax.all_to_all(cache_both[peer_groups], 'sz', 0, 0, tiled=True)  15.9 us
    all_gather x1, blocking collectives, per_device(): gathered = lax.all_gather(hidden_in, 'tp', axis=1, tiled=True)  14.6 us
    ppermute x1, starting transfers between devices, per_device(): lax.ppermute(jnp.stack([keys_new, values_new]), 'sz', partner_pairs)  12.3 us
    all_gather x1, blocking collectives, per_device(): all_queries = lax.all_gather(queries, 'sx', axis=0, tiled=True)  11 us
    pallas_call x1, Pallas kernels, attention(): pl.pallas_call(attention_kernel, out_shape=(jax.ShapeDtypeStruct((rows, w...  9.32 us
    ppermute x1, waiting for transfers between devices, per_device(): lax.ppermute(jnp.stack([keys_new, values_new]), 'sz', partner_pairs)  6.83 us
    all_to_all x1, waiting for transfers between devices, per_device(): lax.all_to_all(jnp.concatenate([acc_half, stats], 1), 'sx', 0, 0, tiled=T...  5.17 us
  transfers between devices with their start and end apart: 3, of which 2 were waited for; matrix products, arithmetic and copies ran while one was open for 8% of the time, Pallas kernels for 0%

profile of v8, /device:TPU:1, one launch (start us, length us, event | category | flops | bytes accessed | tf_op | source)
XLA Modules:
  0.0 130.4 jit_solution(4950956932975768342)
XLA Ops:
  0.0 0.7 copy-done.1
  1.6 1.7 %gather_fusion.1 = bf16[16,2,128,128]{3,2,1,0:T(8,128)(2,1)} fusion(bf16[2,2,128,128]{3,2,0,1:T(8,128)(2,1)S(1)} %pad_maximum_fusion.1, s32[1024]{0:T(1024)S(1)} %pad_clamp_fusion), kind=kCustom, calls=%fused_computation.1 | custom fusion | bytes 2097216 | tf_op jit(solution)/shard_map/gather | solution.py:190
  3.3 15.9 %all-to-all-start = ((bf16[16,2,128,128]{3,2,1,0:T(8,128)(2,1)}), bf16[16,2,128,128]{3,2,1,0:T(8,128)(2,1)S(1)}, u32[]{:S(2)}, u32[]{:S(2)}) async-start(bf16[16,2,128,128]{3,2,1,0:T(8,128)(2,1)} %gather_fusion.1), calls=%async_computation | async-start | bytes 2097152 | tf_op jit(solution)/shard_map/all_to_all | solution.py:190
  19.2 14.6 %all_gather.6 = bf16[128,2048]{1,0:T(8,128)(2,1)S(1)} all-gather(bf16[128,256]{1,0:T(8,128)(2,1)S(1)} %copy-done.4), channel_id=1, replica_groups=mesh['sx'=4,'sz'=16,'tp'=8] {'tp'}, dimensions={1}, use_global_device_ids=true | all-gather | bytes 589824 | tf_op jit(solution)/shard_map/all_gather | solution.py:196
  37.9 1.4 %convolution_convert_fusion.1 = bf16[128,128]{1,0:T(8,128)(2,1)S(1)} fusion(bf16[2048,128]{1,0:T(8,128)(2,1)} %param.17, bf16[128,2048]{1,0:T(8,128)(2,1)S(1)} %all_gather.6, f32[2048]{0:T(1024)S(1)} %copy-done.11, f32[128]{0:T(128)S(1)} %add_rsqrt_fusion.2), kind=kOutput, calls=%fused_computation.5 | convolution fusion | flops 68173824 | bytes 1090048 | tf_op jit(solution)/shard_map/dot_general | solution.py:211
  39.4 12.3 %collective-permute-start = (bf16[2,128,1,128]{3,1,2,0:T(8,128)(2,1)S(1)}, bf16[2,128,1,128]{3,1,2,0:T(8,128)(2,1)S(1)}, u32[]{:S(2)}, u32[]{:S(2)}) collective-permute-start(bf16[2,128,1,128]{3,1,2,0:T(8,128)(2,1)S(1)} %pad_maximum_fusion.3), channel_id=1, source_target_pairs={{0,64},{8,72},{16,80},{24,88},{32,96},{40,104},{48,112},{56,120},{... | collective-permute-start | bytes 196616 | tf_op jit(solution)/shard_map/ppermute | solution.py:220
  51.9 1.0 broadcast_in_dim_reshape.5.qtok_ref
  52.9 1.6 %fusion.29 = f32[128,256]{1,0:T(8,128)S(1)} fusion(bf16[2048,256]{1,0:T(8,128)(2,1)} %param.15, bf16[128,2048]{1,0:T(8,128)(2,1)S(1)} %all_gather.6, f32[2048]{0:T(1024)S(1)} %copy-done.11, f32[128]{0:T(128)S(1)} %add_rsqrt_fusion.2), kind=kOutput, calls=%fused_computation.85 | convolution fusion | flops 135266304 | bytes 1712640 | tf_op jit(solution)/shard_map/dot_general | solution.py:202
  54.5 1.1 pad_add_fusion.1.scalars
  57.9 11.0 %all_gather.7 = bf16[512,1,2,128]{3,2,1,0:T(2,128)(2,1)} all-gather(bf16[128,1,2,128]{3,2,1,0:T(2,128)(2,1)S(1)} %pad_maximum_fusion.2), channel_id=1, replica_groups=mesh['sx'=4,'sz'=16,'tp'=8] {'sx'}, dimensions={0}, use_global_device_ids=true | all-gather | bytes 327680 | tf_op jit(solution)/shard_map/all_gather | solution.py:222
  68.9 6.8 %collective-permute-done = bf16[2,128,1,128]{3,1,2,0:T(8,128)(2,1)S(1)} collective-permute-done((bf16[2,128,1,128]{3,1,2,0:T(8,128)(2,1)S(1)}, bf16[2,128,1,128]{3,1,2,0:T(8,128)(2,1)S(1)}, u32[]{:S(2)}, u32[]{:S(2)}) %collective-permute-start) | collective-permute-done | bytes 65568 | tf_op jit(solution)/shard_map/ppermute | solution.py:220
  76.4 1.1 fusion.32
  77.5 9.3 %shard_map.127 = (f32[1024,128]{1,0:T(8,128)}, f32[1024,1]{1,0:T(8,128)}, f32[1024,1]{1,0:T(8,128)}) custom-call(s32[2]{0:T(128)} %pad_add_fusion.1.scalars, bf16[1024,128]{1,0:T(8,128)(2,1)} %bitcast.77, s32[1024,1]{1,0:T(8,128)} %broadcast_in_dim_reshape.5.qtok_ref, bf16[2048,128]{1,0:T(8,128)(2,1)} %bitcast.72, bf16[2048,128]{1,0:T(8,128)(2,1)} %bitcast.71, ...), custom_call_target="tpu_custom_call" | custom-call | flops 1207959552 | bytes 1966080 | tf_op jit(solution)/shard_map/pallas_call | solution.py:126
  86.9 1.1 convert_element_type.89
  88.2 0.9 copy-done.2
  89.2 1.4 %concatenate.61 = bf16[1024,6]{1,0:T(8,128)(2,1)} concatenate(bf16[1024,1]{1,0:T(8,128)(2,1)S(1)} %get-tuple-element.24, bf16[1024,1]{1,0:T(8,128)(2,1)S(1)} %get-tuple-element.23, bf16[1024,1]{1,0:T(8,128)(2,1)S(1)} %get-tuple-element.22, bf16[1024,1]{1,0:T(8,128)(2,1)S(1)} %get-tuple-element.21, bf16[1024,1]{1,0:T(8,128)(2,1)S(1)} %get-tuple-element.20, ...), dimensions={1} | concatenate | bytes 24576 | tf_op jit(solution)/shard_map/concatenate | solution.py:245
  90.6 1.3 reshape.521
  91.9 0.7 pad_maximum_fusion
  92.6 4.5 %all-to-all-start.1 = ((bf16[4,268,128]{2,1,0:T(8,128)(2,1)}), bf16[4,268,128]{2,1,0:T(8,128)(2,1)S(1)}, u32[]{:S(2)}, u32[]{:S(2)}) async-start(bf16[4,268,128]{2,1,0:T(8,128)(2,1)} %pad_maximum_fusion), calls=%async_computation.1 | async-start | bytes 557056 | tf_op jit(solution)/shard_map/all_to_all | solution.py:247
  97.6 5.2 %all-to-all-done.1 = bf16[4,268,128]{2,1,0:T(8,128)(2,1)S(1)} async-done(((bf16[4,268,128]{2,1,0:T(8,128)(2,1)}), bf16[4,268,128]{2,1,0:T(8,128)(2,1)S(1)}, u32[]{:S(2)}, u32[]{:S(2)}) %all-to-all-start.1) | async-done | bytes 274464 | tf_op jit(solution)/shard_map/all_to_all | solution.py:247
  102.8 0.8 reshape.522
  103.6 3.5 %slice_add_fusion = (f32[4,128,1,2,1]{4,3,1,0,2:T(2,128)}, f32[4,128,1,2,1]{4,3,1,0,2:T(2,128)S(1)}, f32[4,128,1,2,1]{4,3,1,0,2:T(2,128)S(1)}, f32[4,128,1,2,1]{4,3,1,0,2:T(2,128)S(1)}) fusion(f32[4,128,1,2,6]{4,3,1,0,2:T(2,128)S(1)} %reshape.522), kind=kLoop, calls=%fused_computation.25 | loop fusion | flops 2048 | bytes 40960 | tf_op jit(solution)/shard_map/add | solution.py:254
  107.1 1.2 copy.86
  110.5 19.2 %all_to_all.15 = bf16[128,8,256]{2,0,1:T(8,128)(2,1)S(1)} all-to-all(bf16[128,8,256]{2,0,1:T(8,128)(2,1)S(1)} %bitcast.67), channel_id=1, replica_groups=mesh['sx'=4,'sz'=16,'tp'=8] {'tp'}, dimensions={1} | all-to-all | bytes 1048576 | tf_op jit(solution)/shard_map/all_to_all | solution.py:270
  (79 shorter events, 11.1 us)
Async XLA Ops:
  0.0 110.1 %copy-start = (bf16[256,2048]{1,0:T(8,128)(2,1)S(1)}, bf16[256,2048]{1,0:T(8,128)(2,1)}, u32[]{:S(2)}) copy-start(bf16[256,2048]{1,0:T(8,128)(2,1)} %param.19) | copy-start | bytes 3145732
  0.0 0.7 copy-start.1
  0.8 0.8 copy-start.5
  0.8 0.9 copy-start.6
  3.3 15.9 %copy-start.4 = (bf16[128,256]{1,0:T(8,128)(2,1)S(1)}, bf16[128,256]{1,0:T(8,128)(2,1)}, u32[]{:S(2)}) copy-start(bf16[128,256]{1,0:T(8,128)(2,1)} %param.13) | copy-start | bytes 196612
  3.3 73.1 %all-to-all-start = ((bf16[16,2,128,128]{3,2,1,0:T(8,128)(2,1)}), bf16[16,2,128,128]{3,2,1,0:T(8,128)(2,1)S(1)}, u32[]{:S(2)}, u32[]{:S(2)}) async-start(bf16[16,2,128,128]{3,2,1,0:T(8,128)(2,1)} %gather_fusion.1), calls=%async_computation | async-start | bytes 2097152 | tf_op jit(solution)/shard_map/all_to_all | solution.py:190
  19.2 14.8 %copy-start.9 = (bf16[2048,128]{1,0:T(8,128)(2,1)S(1)}, bf16[2048,128]{1,0:T(8,128)(2,1)}, u32[]{:S(2)}) copy-start(bf16[2048,128]{1,0:T(8,128)(2,1)} %param.16) | copy-start | bytes 1572868
  33.8 0.7 copy-start.11
  35.0 0.7 copy-start.12
  36.8 0.7 copy-start.7
  39.4 36.3 %collective-permute-start = (bf16[2,128,1,128]{3,1,2,0:T(8,128)(2,1)S(1)}, bf16[2,128,1,128]{3,1,2,0:T(8,128)(2,1)S(1)}, u32[]{:S(2)}, u32[]{:S(2)}) collective-permute-start(bf16[2,128,1,128]{3,1,2,0:T(8,128)(2,1)S(1)} %pad_maximum_fusion.3), channel_id=1, source_target_pairs={{0,64},{8,72},{16,80},{24,88},{32,96},{40,104},{48,112},{56,120},{... | collective-permute-start | bytes 196616 | tf_op jit(solution)/shard_map/ppermute | solution.py:220
  56.5 0.7 copy-start.8
  86.8 1.2 copy-start.3
  88.0 1.0 copy-start.2
  92.6 4.5 %copy-start.10 = (bf16[2048,2]{0,1:T(2,128)(2,1)S(1)}, bf16[2048,2]{0,1:T(2,128)(2,1)}, u32[]{:S(2)}) copy-start(bf16[2048,2]{0,1:T(2,128)(2,1)} %param.18) | copy-start | bytes 24580
  92.6 10.1 %all-to-all-start.1 = ((bf16[4,268,128]{2,1,0:T(8,128)(2,1)}), bf16[4,268,128]{2,1,0:T(8,128)(2,1)S(1)}, u32[]{:S(2)}, u32[]{:S(2)}) async-start(bf16[4,268,128]{2,1,0:T(8,128)(2,1)} %pad_maximum_fusion), calls=%async_computation.1 | async-start | bytes 557056 | tf_op jit(solution)/shard_map/all_to_all | solution.py:247

commit v9 on v4

--- a/solution.py
+++ b/solution.py
@@ -184,8 +184,12 @@
         tok_rows, kv_local, group_size
     )
 
-    partner_pairs = [(z, (z + req_count) % ring_z) for z in range(ring_z)]
-    partner_kv = lax.ppermute(jnp.stack([keys_new, values_new]), "sz", partner_pairs)
+    hop = req_count // 2
+    ahead = [(z, (z + hop) % ring_z) for z in range(ring_z)]
+    behind = [(z, (z - hop) % ring_z) for z in range(ring_z)]
+    partner_keys = lax.ppermute(lax.ppermute(keys_new, "sz", ahead), "sz", ahead)
+    partner_values = lax.ppermute(lax.ppermute(values_new, "sz", behind), "sz", behind)
+    partner_kv = (partner_keys, partner_values)
     partner_part = x_index * pair + (pair - 1 - parity)
     all_queries = lax.all_gather(queries, "sx", axis=0, tiled=True)
     query_tok = (

time: 126 us -> 143 us (1.13); the launches traced: 123 us -> 142 us
  waiting for transfers between devices: 14.1 us -> 23.7 us
  starting transfers between devices: 32.3 us -> 41 us
    ppermute x1 -> x4, waiting for transfers between devices: 7.54 us -> 17.2 us  [the longest x1 16.8 us: per_device(): lax.ppermute(values_new, 'sz', behind)]
    ppermute x1 -> x4, starting transfers between devices: 12.3 us -> 21.6 us  [the longest x1 9.65 us: per_device(): lax.ppermute(lax.ppermute(keys_new, 'sz', ahead), 'sz', ahead)]
  transfers between devices with their start and end apart: 3 -> 6, of which waited for: 2 -> 3; matrix products, arithmetic and copies ran while one was open for 8% -> 7% of each run, Pallas kernels for 0% -> 0%
where the time goes in v9:
time: 143 us; the launch traced here: 142 us
  blocking collectives  44.9 us (31%)
  starting transfers between devices  41 us (29%)
  waiting for transfers between devices  23.7 us (17%)
  local copies, waits for them, and re-layouts  11.6 us (8%)
  Pallas kernels  8.74 us (6%)
  other arithmetic  8.32 us (6%)
  matrix products  2.98 us (2%)
    all_to_all x1, blocking collectives, per_device(): arrived = lax.all_to_all(pieces, 'tp', 1, 1, tiled=True)  19.9 us
    ppermute x1, waiting for transfers between devices, per_device(): lax.ppermute(values_new, 'sz', behind)  16.8 us
    all_to_all x1, starting transfers between devices, per_device(): incoming = lax.all_to_all(cache_both[peer_groups], 'sz', 0, 0, tiled=True)  15.9 us
    all_gather x1, blocking collectives, per_device(): gathered = lax.all_gather(hidden_in, 'tp', axis=1, tiled=True)  14.6 us
    all_gather x1, blocking collectives, per_device(): all_queries = lax.all_gather(queries, 'sx', axis=0, tiled=True)  10.5 us
    ppermute x1, starting transfers between devices, per_device(): lax.ppermute(lax.ppermute(keys_new, 'sz', ahead), 'sz', ahead)  9.65 us
    pallas_call x1, Pallas kernels, attention(): pl.pallas_call(attention_kernel, out_shape=(jax.ShapeDtypeStruct((rows, w...  8.74 us
    ppermute x1, starting transfers between devices, per_device(): lax.ppermute(values_new, 'sz', behind)  7.46 us
  transfers between devices with their start and end apart: 6, of which 3 were waited for; matrix products, arithmetic and copies ran while one was open for 7% of the time, Pallas kernels for 0%

profile of v9, /device:TPU:1, one launch (start us, length us, event | category | flops | bytes accessed | tf_op | source)
XLA Modules:
  0.0 142.4 jit_solution(18151959238648458359)
XLA Ops:
  0.0 0.7 copy-done.1
  0.8 0.7 gather_fusion
  1.6 1.6 %gather_fusion.1 = bf16[16,2,128,128]{3,2,1,0:T(8,128)(2,1)} fusion(bf16[2,2,128,128]{3,2,0,1:T(8,128)(2,1)S(1)} %pad_maximum_fusion.1, s32[1024]{0:T(1024)S(1)} %pad_clamp_fusion), kind=kCustom, calls=%fused_computation.1 | custom fusion | bytes 2097216 | tf_op jit(solution)/shard_map/gather | solution.py:158
  3.3 15.9 %all-to-all-start = ((bf16[16,2,128,128]{3,2,1,0:T(8,128)(2,1)}), bf16[16,2,128,128]{3,2,1,0:T(8,128)(2,1)S(1)}, u32[]{:S(2)}, u32[]{:S(2)}) async-start(bf16[16,2,128,128]{3,2,1,0:T(8,128)(2,1)} %gather_fusion.1), calls=%async_computation | async-start | bytes 2097152 | tf_op jit(solution)/shard_map/all_to_all | solution.py:158
  19.2 14.6 %all_gather.6 = bf16[128,2048]{1,0:T(8,128)(2,1)S(1)} all-gather(bf16[128,256]{1,0:T(8,128)(2,1)S(1)} %copy-done.4), channel_id=1, replica_groups=mesh['sx'=4,'sz'=16,'tp'=8] {'tp'}, dimensions={1}, use_global_device_ids=true | all-gather | bytes 589824 | tf_op jit(solution)/shard_map/all_gather | solution.py:164
  34.8 7.5 %collective-permute-start.2 = (bf16[128,1,128]{2,0,1:T(8,128)(2,1)S(1)}, bf16[128,1,128]{2,0,1:T(8,128)(2,1)S(1)}, u32[]{:S(2)}, u32[]{:S(2)}) collective-permute-start(bf16[128,1,128]{2,0,1:T(8,128)(2,1)S(1)} %fusion), channel_id=1, source_target_pairs={{0,96},{8,104},{16,112},{24,120},{32,0},{40,8},{48,16},{56,24},{64... | collective-permute-start | bytes 98312 | tf_op jit(solution)/shard_map/ppermute | solution.py:191
  42.9 0.6 copy-done.13
  45.9 1.9 %collective-permute-start = (bf16[128,1,128]{2,0,1:T(8,128)(2,1)S(1)}, bf16[128,1,128]{2,0,1:T(8,128)(2,1)S(1)}, u32[]{:S(2)}, u32[]{:S(2)}) collective-permute-start(bf16[128,1,128]{2,0,1:T(8,128)(2,1)S(1)} %pad_maximum_fusion.3), channel_id=1, source_target_pairs={{0,32},{8,40},{16,48},{24,56},{32,64},{40,72},{48,80},{56,88},{64,... | collective-permute-start | bytes 98312 | tf_op jit(solution)/shard_map/ppermute | solution.py:190
  47.9 1.6 %fusion.25 = f32[128,256]{1,0:T(8,128)S(1)} fusion(bf16[2048,256]{1,0:T(8,128)(2,1)} %param.15, bf16[128,2048]{1,0:T(8,128)(2,1)S(1)} %all_gather.6, f32[2048]{0:T(1024)S(1)} %copy-done.12, f32[128]{0:T(128)S(1)} %add_rsqrt_fusion.2), kind=kOutput, calls=%fused_computation.70 | convolution fusion | flops 135266304 | bytes 1712640 | tf_op jit(solution)/shard_map/dot_general | solution.py:170
  51.8 1.3 pad_add_fusion.1.scalars
  53.1 16.8 %collective-permute-done.2 = bf16[128,1,128]{2,0,1:T(8,128)(2,1)S(1)} collective-permute-done((bf16[128,1,128]{2,0,1:T(8,128)(2,1)S(1)}, bf16[128,1,128]{2,0,1:T(8,128)(2,1)S(1)}, u32[]{:S(2)}, u32[]{:S(2)}) %collective-permute-start.2) | collective-permute-done | bytes 32800 | tf_op jit(solution)/shard_map/ppermute | solution.py:191
  69.9 2.5 %collective-permute-start.3 = (bf16[128,1,128]{2,0,1:T(8,128)(2,1)S(1)}, bf16[128,1,128]{2,0,1:T(8,128)(2,1)S(1)}, u32[]{:S(2)}, u32[]{:S(2)}) collective-permute-start(bf16[128,1,128]{2,0,1:T(8,128)(2,1)S(1)} %collective-permute-done.2), channel_id=1, source_target_pairs={{0,96},{8,104},{16,112},{24,120},{32,0},{40,8},{48,16},{56,24},{64... | collective-permute-start | bytes 98312 | tf_op jit(solution)/shard_map/ppermute | solution.py:191
  72.5 10.5 %all_gather.7 = bf16[512,1,2,128]{3,2,1,0:T(2,128)(2,1)} all-gather(bf16[128,1,2,128]{3,2,1,0:T(2,128)(2,1)S(1)} %pad_maximum_fusion.2), channel_id=1, replica_groups=mesh['sx'=4,'sz'=16,'tp'=8] {'sx'}, dimensions={0}, use_global_device_ids=true | all-gather | bytes 327680 | tf_op jit(solution)/shard_map/all_gather | solution.py:194
  83.1 1.0 broadcast_in_dim_reshape.5.qtok_ref
  84.1 9.7 %collective-permute-start.1 = (bf16[128,1,128]{2,0,1:T(8,128)(2,1)S(1)}, bf16[128,1,128]{2,0,1:T(8,128)(2,1)S(1)}, u32[]{:S(2)}, u32[]{:S(2)}) collective-permute-start(bf16[128,1,128]{2,0,1:T(8,128)(2,1)S(1)} %collective-permute-done), channel_id=1, source_target_pairs={{0,32},{8,40},{16,48},{24,56},{32,64},{40,72},{48,80},{56,88},{64,... | collective-permute-start | bytes 98312 | tf_op jit(solution)/shard_map/ppermute | solution.py:190
  94.7 0.7 maximum_bitcast_fusion.kn_ref
  95.4 1.1 fusion.27
  96.5 8.7 %shard_map.127 = (f32[1024,128]{1,0:T(8,128)}, f32[1024,1]{1,0:T(8,128)}, f32[1024,1]{1,0:T(8,128)}) custom-call(s32[2]{0:T(128)} %pad_add_fusion.1.scalars, bf16[1024,128]{1,0:T(8,128)(2,1)} %bitcast.66, s32[1024,1]{1,0:T(8,128)} %broadcast_in_dim_reshape.5.qtok_ref, bf16[2048,128]{1,0:T(8,128)(2,1)} %bitcast.63, bf16[2048,128]{1,0:T(8,128)(2,1)} %bitcast.62, ...), custom_call_target="tpu_custom_call" | custom-call | flops 1207959552 | bytes 1966080 | tf_op jit(solution)/shard_map/pallas_call | solution.py:94
  105.3 1.3 copy.71
  107.8 0.8 pad_maximum_fusion
  108.6 3.6 %all-to-all-start.1 = ((f32[4,260,128]{2,1,0:T(8,128)}), f32[4,260,128]{2,1,0:T(8,128)S(1)}, u32[]{:S(2)}, u32[]{:S(2)}) async-start(f32[4,260,128]{2,1,0:T(8,128)} %pad_maximum_fusion), calls=%async_computation.1 | async-start | bytes 1081344 | tf_op jit(solution)/shard_map/all_to_all | solution.py:218
  112.7 6.5 %all-to-all-done.1 = f32[4,260,128]{2,1,0:T(8,128)S(1)} async-done(((f32[4,260,128]{2,1,0:T(8,128)}), f32[4,260,128]{2,1,0:T(8,128)S(1)}, u32[]{:S(2)}, u32[]{:S(2)}) %all-to-all-start.1) | async-done | bytes 532512 | tf_op jit(solution)/shard_map/all_to_all | solution.py:218
  121.8 19.9 %all_to_all.15 = bf16[128,8,256]{2,0,1:T(8,128)(2,1)S(1)} all-to-all(bf16[128,8,256]{2,0,1:T(8,128)(2,1)S(1)} %bitcast.54), channel_id=1, replica_groups=mesh['sx'=4,'sz'=16,'tp'=8] {'tp'}, dimensions={1} | all-to-all | bytes 1048576 | tf_op jit(solution)/shard_map/all_to_all | solution.py:233
  141.8 0.6 add_convert_fusion
  (79 shorter events, 11.3 us)
Async XLA Ops:
  0.0 121.5 %copy-start = (bf16[256,2048]{1,0:T(8,128)(2,1)S(1)}, bf16[256,2048]{1,0:T(8,128)(2,1)}, u32[]{:S(2)}) copy-start(bf16[256,2048]{1,0:T(8,128)(2,1)} %param.19) | copy-start | bytes 3145732
  0.0 0.7 copy-start.1
  0.8 0.8 copy-start.5
  0.8 0.9 copy-start.6
  3.3 15.9 %copy-start.4 = (bf16[128,256]{1,0:T(8,128)(2,1)S(1)}, bf16[128,256]{1,0:T(8,128)(2,1)}, u32[]{:S(2)}) copy-start(bf16[128,256]{1,0:T(8,128)(2,1)} %param.13) | copy-start | bytes 196612
  3.3 92.1 %all-to-all-start = ((bf16[16,2,128,128]{3,2,1,0:T(8,128)(2,1)}), bf16[16,2,128,128]{3,2,1,0:T(8,128)(2,1)S(1)}, u32[]{:S(2)}, u32[]{:S(2)}) async-start(bf16[16,2,128,128]{3,2,1,0:T(8,128)(2,1)} %gather_fusion.1), calls=%async_computation | async-start | bytes 2097152 | tf_op jit(solution)/shard_map/all_to_all | solution.py:158
  19.2 14.8 %copy-start.9 = (bf16[2048,128]{1,0:T(8,128)(2,1)S(1)}, bf16[2048,128]{1,0:T(8,128)(2,1)}, u32[]{:S(2)}) copy-start(bf16[2048,128]{1,0:T(8,128)(2,1)} %param.17) | copy-start | bytes 1572868
  33.7 0.7 copy-start.12
  34.4 7.9 %copy-start.10 = (bf16[2048,128]{1,0:T(8,128)(2,1)S(1)}, bf16[2048,128]{1,0:T(8,128)(2,1)}, u32[]{:S(2)}) copy-start(bf16[2048,128]{1,0:T(8,128)(2,1)} %param.16) | copy-start | bytes 1572868
  34.8 35.1 %collective-permute-start.2 = (bf16[128,1,128]{2,0,1:T(8,128)(2,1)S(1)}, bf16[128,1,128]{2,0,1:T(8,128)(2,1)S(1)}, u32[]{:S(2)}, u32[]{:S(2)}) collective-permute-start(bf16[128,1,128]{2,0,1:T(8,128)(2,1)S(1)} %fusion), channel_id=1, source_target_pairs={{0,96},{8,104},{16,112},{24,120},{32,0},{40,8},{48,16},{56,24},{64... | collective-permute-start | bytes 98312 | tf_op jit(solution)/shard_map/ppermute | solution.py:191
  42.9 0.7 copy-start.13
  44.8 0.7 copy-start.7
  45.9 38.1 %collective-permute-start = (bf16[128,1,128]{2,0,1:T(8,128)(2,1)S(1)}, bf16[128,1,128]{2,0,1:T(8,128)(2,1)S(1)}, u32[]{:S(2)}, u32[]{:S(2)}) collective-permute-start(bf16[128,1,128]{2,0,1:T(8,128)(2,1)S(1)} %pad_maximum_fusion.3), channel_id=1, source_target_pairs={{0,32},{8,40},{16,48},{24,56},{32,64},{40,72},{48,80},{56,88},{64,... | collective-permute-start | bytes 98312 | tf_op jit(solution)/shard_map/ppermute | solution.py:190
  50.4 0.7 copy-start.8
  69.9 23.8 %collective-permute-start.3 = (bf16[128,1,128]{2,0,1:T(8,128)(2,1)S(1)}, bf16[128,1,128]{2,0,1:T(8,128)(2,1)S(1)}, u32[]{:S(2)}, u32[]{:S(2)}) collective-permute-start(bf16[128,1,128]{2,0,1:T(8,128)(2,1)S(1)} %collective-permute-done.2), channel_id=1, source_target_pairs={{0,96},{8,104},{16,112},{24,120},{32,0},{40,8},{48,16},{56,24},{64... | collective-permute-start | bytes 98312 | tf_op jit(solution)/shard_map/ppermute | solution.py:191
  84.1 10.7 %collective-permute-start.1 = (bf16[128,1,128]{2,0,1:T(8,128)(2,1)S(1)}, bf16[128,1,128]{2,0,1:T(8,128)(2,1)S(1)}, u32[]{:S(2)}, u32[]{:S(2)}) collective-permute-start(bf16[128,1,128]{2,0,1:T(8,128)(2,1)S(1)} %collective-permute-done), channel_id=1, source_target_pairs={{0,32},{8,40},{16,48},{24,56},{32,64},{40,72},{48,80},{56,88},{64,... | collective-permute-start | bytes 98312 | tf_op jit(solution)/shard_map/ppermute | solution.py:190
  105.3 1.3 copy-start.3
  106.8 1.0 copy-start.2
  108.6 3.6 %copy-start.11 = (bf16[2048,2]{0,1:T(2,128)(2,1)S(1)}, bf16[2048,2]{0,1:T(2,128)(2,1)}, u32[]{:S(2)}) copy-start(bf16[2048,2]{0,1:T(2,128)(2,1)} %param.18) | copy-start | bytes 24580
  108.6 10.6 %all-to-all-start.1 = ((f32[4,260,128]{2,1,0:T(8,128)}), f32[4,260,128]{2,1,0:T(8,128)S(1)}, u32[]{:S(2)}, u32[]{:S(2)}) async-start(f32[4,260,128]{2,1,0:T(8,128)} %pad_maximum_fusion), calls=%async_computation.1 | async-start | bytes 1081344 | tf_op jit(solution)/shard_map/all_to_all | solution.py:218

commit v10 on v4

--- a/solution.py
+++ b/solution.py
@@ -74,13 +74,16 @@
     top = jnp.maximum(
         jnp.max(cache_scores, 1, keepdims=True), jnp.max(new_scores, 1, keepdims=True)
     )
-    cache_expo = jnp.where(cache_seen, jnp.exp(cache_scores - top), 0.0)
-    new_expo = jnp.where(new_seen, jnp.exp(new_scores - top), 0.0)
-    total_ref[...] = jnp.sum(cache_expo, 1, keepdims=True) + jnp.sum(new_expo, 1, keepdims=True)
+    zero = jnp.zeros((), jnp.bfloat16)
+    cache_expo = jnp.where(cache_seen, jnp.exp((cache_scores - top).astype(jnp.bfloat16)), zero)
+    new_expo = jnp.where(new_seen, jnp.exp((new_scores - top).astype(jnp.bfloat16)), zero)
+    total_ref[...] = jnp.sum(cache_expo.astype(jnp.float32), 1, keepdims=True) + jnp.sum(
+        new_expo.astype(jnp.float32), 1, keepdims=True
+    )
     top_ref[...] = top
-    acc_ref[...] = jnp.dot(
-        cache_expo.astype(jnp.bfloat16), vc_ref[...], preferred_element_type=jnp.float32
-    ) + jnp.dot(new_expo.astype(jnp.bfloat16), vn_ref[...], preferred_element_type=jnp.float32)
+    acc_ref[...] = jnp.dot(cache_expo, vc_ref[...], preferred_element_type=jnp.float32) + jnp.dot(
+        new_expo, vn_ref[...], preferred_element_type=jnp.float32
+    )
 
 
 def attention(scalars, q_rows, q_tok, keys_cache, values_cache, keys_new, values_new, key_tok):

time: 126 us -> 126 us (level)
  transfers between devices with their start and end apart: 3 -> 3, of which waited for: 2 -> 2; matrix products, arithmetic and copies ran while one was open for 8% -> 7% of each run, Pallas kernels for 0% -> 0%
where the time goes in v10:
time: 126 us; the launch traced here: 124 us
  blocking collectives  44.8 us (36%)
  starting transfers between devices  32.3 us (26%)
  waiting for transfers between devices  14.1 us (11%)
  local copies, waits for them, and re-layouts  11.7 us (9%)
  Pallas kernels  9.02 us (7%)
  other arithmetic  7.67 us (6%)
  matrix products  2.98 us (2%)
    all_to_all x1, blocking collectives, per_device(): arrived = lax.all_to_all(pieces, 'tp', 1, 1, tiled=True)  19.2 us
    all_to_all x1, starting transfers between devices, per_device(): incoming = lax.all_to_all(cache_both[peer_groups], 'sz', 0, 0, tiled=True)  15.9 us
    all_gather x1, blocking collectives, per_device(): gathered = lax.all_gather(hidden_in, 'tp', axis=1, tiled=True)  14.6 us
    ppermute x1, starting transfers between devices, per_device(): lax.ppermute(jnp.stack([keys_new, values_new]), 'sz', partner_pairs)  12.3 us
    all_gather x1, blocking collectives, per_device(): all_queries = lax.all_gather(queries, 'sx', axis=0, tiled=True)  11 us
    pallas_call x1, Pallas kernels, attention(): pl.pallas_call(attention_kernel, out_shape=(jax.ShapeDtypeStruct((rows, w...  9.02 us
    ppermute x1, waiting for transfers between devices, per_device(): lax.ppermute(jnp.stack([keys_new, values_new]), 'sz', partner_pairs)  7.54 us
    all_to_all x1, waiting for transfers between devices, per_device(): packed_in = lax.all_to_all(packed, 'sx', 0, 0, tiled=True)  6.57 us
  transfers between devices with their start and end apart: 3, of which 2 were waited for; matrix products, arithmetic and copies ran while one was open for 7% of the time, Pallas kernels for 0%

profile of v10, /device:TPU:1, one launch (start us, length us, event | category | flops | bytes accessed | tf_op | source)
XLA Modules:
  0.0 123.6 jit_solution(3286005662960512923)
XLA Ops:
  0.0 0.7 copy-done.1
  0.8 0.7 gather_fusion
  1.6 1.6 %gather_fusion.1 = bf16[16,2,128,128]{3,2,1,0:T(8,128)(2,1)} fusion(bf16[2,2,128,128]{3,2,0,1:T(8,128)(2,1)S(1)} %pad_maximum_fusion.1, s32[1024]{0:T(1024)S(1)} %pad_clamp_fusion), kind=kCustom, calls=%fused_computation.1 | custom fusion | bytes 2097216 | tf_op jit(solution)/shard_map/gather | solution.py:161
  3.3 15.9 %all-to-all-start = ((bf16[16,2,128,128]{3,2,1,0:T(8,128)(2,1)}), bf16[16,2,128,128]{3,2,1,0:T(8,128)(2,1)S(1)}, u32[]{:S(2)}, u32[]{:S(2)}) async-start(bf16[16,2,128,128]{3,2,1,0:T(8,128)(2,1)} %gather_fusion.1), calls=%async_computation | async-start | bytes 2097152 | tf_op jit(solution)/shard_map/all_to_all | solution.py:161
  19.2 14.6 %all_gather.6 = bf16[128,2048]{1,0:T(8,128)(2,1)S(1)} all-gather(bf16[128,256]{1,0:T(8,128)(2,1)S(1)} %copy-done.4), channel_id=1, replica_groups=mesh['sx'=4,'sz'=16,'tp'=8] {'tp'}, dimensions={1}, use_global_device_ids=true | all-gather | bytes 589824 | tf_op jit(solution)/shard_map/all_gather | solution.py:167
  35.0 0.6 copy-done.13
  35.7 0.6 dynamic_slice.3
  37.0 0.6 copy-done.7
  38.6 12.3 %collective-permute-start = (bf16[2,128,1,128]{3,1,2,0:T(8,128)(2,1)S(1)}, bf16[2,128,1,128]{3,1,2,0:T(8,128)(2,1)S(1)}, u32[]{:S(2)}, u32[]{:S(2)}) collective-permute-start(bf16[2,128,1,128]{3,1,2,0:T(8,128)(2,1)S(1)} %pad_maximum_fusion.3), channel_id=1, source_target_pairs={{0,64},{8,72},{16,80},{24,88},{32,96},{40,104},{48,112},{56,120},{... | collective-permute-start | bytes 196616 | tf_op jit(solution)/shard_map/ppermute | solution.py:191
  51.1 1.0 broadcast_in_dim_reshape.5.qtok_ref
  52.0 1.6 %fusion.24 = f32[128,256]{1,0:T(8,128)S(1)} fusion(bf16[2048,256]{1,0:T(8,128)(2,1)} %param.15, bf16[128,2048]{1,0:T(8,128)(2,1)S(1)} %all_gather.6, f32[2048]{0:T(1024)S(1)} %copy-done.12, f32[128]{0:T(128)S(1)} %add_rsqrt_fusion.2), kind=kOutput, calls=%fused_computation.71 | convolution fusion | flops 135266304 | bytes 1712640 | tf_op jit(solution)/shard_map/dot_general | solution.py:173
  53.7 1.3 %pad_add_fusion.1.scalars = s32[2]{0:T(128)} fusion(s32[1]{0:T(128)} %bitcast, s32[1]{0:T(128)} %dynamic_slice.3), kind=kLoop, calls=%fused_computation.61 | loop fusion | flops 2 | bytes 16 | tf_op jit(solution)/shard_map/stack | solution.py:203
  57.1 11.0 %all_gather.7 = bf16[512,1,2,128]{3,2,1,0:T(2,128)(2,1)} all-gather(bf16[128,1,2,128]{3,2,1,0:T(2,128)(2,1)S(1)} %pad_maximum_fusion.2), channel_id=1, replica_groups=mesh['sx'=4,'sz'=16,'tp'=8] {'sx'}, dimensions={0}, use_global_device_ids=true | all-gather | bytes 327680 | tf_op jit(solution)/shard_map/all_gather | solution.py:193
  68.2 7.5 %collective-permute-done = bf16[2,128,1,128]{3,1,2,0:T(8,128)(2,1)S(1)} collective-permute-done((bf16[2,128,1,128]{3,1,2,0:T(8,128)(2,1)S(1)}, bf16[2,128,1,128]{3,1,2,0:T(8,128)(2,1)S(1)}, u32[]{:S(2)}, u32[]{:S(2)}) %collective-permute-start) | collective-permute-done | bytes 65568 | tf_op jit(solution)/shard_map/ppermute | solution.py:191
  75.7 0.7 maximum_bitcast_fusion
  76.4 1.1 fusion.26
  77.5 9.0 %shard_map.127 = (f32[1024,128]{1,0:T(8,128)}, f32[1024,1]{1,0:T(8,128)}, f32[1024,1]{1,0:T(8,128)}) custom-call(s32[2]{0:T(128)} %pad_add_fusion.1.scalars, bf16[1024,128]{1,0:T(8,128)(2,1)} %bitcast.74, s32[1024,1]{1,0:T(8,128)} %broadcast_in_dim_reshape.5.qtok_ref, bf16[2048,128]{1,0:T(8,128)(2,1)} %bitcast.69, bf16[2048,128]{1,0:T(8,128)(2,1)} %bitcast.68, ...), custom_call_target="tpu_custom_call" | custom-call | flops 1207959552 | bytes 1966080 | tf_op jit(solution)/shard_map/pallas_call | solution.py:97
  86.5 1.3 %copy.69 = f32[1024,1]{0,1:T(1,128)S(1)} copy(f32[1024,1]{1,0:T(8,128)} %get-tuple-element.9) | data formatting | bytes 8192 | tf_op jit(solution)/shard_map/pallas_call | solution.py:97
  89.1 0.8 pad_maximum_fusion
  89.9 4.2 %all-to-all-start.1 = ((f32[4,260,128]{2,1,0:T(8,128)}), f32[4,260,128]{2,1,0:T(8,128)S(1)}, u32[]{:S(2)}, u32[]{:S(2)}) async-start(f32[4,260,128]{2,1,0:T(8,128)} %pad_maximum_fusion), calls=%async_computation.1 | async-start | bytes 1081344 | tf_op jit(solution)/shard_map/all_to_all | solution.py:217
  94.5 6.6 %all-to-all-done.1 = f32[4,260,128]{2,1,0:T(8,128)S(1)} async-done(((f32[4,260,128]{2,1,0:T(8,128)}), f32[4,260,128]{2,1,0:T(8,128)S(1)}, u32[]{:S(2)}, u32[]{:S(2)}) %all-to-all-start.1) | async-done | bytes 532512 | tf_op jit(solution)/shard_map/all_to_all | solution.py:217
  101.3 0.6 fusion.27
  103.7 19.2 %all_to_all.15 = bf16[128,8,256]{2,0,1:T(8,128)(2,1)S(1)} all-to-all(bf16[128,8,256]{2,0,1:T(8,128)(2,1)S(1)} %bitcast.60), channel_id=1, replica_groups=mesh['sx'=4,'sz'=16,'tp'=8] {'tp'}, dimensions={1} | all-to-all | bytes 1048576 | tf_op jit(solution)/shard_map/all_to_all | solution.py:232
  123.0 0.6 add_convert_fusion
  (73 shorter events, 8.4 us)
Async XLA Ops:
  0.0 103.3 %copy-start = (bf16[256,2048]{1,0:T(8,128)(2,1)S(1)}, bf16[256,2048]{1,0:T(8,128)(2,1)}, u32[]{:S(2)}) copy-start(bf16[256,2048]{1,0:T(8,128)(2,1)} %param.19) | copy-start | bytes 3145732
  0.0 0.7 copy-start.1
  0.8 0.8 copy-start.5
  0.8 0.9 copy-start.6
  3.3 15.9 %copy-start.4 = (bf16[128,256]{1,0:T(8,128)(2,1)S(1)}, bf16[128,256]{1,0:T(8,128)(2,1)}, u32[]{:S(2)}) copy-start(bf16[128,256]{1,0:T(8,128)(2,1)} %param.13) | copy-start | bytes 196612
  3.3 73.1 %all-to-all-start = ((bf16[16,2,128,128]{3,2,1,0:T(8,128)(2,1)}), bf16[16,2,128,128]{3,2,1,0:T(8,128)(2,1)S(1)}, u32[]{:S(2)}, u32[]{:S(2)}) async-start(bf16[16,2,128,128]{3,2,1,0:T(8,128)(2,1)} %gather_fusion.1), calls=%async_computation | async-start | bytes 2097152 | tf_op jit(solution)/shard_map/all_to_all | solution.py:161
  19.2 14.8 %copy-start.9 = (bf16[2048,128]{1,0:T(8,128)(2,1)S(1)}, bf16[2048,128]{1,0:T(8,128)(2,1)}, u32[]{:S(2)}) copy-start(bf16[2048,128]{1,0:T(8,128)(2,1)} %param.16) | copy-start | bytes 1572868
  33.8 0.7 copy-start.12
  34.5 3.6 %copy-start.10 = (bf16[2048,128]{1,0:T(8,128)(2,1)S(1)}, bf16[2048,128]{1,0:T(8,128)(2,1)}, u32[]{:S(2)}) copy-start(bf16[2048,128]{1,0:T(8,128)(2,1)} %param.17) | copy-start | bytes 1572868
  35.0 0.7 copy-start.13
  37.0 0.7 copy-start.7
  38.6 37.1 %collective-permute-start = (bf16[2,128,1,128]{3,1,2,0:T(8,128)(2,1)S(1)}, bf16[2,128,1,128]{3,1,2,0:T(8,128)(2,1)S(1)}, u32[]{:S(2)}, u32[]{:S(2)}) collective-permute-start(bf16[2,128,1,128]{3,1,2,0:T(8,128)(2,1)S(1)} %pad_maximum_fusion.3), channel_id=1, source_target_pairs={{0,64},{8,72},{16,80},{24,88},{32,96},{40,104},{48,112},{56,120},{... | collective-permute-start | bytes 196616 | tf_op jit(solution)/shard_map/ppermute | solution.py:191
  55.8 0.7 copy-start.8
  86.5 1.3 %copy-start.3 = (f32[1024,1]{1,0:T(8,128)S(1)}, f32[1024,1]{1,0:T(8,128)}, u32[]{:S(2)}) copy-start(f32[1024,1]{1,0:T(8,128)} %get-tuple-element.10) | copy-start | bytes 12292
  88.1 1.0 copy-start.2
  89.9 4.2 %copy-start.11 = (bf16[2048,2]{0,1:T(2,128)(2,1)S(1)}, bf16[2048,2]{0,1:T(2,128)(2,1)}, u32[]{:S(2)}) copy-start(bf16[2048,2]{0,1:T(2,128)(2,1)} %param.18) | copy-start | bytes 24580
  89.9 11.2 %all-to-all-start.1 = ((f32[4,260,128]{2,1,0:T(8,128)}), f32[4,260,128]{2,1,0:T(8,128)S(1)}, u32[]{:S(2)}, u32[]{:S(2)}) async-start(f32[4,260,128]{2,1,0:T(8,128)} %pad_maximum_fusion), calls=%async_computation.1 | async-start | bytes 1081344 | tf_op jit(solution)/shard_map/all_to_all | solution.py:217

commit v11 on v4

--- a/solution.py
+++ b/solution.py
@@ -64,11 +64,11 @@
     scale = q_ref.shape[-1] ** (-0.5)
     dims = (((1,), (1,)), ((), ()))
     q = q_ref[...]
-    cache_scores = lax.dot_general(q, kc_ref[...], dims, preferred_element_type=jnp.float32) * scale
-    cache_pos = scalars[1] + lax.broadcasted_iota(jnp.int32, (1, kc_ref.shape[0]), 1)
+    cache_scores = jnp.dot(q, kc_ref[...], preferred_element_type=jnp.float32) * scale
+    cache_pos = scalars[1] + lax.broadcasted_iota(jnp.int32, (1, kc_ref.shape[1]), 1)
     cache_seen = cache_pos < scalars[0]
     cache_scores = jnp.where(cache_seen, cache_scores, masked_score)
-    new_scores = lax.dot_general(q, kn_ref[...], dims, preferred_element_type=jnp.float32) * scale
+    new_scores = jnp.dot(q, kn_ref[...], preferred_element_type=jnp.float32) * scale
     new_seen = ktok_ref[...] <= qtok_ref[...]
     new_scores = jnp.where(new_seen, new_scores, masked_score)
     top = jnp.maximum(
@@ -85,8 +85,8 @@
 
 def attention(scalars, q_rows, q_tok, keys_cache, values_cache, keys_new, values_new, key_tok):
     rows, width = q_rows.shape
-    cache_rows = keys_cache.shape[0]
-    new_rows = keys_new.shape[0]
+    cache_rows = keys_cache.shape[1]
+    new_rows = keys_new.shape[1]
     block = 256
     full = lambda shape: pl.BlockSpec(shape, lambda i, s: (0, 0))
     row_block = lambda cols: pl.BlockSpec((block, cols), lambda i, s: (i, 0))
@@ -104,9 +104,9 @@
             in_specs=[
                 row_block(width),
                 row_block(1),
+                full((width, cache_rows)),
                 full((cache_rows, width)),
-                full((cache_rows, width)),
-                full((new_rows, width)),
+                full((width, new_rows)),
                 full((new_rows, width)),
                 full((1, new_rows)),
             ],
@@ -202,9 +202,9 @@
         scalars,
         all_queries.reshape(-1, head_dim),
         jnp.repeat(query_tok, heads_local)[:, None],
-        keys_cache.reshape(cache_rows, head_dim),
+        keys_cache.reshape(cache_rows, head_dim).T,
         values_cache.reshape(cache_rows, head_dim),
-        keys_two,
+        keys_two.T,
         values_two,
         key_tok[None, :],
     )

time: 126 us -> 127 us (level)
  local copies, waits for them, and re-layouts: 11.7 us -> 13.2 us
where the time goes in v11:
time: 127 us; the launch traced here: 125 us
  blocking collectives  44.8 us (35%)
  starting transfers between devices  32.3 us (25%)
  waiting for transfers between devices  14.2 us (11%)
  local copies, waits for them, and re-layouts  13.2 us (10%)
  Pallas kernels  8.72 us (7%)
  other arithmetic  7.67 us (6%)
  matrix products  2.97 us (2%)
    all_to_all x1, blocking collectives, per_device(): arrived = lax.all_to_all(pieces, 'tp', 1, 1, tiled=True)  19.2 us
    all_to_all x1, starting transfers between devices, per_device(): incoming = lax.all_to_all(cache_both[peer_groups], 'sz', 0, 0, tiled=True)  15.9 us
    all_gather x1, blocking collectives, per_device(): gathered = lax.all_gather(hidden_in, 'tp', axis=1, tiled=True)  14.6 us
    ppermute x1, starting transfers between devices, per_device(): lax.ppermute(jnp.stack([keys_new, values_new]), 'sz', partner_pairs)  12.3 us
    all_gather x1, blocking collectives, per_device(): all_queries = lax.all_gather(queries, 'sx', axis=0, tiled=True)  11 us
    pallas_call x1, Pallas kernels, attention(): pl.pallas_call(attention_kernel, out_shape=(jax.ShapeDtypeStruct((rows, w...  8.72 us
    ppermute x1, waiting for transfers between devices, per_device(): lax.ppermute(jnp.stack([keys_new, values_new]), 'sz', partner_pairs)  7.61 us
    all_to_all x1, waiting for transfers between devices, per_device(): packed_in = lax.all_to_all(packed, 'sx', 0, 0, tiled=True)  6.57 us
  transfers between devices with their start and end apart: 3, of which 2 were waited for; matrix products, arithmetic and copies ran while one was open for 8% of the time, Pallas kernels for 0%

profile of v11, /device:TPU:1, one launch (start us, length us, event | category | flops | bytes accessed | tf_op | source)
XLA Modules:
  0.0 124.9 jit_solution(2661364013551251580)
XLA Ops:
  0.0 0.7 copy-done.1
  0.8 0.7 gather_fusion
  1.6 1.6 %gather_fusion.1 = bf16[16,2,128,128]{3,2,1,0:T(8,128)(2,1)} fusion(bf16[2,2,128,128]{3,2,0,1:T(8,128)(2,1)S(1)} %pad_maximum_fusion.1, s32[1024]{0:T(1024)S(1)} %pad_clamp_fusion), kind=kCustom, calls=%fused_computation.1 | custom fusion | bytes 2097216 | tf_op jit(solution)/shard_map/gather | solution.py:158
  3.3 15.9 %all-to-all-start = ((bf16[16,2,128,128]{3,2,1,0:T(8,128)(2,1)}), bf16[16,2,128,128]{3,2,1,0:T(8,128)(2,1)S(1)}, u32[]{:S(2)}, u32[]{:S(2)}) async-start(bf16[16,2,128,128]{3,2,1,0:T(8,128)(2,1)} %gather_fusion.1), calls=%async_computation | async-start | bytes 2097152 | tf_op jit(solution)/shard_map/all_to_all | solution.py:158
  19.2 14.6 %all_gather.6 = bf16[128,2048]{1,0:T(8,128)(2,1)S(1)} all-gather(bf16[128,256]{1,0:T(8,128)(2,1)S(1)} %copy-done.4), channel_id=1, replica_groups=mesh['sx'=4,'sz'=16,'tp'=8] {'tp'}, dimensions={1}, use_global_device_ids=true | all-gather | bytes 589824 | tf_op jit(solution)/shard_map/all_gather | solution.py:164
  35.0 0.6 copy-done.13
  37.0 0.6 copy-done.7
  38.5 12.3 %collective-permute-start = (bf16[2,128,1,128]{3,1,2,0:T(8,128)(2,1)S(1)}, bf16[2,128,1,128]{3,1,2,0:T(8,128)(2,1)S(1)}, u32[]{:S(2)}, u32[]{:S(2)}) collective-permute-start(bf16[2,128,1,128]{3,1,2,0:T(8,128)(2,1)S(1)} %pad_maximum_fusion.3), channel_id=1, source_target_pairs={{0,64},{8,72},{16,80},{24,88},{32,96},{40,104},{48,112},{56,120},{... | collective-permute-start | bytes 196616 | tf_op jit(solution)/shard_map/ppermute | solution.py:188
  51.0 1.0 broadcast_in_dim_reshape.5.qtok_ref
  52.0 1.6 %fusion.24 = f32[128,256]{1,0:T(8,128)S(1)} fusion(bf16[2048,256]{1,0:T(8,128)(2,1)} %param.15, bf16[128,2048]{1,0:T(8,128)(2,1)S(1)} %all_gather.6, f32[2048]{0:T(1024)S(1)} %copy-done.12, f32[128]{0:T(128)S(1)} %add_rsqrt_fusion.2), kind=kOutput, calls=%fused_computation.71 | convolution fusion | flops 135266304 | bytes 1712640 | tf_op jit(solution)/shard_map/dot_general | solution.py:170
  53.6 1.3 %pad_add_fusion.1.scalars = s32[2]{0:T(128)} fusion(s32[1]{0:T(128)} %bitcast, s32[1]{0:T(128)} %dynamic_slice.3), kind=kLoop, calls=%fused_computation.61 | loop fusion | flops 2 | bytes 16 | tf_op jit(solution)/shard_map/stack | solution.py:200
  57.1 11.0 %all_gather.7 = bf16[512,1,2,128]{3,2,1,0:T(2,128)(2,1)} all-gather(bf16[128,1,2,128]{3,2,1,0:T(2,128)(2,1)S(1)} %pad_maximum_fusion.2), channel_id=1, replica_groups=mesh['sx'=4,'sz'=16,'tp'=8] {'sx'}, dimensions={0}, use_global_device_ids=true | all-gather | bytes 327680 | tf_op jit(solution)/shard_map/all_gather | solution.py:190
  68.1 7.6 %collective-permute-done = bf16[2,128,1,128]{3,1,2,0:T(8,128)(2,1)S(1)} collective-permute-done((bf16[2,128,1,128]{3,1,2,0:T(8,128)(2,1)S(1)}, bf16[2,128,1,128]{3,1,2,0:T(8,128)(2,1)S(1)}, u32[]{:S(2)}, u32[]{:S(2)}) %collective-permute-start) | collective-permute-done | bytes 65568 | tf_op jit(solution)/shard_map/ppermute | solution.py:188
  75.8 0.7 copy.80.kn_ref
  76.5 0.6 maximum_bitcast_fusion.1.vn_ref
  77.2 0.9 fusion.26
  78.1 1.0 copy.90
  79.1 8.7 %shard_map.127 = (f32[1024,128]{1,0:T(8,128)}, f32[1024,1]{1,0:T(8,128)}, f32[1024,1]{1,0:T(8,128)}) custom-call(s32[2]{0:T(128)} %pad_add_fusion.1.scalars, bf16[1024,128]{1,0:T(8,128)(2,1)} %bitcast.78, s32[1024,1]{1,0:T(8,128)} %broadcast_in_dim_reshape.5.qtok_ref, bf16[128,2048]{1,0:T(8,128)(2,1)} %bitcast.69, bf16[2048,128]{1,0:T(8,128)(2,1)} %bitcast.73, ...), custom_call_target="tpu_custom_call" | custom-call | flops 1207959552 | bytes 1966080 | tf_op jit(solution)/shard_map/pallas_call | solution.py:94
  87.8 1.3 %copy.81 = f32[1024,1]{0,1:T(1,128)S(1)} copy(f32[1024,1]{1,0:T(8,128)} %get-tuple-element.9) | data formatting | bytes 8192 | tf_op jit(solution)/shard_map/pallas_call | solution.py:94
  90.3 0.8 pad_maximum_fusion
  91.2 4.1 %all-to-all-start.1 = ((f32[4,260,128]{2,1,0:T(8,128)}), f32[4,260,128]{2,1,0:T(8,128)S(1)}, u32[]{:S(2)}, u32[]{:S(2)}) async-start(f32[4,260,128]{2,1,0:T(8,128)} %pad_maximum_fusion), calls=%async_computation.1 | async-start | bytes 1081344 | tf_op jit(solution)/shard_map/all_to_all | solution.py:214
  95.8 6.6 %all-to-all-done.1 = f32[4,260,128]{2,1,0:T(8,128)S(1)} async-done(((f32[4,260,128]{2,1,0:T(8,128)}), f32[4,260,128]{2,1,0:T(8,128)S(1)}, u32[]{:S(2)}, u32[]{:S(2)}) %all-to-all-start.1) | async-done | bytes 532512 | tf_op jit(solution)/shard_map/all_to_all | solution.py:214
  104.9 19.2 %all_to_all.15 = bf16[128,8,256]{2,0,1:T(8,128)(2,1)S(1)} all-to-all(bf16[128,8,256]{2,0,1:T(8,128)(2,1)S(1)} %bitcast.63), channel_id=1, replica_groups=mesh['sx'=4,'sz'=16,'tp'=8] {'tp'}, dimensions={1} | all-to-all | bytes 1048576 | tf_op jit(solution)/shard_map/all_to_all | solution.py:229
  124.2 0.6 add_convert_fusion
  (76 shorter events, 9.7 us)
Async XLA Ops:
  0.0 104.6 %copy-start = (bf16[256,2048]{1,0:T(8,128)(2,1)S(1)}, bf16[256,2048]{1,0:T(8,128)(2,1)}, u32[]{:S(2)}) copy-start(bf16[256,2048]{1,0:T(8,128)(2,1)} %param.19) | copy-start | bytes 3145732
  0.0 0.7 copy-start.1
  0.8 0.8 copy-start.5
  0.8 0.9 copy-start.6
  3.3 15.9 %copy-start.4 = (bf16[128,256]{1,0:T(8,128)(2,1)S(1)}, bf16[128,256]{1,0:T(8,128)(2,1)}, u32[]{:S(2)}) copy-start(bf16[128,256]{1,0:T(8,128)(2,1)} %param.13) | copy-start | bytes 196612
  3.3 73.9 %all-to-all-start = ((bf16[16,2,128,128]{3,2,1,0:T(8,128)(2,1)}), bf16[16,2,128,128]{3,2,1,0:T(8,128)(2,1)S(1)}, u32[]{:S(2)}, u32[]{:S(2)}) async-start(bf16[16,2,128,128]{3,2,1,0:T(8,128)(2,1)} %gather_fusion.1), calls=%async_computation | async-start | bytes 2097152 | tf_op jit(solution)/shard_map/all_to_all | solution.py:158
  19.2 14.8 %copy-start.9 = (bf16[2048,128]{1,0:T(8,128)(2,1)S(1)}, bf16[2048,128]{1,0:T(8,128)(2,1)}, u32[]{:S(2)}) copy-start(bf16[2048,128]{1,0:T(8,128)(2,1)} %param.16) | copy-start | bytes 1572868
  33.8 0.7 copy-start.12
  34.5 3.6 %copy-start.10 = (bf16[2048,128]{1,0:T(8,128)(2,1)S(1)}, bf16[2048,128]{1,0:T(8,128)(2,1)}, u32[]{:S(2)}) copy-start(bf16[2048,128]{1,0:T(8,128)(2,1)} %param.17) | copy-start | bytes 1572868
  35.0 0.7 copy-start.13
  36.9 0.7 copy-start.7
  38.5 37.2 %collective-permute-start = (bf16[2,128,1,128]{3,1,2,0:T(8,128)(2,1)S(1)}, bf16[2,128,1,128]{3,1,2,0:T(8,128)(2,1)S(1)}, u32[]{:S(2)}, u32[]{:S(2)}) collective-permute-start(bf16[2,128,1,128]{3,1,2,0:T(8,128)(2,1)S(1)} %pad_maximum_fusion.3), channel_id=1, source_target_pairs={{0,64},{8,72},{16,80},{24,88},{32,96},{40,104},{48,112},{56,120},{... | collective-permute-start | bytes 196616 | tf_op jit(solution)/shard_map/ppermute | solution.py:188
  55.7 0.7 copy-start.8
  87.8 1.3 %copy-start.3 = (f32[1024,1]{1,0:T(8,128)S(1)}, f32[1024,1]{1,0:T(8,128)}, u32[]{:S(2)}) copy-start(f32[1024,1]{1,0:T(8,128)} %get-tuple-element.10) | copy-start | bytes 12292
  89.3 1.0 copy-start.2
  91.2 4.2 %copy-start.11 = (bf16[2048,2]{0,1:T(2,128)(2,1)S(1)}, bf16[2048,2]{0,1:T(2,128)(2,1)}, u32[]{:S(2)}) copy-start(bf16[2048,2]{0,1:T(2,128)(2,1)} %param.18) | copy-start | bytes 24580
  91.2 11.2 %all-to-all-start.1 = ((f32[4,260,128]{2,1,0:T(8,128)}), f32[4,260,128]{2,1,0:T(8,128)S(1)}, u32[]{:S(2)}, u32[]{:S(2)}) async-start(f32[4,260,128]{2,1,0:T(8,128)} %pad_maximum_fusion), calls=%async_computation.1 | async-start | bytes 1081344 | tf_op jit(solution)/shard_map/all_to_all | solution.py:214

commit v12 on v4

--- a/solution.py
+++ b/solution.py
@@ -87,7 +87,7 @@
     rows, width = q_rows.shape
     cache_rows = keys_cache.shape[0]
     new_rows = keys_new.shape[0]
-    block = 256
+    block = 512
     full = lambda shape: pl.BlockSpec(shape, lambda i, s: (0, 0))
     row_block = lambda cols: pl.BlockSpec((block, cols), lambda i, s: (i, 0))
     flops = 4 * rows * (cache_rows + new_rows) * width

time: 126 us -> 127 us (level)
  transfers between devices with their start and end apart: 3 -> 3, of which waited for: 2 -> 2; matrix products, arithmetic and copies ran while one was open for 8% -> 7% of each run, Pallas kernels for 0% -> 0%
where the time goes in v12:
time: 127 us; the launch traced here: 125 us
  blocking collectives  44.8 us (35%)
  starting transfers between devices  32.3 us (25%)
  waiting for transfers between devices  14.1 us (11%)
  local copies, waits for them, and re-layouts  11.7 us (9%)
  Pallas kernels  10 us (8%)
  other arithmetic  7.67 us (6%)
  matrix products  2.98 us (2%)
    all_to_all x1, blocking collectives, per_device(): arrived = lax.all_to_all(pieces, 'tp', 1, 1, tiled=True)  19.2 us
    all_to_all x1, starting transfers between devices, per_device(): incoming = lax.all_to_all(cache_both[peer_groups], 'sz', 0, 0, tiled=True)  15.9 us
    all_gather x1, blocking collectives, per_device(): gathered = lax.all_gather(hidden_in, 'tp', axis=1, tiled=True)  14.6 us
    ppermute x1, starting transfers between devices, per_device(): lax.ppermute(jnp.stack([keys_new, values_new]), 'sz', partner_pairs)  12.3 us
    all_gather x1, blocking collectives, per_device(): all_queries = lax.all_gather(queries, 'sx', axis=0, tiled=True)  11 us
    pallas_call x1, Pallas kernels, attention(): pl.pallas_call(attention_kernel, out_shape=(jax.ShapeDtypeStruct((rows, w...  10 us
    ppermute x1, waiting for transfers between devices, per_device(): lax.ppermute(jnp.stack([keys_new, values_new]), 'sz', partner_pairs)  7.54 us
    all_to_all x1, waiting for transfers between devices, per_device(): packed_in = lax.all_to_all(packed, 'sx', 0, 0, tiled=True)  6.57 us
  transfers between devices with their start and end apart: 3, of which 2 were waited for; matrix products, arithmetic and copies ran while one was open for 7% of the time, Pallas kernels for 0%

profile of v12, /device:TPU:1, one launch (start us, length us, event | category | flops | bytes accessed | tf_op | source)
XLA Modules:
  0.0 124.6 jit_solution(1467315786248675877)
XLA Ops:
  0.0 0.7 copy-done.1
  0.8 0.7 gather_fusion
  1.6 1.6 %gather_fusion.1 = bf16[16,2,128,128]{3,2,1,0:T(8,128)(2,1)} fusion(bf16[2,2,128,128]{3,2,0,1:T(8,128)(2,1)S(1)} %pad_maximum_fusion.1, s32[1024]{0:T(1024)S(1)} %pad_clamp_fusion), kind=kCustom, calls=%fused_computation.1 | custom fusion | bytes 2097216 | tf_op jit(solution)/shard_map/gather | solution.py:158
  3.3 15.9 %all-to-all-start = ((bf16[16,2,128,128]{3,2,1,0:T(8,128)(2,1)}), bf16[16,2,128,128]{3,2,1,0:T(8,128)(2,1)S(1)}, u32[]{:S(2)}, u32[]{:S(2)}) async-start(bf16[16,2,128,128]{3,2,1,0:T(8,128)(2,1)} %gather_fusion.1), calls=%async_computation | async-start | bytes 2097152 | tf_op jit(solution)/shard_map/all_to_all | solution.py:158
  19.2 14.6 %all_gather.6 = bf16[128,2048]{1,0:T(8,128)(2,1)S(1)} all-gather(bf16[128,256]{1,0:T(8,128)(2,1)S(1)} %copy-done.4), channel_id=1, replica_groups=mesh['sx'=4,'sz'=16,'tp'=8] {'tp'}, dimensions={1}, use_global_device_ids=true | all-gather | bytes 589824 | tf_op jit(solution)/shard_map/all_gather | solution.py:164
  35.0 0.6 copy-done.13
  35.7 0.6 dynamic_slice.3
  37.0 0.6 copy-done.7
  38.6 12.3 %collective-permute-start = (bf16[2,128,1,128]{3,1,2,0:T(8,128)(2,1)S(1)}, bf16[2,128,1,128]{3,1,2,0:T(8,128)(2,1)S(1)}, u32[]{:S(2)}, u32[]{:S(2)}) collective-permute-start(bf16[2,128,1,128]{3,1,2,0:T(8,128)(2,1)S(1)} %pad_maximum_fusion.3), channel_id=1, source_target_pairs={{0,64},{8,72},{16,80},{24,88},{32,96},{40,104},{48,112},{56,120},{... | collective-permute-start | bytes 196616 | tf_op jit(solution)/shard_map/ppermute | solution.py:188
  51.1 1.0 broadcast_in_dim_reshape.5.qtok_ref
  52.0 1.6 %fusion.24 = f32[128,256]{1,0:T(8,128)S(1)} fusion(bf16[2048,256]{1,0:T(8,128)(2,1)} %param.15, bf16[128,2048]{1,0:T(8,128)(2,1)S(1)} %all_gather.6, f32[2048]{0:T(1024)S(1)} %copy-done.12, f32[128]{0:T(128)S(1)} %add_rsqrt_fusion.2), kind=kOutput, calls=%fused_computation.71 | convolution fusion | flops 135266304 | bytes 1712640 | tf_op jit(solution)/shard_map/dot_general | solution.py:170
  53.7 1.3 %pad_add_fusion.1.scalars = s32[2]{0:T(128)} fusion(s32[1]{0:T(128)} %bitcast, s32[1]{0:T(128)} %dynamic_slice.3), kind=kLoop, calls=%fused_computation.61 | loop fusion | flops 2 | bytes 16 | tf_op jit(solution)/shard_map/stack | solution.py:200
  57.1 11.0 %all_gather.7 = bf16[512,1,2,128]{3,2,1,0:T(2,128)(2,1)} all-gather(bf16[128,1,2,128]{3,2,1,0:T(2,128)(2,1)S(1)} %pad_maximum_fusion.2), channel_id=1, replica_groups=mesh['sx'=4,'sz'=16,'tp'=8] {'sx'}, dimensions={0}, use_global_device_ids=true | all-gather | bytes 327680 | tf_op jit(solution)/shard_map/all_gather | solution.py:190
  68.2 7.5 %collective-permute-done = bf16[2,128,1,128]{3,1,2,0:T(8,128)(2,1)S(1)} collective-permute-done((bf16[2,128,1,128]{3,1,2,0:T(8,128)(2,1)S(1)}, bf16[2,128,1,128]{3,1,2,0:T(8,128)(2,1)S(1)}, u32[]{:S(2)}, u32[]{:S(2)}) %collective-permute-start) | collective-permute-done | bytes 65568 | tf_op jit(solution)/shard_map/ppermute | solution.py:188
  75.7 0.7 maximum_bitcast_fusion
  76.4 1.1 fusion.26
  77.5 10.0 %shard_map.127 = (f32[1024,128]{1,0:T(8,128)}, f32[1024,1]{1,0:T(8,128)}, f32[1024,1]{1,0:T(8,128)}) custom-call(s32[2]{0:T(128)} %pad_add_fusion.1.scalars, bf16[1024,128]{1,0:T(8,128)(2,1)} %bitcast.74, s32[1024,1]{1,0:T(8,128)} %broadcast_in_dim_reshape.5.qtok_ref, bf16[2048,128]{1,0:T(8,128)(2,1)} %bitcast.69, bf16[2048,128]{1,0:T(8,128)(2,1)} %bitcast.68, ...), custom_call_target="tpu_custom_call" | custom-call | flops 1207959552 | bytes 1966080 | tf_op jit(solution)/shard_map/pallas_call | solution.py:94
  87.5 1.3 %copy.69 = f32[1024,1]{0,1:T(1,128)S(1)} copy(f32[1024,1]{1,0:T(8,128)} %get-tuple-element.9) | data formatting | bytes 8192 | tf_op jit(solution)/shard_map/pallas_call | solution.py:94
  90.1 0.8 pad_maximum_fusion
  90.9 4.1 %all-to-all-start.1 = ((f32[4,260,128]{2,1,0:T(8,128)}), f32[4,260,128]{2,1,0:T(8,128)S(1)}, u32[]{:S(2)}, u32[]{:S(2)}) async-start(f32[4,260,128]{2,1,0:T(8,128)} %pad_maximum_fusion), calls=%async_computation.1 | async-start | bytes 1081344 | tf_op jit(solution)/shard_map/all_to_all | solution.py:214
  95.5 6.6 %all-to-all-done.1 = f32[4,260,128]{2,1,0:T(8,128)S(1)} async-done(((f32[4,260,128]{2,1,0:T(8,128)}), f32[4,260,128]{2,1,0:T(8,128)S(1)}, u32[]{:S(2)}, u32[]{:S(2)}) %all-to-all-start.1) | async-done | bytes 532512 | tf_op jit(solution)/shard_map/all_to_all | solution.py:214
  102.2 0.6 fusion.27
  104.7 19.2 %all_to_all.15 = bf16[128,8,256]{2,0,1:T(8,128)(2,1)S(1)} all-to-all(bf16[128,8,256]{2,0,1:T(8,128)(2,1)S(1)} %bitcast.60), channel_id=1, replica_groups=mesh['sx'=4,'sz'=16,'tp'=8] {'tp'}, dimensions={1} | all-to-all | bytes 1048576 | tf_op jit(solution)/shard_map/all_to_all | solution.py:229
  124.0 0.6 add_convert_fusion
  (73 shorter events, 8.4 us)
Async XLA Ops:
  0.0 104.3 %copy-start = (bf16[256,2048]{1,0:T(8,128)(2,1)S(1)}, bf16[256,2048]{1,0:T(8,128)(2,1)}, u32[]{:S(2)}) copy-start(bf16[256,2048]{1,0:T(8,128)(2,1)} %param.19) | copy-start | bytes 3145732
  0.0 0.7 copy-start.1
  0.8 0.8 copy-start.5
  0.8 0.9 copy-start.6
  3.3 15.9 %copy-start.4 = (bf16[128,256]{1,0:T(8,128)(2,1)S(1)}, bf16[128,256]{1,0:T(8,128)(2,1)}, u32[]{:S(2)}) copy-start(bf16[128,256]{1,0:T(8,128)(2,1)} %param.13) | copy-start | bytes 196612
  3.3 73.1 %all-to-all-start = ((bf16[16,2,128,128]{3,2,1,0:T(8,128)(2,1)}), bf16[16,2,128,128]{3,2,1,0:T(8,128)(2,1)S(1)}, u32[]{:S(2)}, u32[]{:S(2)}) async-start(bf16[16,2,128,128]{3,2,1,0:T(8,128)(2,1)} %gather_fusion.1), calls=%async_computation | async-start | bytes 2097152 | tf_op jit(solution)/shard_map/all_to_all | solution.py:158
  19.2 14.8 %copy-start.9 = (bf16[2048,128]{1,0:T(8,128)(2,1)S(1)}, bf16[2048,128]{1,0:T(8,128)(2,1)}, u32[]{:S(2)}) copy-start(bf16[2048,128]{1,0:T(8,128)(2,1)} %param.16) | copy-start | bytes 1572868
  33.8 0.7 copy-start.12
  34.5 3.6 %copy-start.10 = (bf16[2048,128]{1,0:T(8,128)(2,1)S(1)}, bf16[2048,128]{1,0:T(8,128)(2,1)}, u32[]{:S(2)}) copy-start(bf16[2048,128]{1,0:T(8,128)(2,1)} %param.17) | copy-start | bytes 1572868
  35.0 0.7 copy-start.13
  37.0 0.7 copy-start.7
  38.6 37.1 %collective-permute-start = (bf16[2,128,1,128]{3,1,2,0:T(8,128)(2,1)S(1)}, bf16[2,128,1,128]{3,1,2,0:T(8,128)(2,1)S(1)}, u32[]{:S(2)}, u32[]{:S(2)}) collective-permute-start(bf16[2,128,1,128]{3,1,2,0:T(8,128)(2,1)S(1)} %pad_maximum_fusion.3), channel_id=1, source_target_pairs={{0,64},{8,72},{16,80},{24,88},{32,96},{40,104},{48,112},{56,120},{... | collective-permute-start | bytes 196616 | tf_op jit(solution)/shard_map/ppermute | solution.py:188
  55.8 0.7 copy-start.8
  87.5 1.3 %copy-start.3 = (f32[1024,1]{1,0:T(8,128)S(1)}, f32[1024,1]{1,0:T(8,128)}, u32[]{:S(2)}) copy-start(f32[1024,1]{1,0:T(8,128)} %get-tuple-element.10) | copy-start | bytes 12292
  89.0 1.0 copy-start.2
  90.9 4.1 %copy-start.11 = (bf16[2048,2]{0,1:T(2,128)(2,1)S(1)}, bf16[2048,2]{0,1:T(2,128)(2,1)}, u32[]{:S(2)}) copy-start(bf16[2048,2]{0,1:T(2,128)(2,1)} %param.18) | copy-start | bytes 24580
  90.9 11.2 %all-to-all-start.1 = ((f32[4,260,128]{2,1,0:T(8,128)}), f32[4,260,128]{2,1,0:T(8,128)S(1)}, u32[]{:S(2)}, u32[]{:S(2)}) async-start(f32[4,260,128]{2,1,0:T(8,128)} %pad_maximum_fusion), calls=%async_computation.1 | async-start | bytes 1081344 | tf_op jit(solution)/shard_map/all_to_all | solution.py:214

commit v13 on v12

--- a/solution.py
+++ b/solution.py
@@ -87,7 +87,7 @@
     rows, width = q_rows.shape
     cache_rows = keys_cache.shape[0]
     new_rows = keys_new.shape[0]
-    block = 512
+    block = 128
     full = lambda shape: pl.BlockSpec(shape, lambda i, s: (0, 0))
     row_block = lambda cols: pl.BlockSpec((block, cols), lambda i, s: (i, 0))
     flops = 4 * rows * (cache_rows + new_rows) * width

time: 127 us -> 127 us (level)
  no operation moved by 1% of the time
where the time goes in v13:
time: 127 us; the launch traced here: 125 us
  blocking collectives  44.8 us (35%)
  starting transfers between devices  32.3 us (25%)
  waiting for transfers between devices  14.1 us (11%)
  local copies, waits for them, and re-layouts  11.7 us (9%)
  Pallas kernels  10.1 us (8%)
  other arithmetic  7.67 us (6%)
  matrix products  2.98 us (2%)
    all_to_all x1, blocking collectives, per_device(): arrived = lax.all_to_all(pieces, 'tp', 1, 1, tiled=True)  19.2 us
    all_to_all x1, starting transfers between devices, per_device(): incoming = lax.all_to_all(cache_both[peer_groups], 'sz', 0, 0, tiled=True)  15.9 us
    all_gather x1, blocking collectives, per_device(): gathered = lax.all_gather(hidden_in, 'tp', axis=1, tiled=True)  14.6 us
    ppermute x1, starting transfers between devices, per_device(): lax.ppermute(jnp.stack([keys_new, values_new]), 'sz', partner_pairs)  12.3 us
    all_gather x1, blocking collectives, per_device(): all_queries = lax.all_gather(queries, 'sx', axis=0, tiled=True)  11 us
    pallas_call x1, Pallas kernels, attention(): pl.pallas_call(attention_kernel, out_shape=(jax.ShapeDtypeStruct((rows, w...  10.1 us
    ppermute x1, waiting for transfers between devices, per_device(): lax.ppermute(jnp.stack([keys_new, values_new]), 'sz', partner_pairs)  7.54 us
    all_to_all x1, waiting for transfers between devices, per_device(): packed_in = lax.all_to_all(packed, 'sx', 0, 0, tiled=True)  6.57 us
  transfers between devices with their start and end apart: 3, of which 2 were waited for; matrix products, arithmetic and copies ran while one was open for 7% of the time, Pallas kernels for 0%

profile of v13, /device:TPU:1, one launch (start us, length us, event | category | flops | bytes accessed | tf_op | source)
XLA Modules:
  0.0 124.7 jit_solution(7673551485129835336)
XLA Ops:
  0.0 0.7 copy-done.1
  0.8 0.7 gather_fusion
  1.6 1.6 %gather_fusion.1 = bf16[16,2,128,128]{3,2,1,0:T(8,128)(2,1)} fusion(bf16[2,2,128,128]{3,2,0,1:T(8,128)(2,1)S(1)} %pad_maximum_fusion.1, s32[1024]{0:T(1024)S(1)} %pad_clamp_fusion), kind=kCustom, calls=%fused_computation.1 | custom fusion | bytes 2097216 | tf_op jit(solution)/shard_map/gather | solution.py:158
  3.3 15.9 %all-to-all-start = ((bf16[16,2,128,128]{3,2,1,0:T(8,128)(2,1)}), bf16[16,2,128,128]{3,2,1,0:T(8,128)(2,1)S(1)}, u32[]{:S(2)}, u32[]{:S(2)}) async-start(bf16[16,2,128,128]{3,2,1,0:T(8,128)(2,1)} %gather_fusion.1), calls=%async_computation | async-start | bytes 2097152 | tf_op jit(solution)/shard_map/all_to_all | solution.py:158
  19.2 14.6 %all_gather.6 = bf16[128,2048]{1,0:T(8,128)(2,1)S(1)} all-gather(bf16[128,256]{1,0:T(8,128)(2,1)S(1)} %copy-done.4), channel_id=1, replica_groups=mesh['sx'=4,'sz'=16,'tp'=8] {'tp'}, dimensions={1}, use_global_device_ids=true | all-gather | bytes 589824 | tf_op jit(solution)/shard_map/all_gather | solution.py:164
  35.0 0.6 copy-done.13
  35.7 0.6 dynamic_slice.3
  37.0 0.6 copy-done.7
  38.6 12.3 %collective-permute-start = (bf16[2,128,1,128]{3,1,2,0:T(8,128)(2,1)S(1)}, bf16[2,128,1,128]{3,1,2,0:T(8,128)(2,1)S(1)}, u32[]{:S(2)}, u32[]{:S(2)}) collective-permute-start(bf16[2,128,1,128]{3,1,2,0:T(8,128)(2,1)S(1)} %pad_maximum_fusion.3), channel_id=1, source_target_pairs={{0,64},{8,72},{16,80},{24,88},{32,96},{40,104},{48,112},{56,120},{... | collective-permute-start | bytes 196616 | tf_op jit(solution)/shard_map/ppermute | solution.py:188
  51.1 1.0 broadcast_in_dim_reshape.5.qtok_ref
  52.0 1.6 %fusion.24 = f32[128,256]{1,0:T(8,128)S(1)} fusion(bf16[2048,256]{1,0:T(8,128)(2,1)} %param.15, bf16[128,2048]{1,0:T(8,128)(2,1)S(1)} %all_gather.6, f32[2048]{0:T(1024)S(1)} %copy-done.12, f32[128]{0:T(128)S(1)} %add_rsqrt_fusion.2), kind=kOutput, calls=%fused_computation.71 | convolution fusion | flops 135266304 | bytes 1712640 | tf_op jit(solution)/shard_map/dot_general | solution.py:170
  53.7 1.3 %pad_add_fusion.1.scalars = s32[2]{0:T(128)} fusion(s32[1]{0:T(128)} %bitcast, s32[1]{0:T(128)} %dynamic_slice.3), kind=kLoop, calls=%fused_computation.61 | loop fusion | flops 2 | bytes 16 | tf_op jit(solution)/shard_map/stack | solution.py:200
  57.1 11.0 %all_gather.7 = bf16[512,1,2,128]{3,2,1,0:T(2,128)(2,1)} all-gather(bf16[128,1,2,128]{3,2,1,0:T(2,128)(2,1)S(1)} %pad_maximum_fusion.2), channel_id=1, replica_groups=mesh['sx'=4,'sz'=16,'tp'=8] {'sx'}, dimensions={0}, use_global_device_ids=true | all-gather | bytes 327680 | tf_op jit(solution)/shard_map/all_gather | solution.py:190
  68.2 7.5 %collective-permute-done = bf16[2,128,1,128]{3,1,2,0:T(8,128)(2,1)S(1)} collective-permute-done((bf16[2,128,1,128]{3,1,2,0:T(8,128)(2,1)S(1)}, bf16[2,128,1,128]{3,1,2,0:T(8,128)(2,1)S(1)}, u32[]{:S(2)}, u32[]{:S(2)}) %collective-permute-start) | collective-permute-done | bytes 65568 | tf_op jit(solution)/shard_map/ppermute | solution.py:188
  75.7 0.7 maximum_bitcast_fusion
  76.4 1.1 fusion.26
  77.5 10.1 %shard_map.127 = (f32[1024,128]{1,0:T(8,128)}, f32[1024,1]{1,0:T(8,128)}, f32[1024,1]{1,0:T(8,128)}) custom-call(s32[2]{0:T(128)} %pad_add_fusion.1.scalars, bf16[1024,128]{1,0:T(8,128)(2,1)} %bitcast.74, s32[1024,1]{1,0:T(8,128)} %broadcast_in_dim_reshape.5.qtok_ref, bf16[2048,128]{1,0:T(8,128)(2,1)} %bitcast.69, bf16[2048,128]{1,0:T(8,128)(2,1)} %bitcast.68, ...), custom_call_target="tpu_custom_call" | custom-call | flops 1207959552 | bytes 1966080 | tf_op jit(solution)/shard_map/pallas_call | solution.py:94
  87.6 1.3 %copy.69 = f32[1024,1]{0,1:T(1,128)S(1)} copy(f32[1024,1]{1,0:T(8,128)} %get-tuple-element.9) | data formatting | bytes 8192 | tf_op jit(solution)/shard_map/pallas_call | solution.py:94
  90.2 0.8 pad_maximum_fusion
  91.0 4.1 %all-to-all-start.1 = ((f32[4,260,128]{2,1,0:T(8,128)}), f32[4,260,128]{2,1,0:T(8,128)S(1)}, u32[]{:S(2)}, u32[]{:S(2)}) async-start(f32[4,260,128]{2,1,0:T(8,128)} %pad_maximum_fusion), calls=%async_computation.1 | async-start | bytes 1081344 | tf_op jit(solution)/shard_map/all_to_all | solution.py:214
  95.6 6.6 %all-to-all-done.1 = f32[4,260,128]{2,1,0:T(8,128)S(1)} async-done(((f32[4,260,128]{2,1,0:T(8,128)}), f32[4,260,128]{2,1,0:T(8,128)S(1)}, u32[]{:S(2)}, u32[]{:S(2)}) %all-to-all-start.1) | async-done | bytes 532512 | tf_op jit(solution)/shard_map/all_to_all | solution.py:214
  102.3 0.6 fusion.27
  104.8 19.2 %all_to_all.15 = bf16[128,8,256]{2,0,1:T(8,128)(2,1)S(1)} all-to-all(bf16[128,8,256]{2,0,1:T(8,128)(2,1)S(1)} %bitcast.60), channel_id=1, replica_groups=mesh['sx'=4,'sz'=16,'tp'=8] {'tp'}, dimensions={1} | all-to-all | bytes 1048576 | tf_op jit(solution)/shard_map/all_to_all | solution.py:229
  124.1 0.6 add_convert_fusion
  (73 shorter events, 8.4 us)
Async XLA Ops:
  0.0 104.4 %copy-start = (bf16[256,2048]{1,0:T(8,128)(2,1)S(1)}, bf16[256,2048]{1,0:T(8,128)(2,1)}, u32[]{:S(2)}) copy-start(bf16[256,2048]{1,0:T(8,128)(2,1)} %param.19) | copy-start | bytes 3145732
  0.0 0.7 copy-start.1
  0.8 0.8 copy-start.5
  0.8 0.9 copy-start.6
  3.3 15.9 %copy-start.4 = (bf16[128,256]{1,0:T(8,128)(2,1)S(1)}, bf16[128,256]{1,0:T(8,128)(2,1)}, u32[]{:S(2)}) copy-start(bf16[128,256]{1,0:T(8,128)(2,1)} %param.13) | copy-start | bytes 196612
  3.3 73.1 %all-to-all-start = ((bf16[16,2,128,128]{3,2,1,0:T(8,128)(2,1)}), bf16[16,2,128,128]{3,2,1,0:T(8,128)(2,1)S(1)}, u32[]{:S(2)}, u32[]{:S(2)}) async-start(bf16[16,2,128,128]{3,2,1,0:T(8,128)(2,1)} %gather_fusion.1), calls=%async_computation | async-start | bytes 2097152 | tf_op jit(solution)/shard_map/all_to_all | solution.py:158
  19.2 14.8 %copy-start.9 = (bf16[2048,128]{1,0:T(8,128)(2,1)S(1)}, bf16[2048,128]{1,0:T(8,128)(2,1)}, u32[]{:S(2)}) copy-start(bf16[2048,128]{1,0:T(8,128)(2,1)} %param.16) | copy-start | bytes 1572868
  33.8 0.7 copy-start.12
  34.5 3.6 %copy-start.10 = (bf16[2048,128]{1,0:T(8,128)(2,1)S(1)}, bf16[2048,128]{1,0:T(8,128)(2,1)}, u32[]{:S(2)}) copy-start(bf16[2048,128]{1,0:T(8,128)(2,1)} %param.17) | copy-start | bytes 1572868
  35.0 0.7 copy-start.13
  37.0 0.7 copy-start.7
  38.6 37.1 %collective-permute-start = (bf16[2,128,1,128]{3,1,2,0:T(8,128)(2,1)S(1)}, bf16[2,128,1,128]{3,1,2,0:T(8,128)(2,1)S(1)}, u32[]{:S(2)}, u32[]{:S(2)}) collective-permute-start(bf16[2,128,1,128]{3,1,2,0:T(8,128)(2,1)S(1)} %pad_maximum_fusion.3), channel_id=1, source_target_pairs={{0,64},{8,72},{16,80},{24,88},{32,96},{40,104},{48,112},{56,120},{... | collective-permute-start | bytes 196616 | tf_op jit(solution)/shard_map/ppermute | solution.py:188
  55.8 0.7 copy-start.8
  87.6 1.3 %copy-start.3 = (f32[1024,1]{1,0:T(8,128)S(1)}, f32[1024,1]{1,0:T(8,128)}, u32[]{:S(2)}) copy-start(f32[1024,1]{1,0:T(8,128)} %get-tuple-element.10) | copy-start | bytes 12292
  89.1 1.0 copy-start.2
  91.0 4.1 %copy-start.11 = (bf16[2048,2]{0,1:T(2,128)(2,1)S(1)}, bf16[2048,2]{0,1:T(2,128)(2,1)}, u32[]{:S(2)}) copy-start(bf16[2048,2]{0,1:T(2,128)(2,1)} %param.18) | copy-start | bytes 24580
  91.0 11.2 %all-to-all-start.1 = ((f32[4,260,128]{2,1,0:T(8,128)}), f32[4,260,128]{2,1,0:T(8,128)S(1)}, u32[]{:S(2)}, u32[]{:S(2)}) async-start(f32[4,260,128]{2,1,0:T(8,128)} %pad_maximum_fusion), calls=%async_computation.1 | async-start | bytes 1081344 | tf_op jit(solution)/shard_map/all_to_all | solution.py:214

commit v14 on v4

--- a/solution.py
+++ b/solution.py
@@ -58,9 +58,7 @@
     return (new_max, new_sum, running_acc * rescale[..., None] + update)
 
 
-def attention_kernel(
-    scalars, q_ref, qtok_ref, kc_ref, vc_ref, kn_ref, vn_ref, ktok_ref, acc_ref, top_ref, total_ref
-):
+def attention_kernel(scalars, q_ref, qtok_ref, kc_ref, vc_ref, kn_ref, vn_ref, ktok_ref, out_ref):
     scale = q_ref.shape[-1] ** (-0.5)
     dims = (((1,), (1,)), ((), ()))
     q = q_ref[...]
@@ -76,11 +74,18 @@
     )
     cache_expo = jnp.where(cache_seen, jnp.exp(cache_scores - top), 0.0)
     new_expo = jnp.where(new_seen, jnp.exp(new_scores - top), 0.0)
-    total_ref[...] = jnp.sum(cache_expo, 1, keepdims=True) + jnp.sum(new_expo, 1, keepdims=True)
-    top_ref[...] = top
-    acc_ref[...] = jnp.dot(
+    total = jnp.sum(cache_expo, 1, keepdims=True) + jnp.sum(new_expo, 1, keepdims=True)
+    acc = jnp.dot(
         cache_expo.astype(jnp.bfloat16), vc_ref[...], preferred_element_type=jnp.float32
     ) + jnp.dot(new_expo.astype(jnp.bfloat16), vn_ref[...], preferred_element_type=jnp.float32)
+    rows, width = acc.shape
+    top_t = jnp.transpose(jnp.broadcast_to(top, (rows, width)))[0:1]
+    total_t = jnp.transpose(jnp.broadcast_to(total, (rows, width)))[0:1]
+    out_ref[0, :rows, :] = acc
+    for half in range(rows // width):
+        cols = slice(half * width, (half + 1) * width)
+        out_ref[0, rows + half : rows + half + 1, :] = top_t[:, cols]
+        out_ref[0, rows + rows // width + half : rows + rows // width + half + 1, :] = total_t[:, cols]
 
 
 def attention(scalars, q_rows, q_tok, keys_cache, values_cache, keys_new, values_new, key_tok):
@@ -88,16 +93,13 @@
     cache_rows = keys_cache.shape[0]
     new_rows = keys_new.shape[0]
     block = 256
+    packed_rows = block + 2 * (block // width)
     full = lambda shape: pl.BlockSpec(shape, lambda i, s: (0, 0))
     row_block = lambda cols: pl.BlockSpec((block, cols), lambda i, s: (i, 0))
     flops = 4 * rows * (cache_rows + new_rows) * width
     return pl.pallas_call(
         attention_kernel,
-        out_shape=(
-            jax.ShapeDtypeStruct((rows, width), jnp.float32),
-            jax.ShapeDtypeStruct((rows, 1), jnp.float32),
-            jax.ShapeDtypeStruct((rows, 1), jnp.float32),
-        ),
+        out_shape=jax.ShapeDtypeStruct((rows // block, packed_rows, width), jnp.float32),
         grid_spec=pltpu.PrefetchScalarGridSpec(
             num_scalar_prefetch=1,
             grid=(rows // block,),
@@ -110,7 +112,7 @@
                 full((new_rows, width)),
                 full((1, new_rows)),
             ],
-            out_specs=[row_block(width), row_block(1), row_block(1)],
+            out_specs=pl.BlockSpec((1, packed_rows, width), lambda i, s: (i, 0, 0)),
         ),
         cost_estimate=pl.CostEstimate(
             flops=flops,
@@ -198,7 +200,7 @@
     values_two = jnp.concatenate([values_new, partner_kv[1]], 0).reshape(-1, head_dim)
     query_count = query_tok.shape[0]
     scalars = jnp.stack([length, x_index * cache_rows]).astype(jnp.int32)
-    acc, top, total = attention(
+    packed = attention(
         scalars,
         all_queries.reshape(-1, head_dim),
         jnp.repeat(query_tok, heads_local)[:, None],
@@ -209,11 +211,10 @@
         key_tok[None, :],
     )
     slot_rows = tok_rows * heads_local
-    stats = jnp.concatenate([top, total], -1).reshape(ring_x, -1, head_dim)
-    packed = jnp.concatenate([acc.reshape(ring_x, slot_rows, head_dim), stats], 1)
     packed_in = lax.all_to_all(packed, "sx", 0, 0, tiled=True)
     acc_in = packed_in[:, :slot_rows].reshape(ring_x, tok_rows, kv_local, group_size, head_dim)
-    stats_in = packed_in[:, slot_rows:].reshape(ring_x, tok_rows, kv_local, group_size, 2)
+    stats_in = packed_in[:, slot_rows:].reshape(ring_x, 2, tok_rows, kv_local, group_size)
+    stats_in = jnp.moveaxis(stats_in, 1, -1)
     best = jnp.max(stats_in[..., 0], 0)
     factor = jnp.exp(stats_in[..., 0] - best[None])
     total = jnp.sum(stats_in[..., 1] * factor, 0)

time: 126 us -> 121 us (0.960)
  local copies, waits for them, and re-layouts: 11.7 us -> 9.15 us
  other arithmetic: 7.67 us -> 6.37 us
    pallas_call x2 -> x0, local copies, waits for them, and re-layouts: 1.47 us -> none  [attention(): pl.pallas_call(attention_kernel, out_shape=(jax.ShapeDtypeStruct((rows, w...]
    unnamed x28 -> x24, local copies, waits for them, and re-layouts: 3.57 us -> 3.05 us
where the time goes in v14:
time: 121 us; the launch traced here: 119 us
  blocking collectives  44.8 us (37%)
  starting transfers between devices  32.3 us (27%)
  waiting for transfers between devices  14 us (12%)
  local copies, waits for them, and re-layouts  9.15 us (8%)
  Pallas kernels  8.58 us (7%)
  other arithmetic  6.37 us (5%)
  matrix products  2.98 us (2%)
    all_to_all x1, blocking collectives, per_device(): arrived = lax.all_to_all(pieces, 'tp', 1, 1, tiled=True)  19.2 us
    all_to_all x1, starting transfers between devices, per_device(): incoming = lax.all_to_all(cache_both[peer_groups], 'sz', 0, 0, tiled=True)  15.9 us
    all_gather x1, blocking collectives, per_device(): gathered = lax.all_gather(hidden_in, 'tp', axis=1, tiled=True)  14.6 us
    ppermute x1, starting transfers between devices, per_device(): lax.ppermute(jnp.stack([keys_new, values_new]), 'sz', partner_pairs)  12.3 us
    all_gather x1, blocking collectives, per_device(): all_queries = lax.all_gather(queries, 'sx', axis=0, tiled=True)  11 us
    pallas_call x1, Pallas kernels, attention(): pl.pallas_call(attention_kernel, out_shape=jax.ShapeDtypeStruct((rows //...  8.58 us
    ppermute x1, waiting for transfers between devices, per_device(): lax.ppermute(jnp.stack([keys_new, values_new]), 'sz', partner_pairs)  7.47 us
    all_to_all x1, waiting for transfers between devices, per_device(): packed_in = lax.all_to_all(packed, 'sx', 0, 0, tiled=True)  6.57 us
  transfers between devices with their start and end apart: 3, of which 2 were waited for; matrix products, arithmetic and copies ran while one was open for 8% of the time, Pallas kernels for 0%

profile of v14, /device:TPU:1, one launch (start us, length us, event | category | flops | bytes accessed | tf_op | source)
XLA Modules:
  0.0 119.3 jit_solution(10101361166572598232)
XLA Ops:
  0.0 0.7 copy-done.1
  0.8 0.7 gather_fusion
  1.6 1.7 %gather_fusion.1 = bf16[16,2,128,128]{3,2,1,0:T(8,128)(2,1)} fusion(bf16[2,2,128,128]{3,2,0,1:T(8,128)(2,1)S(1)} %pad_maximum_fusion, s32[1024]{0:T(1024)S(1)} %pad_clamp_fusion), kind=kCustom, calls=%fused_computation.1 | custom fusion | bytes 2097216 | tf_op jit(solution)/shard_map/gather | solution.py:160
  3.4 15.9 %all-to-all-start = ((bf16[16,2,128,128]{3,2,1,0:T(8,128)(2,1)}), bf16[16,2,128,128]{3,2,1,0:T(8,128)(2,1)S(1)}, u32[]{:S(2)}, u32[]{:S(2)}) async-start(bf16[16,2,128,128]{3,2,1,0:T(8,128)(2,1)} %gather_fusion.1), calls=%async_computation | async-start | bytes 2097152 | tf_op jit(solution)/shard_map/all_to_all | solution.py:160
  19.3 14.6 %all_gather.6 = bf16[128,2048]{1,0:T(8,128)(2,1)S(1)} all-gather(bf16[128,256]{1,0:T(8,128)(2,1)S(1)} %copy-done.2), channel_id=1, replica_groups=mesh['sx'=4,'sz'=16,'tp'=8] {'tp'}, dimensions={1}, use_global_device_ids=true | all-gather | bytes 589824 | tf_op jit(solution)/shard_map/all_gather | solution.py:166
  34.0 0.5 copy-done.10
  34.5 0.4 multiply_reduce_fusion.1
  35.1 0.6 copy-done.11
  35.7 0.6 dynamic_slice.3
  37.1 0.6 copy-done.5
  38.6 12.3 %collective-permute-start = (bf16[2,128,1,128]{3,1,2,0:T(8,128)(2,1)S(1)}, bf16[2,128,1,128]{3,1,2,0:T(8,128)(2,1)S(1)}, u32[]{:S(2)}, u32[]{:S(2)}) collective-permute-start(bf16[2,128,1,128]{3,1,2,0:T(8,128)(2,1)S(1)} %pad_maximum_fusion.2), channel_id=1, source_target_pairs={{0,64},{8,72},{16,80},{24,88},{32,96},{40,104},{48,112},{56,120},{... | collective-permute-start | bytes 196616 | tf_op jit(solution)/shard_map/ppermute | solution.py:190
  51.1 1.0 broadcast_in_dim_reshape.5.qtok_ref
  52.1 1.6 %fusion.27 = f32[128,256]{1,0:T(8,128)S(1)} fusion(bf16[2048,256]{1,0:T(8,128)(2,1)} %param.15, bf16[128,2048]{1,0:T(8,128)(2,1)S(1)} %all_gather.6, f32[2048]{0:T(1024)S(1)} %copy-done.10, f32[128]{0:T(128)S(1)} %add_rsqrt_fusion.2), kind=kOutput, calls=%fused_computation.73 | convolution fusion | flops 135266304 | bytes 1712640 | tf_op jit(solution)/shard_map/dot_general | solution.py:172
  53.7 1.3 %pad_add_fusion.1.scalars = s32[2]{0:T(128)} fusion(s32[1]{0:T(128)} %bitcast, s32[1]{0:T(128)} %dynamic_slice.3), kind=kLoop, calls=%fused_computation.64 | loop fusion | flops 2 | bytes 16 | tf_op jit(solution)/shard_map/stack | solution.py:202
  55.1 0.6 pad_add_fusion
  57.3 11.0 %all_gather.7 = bf16[512,1,2,128]{3,2,1,0:T(2,128)(2,1)} all-gather(bf16[128,1,2,128]{3,2,1,0:T(2,128)(2,1)S(1)} %pad_maximum_fusion.1), channel_id=1, replica_groups=mesh['sx'=4,'sz'=16,'tp'=8] {'sx'}, dimensions={0}, use_global_device_ids=true | all-gather | bytes 327680 | tf_op jit(solution)/shard_map/all_gather | solution.py:192
  68.3 7.5 %collective-permute-done = bf16[2,128,1,128]{3,1,2,0:T(8,128)(2,1)S(1)} collective-permute-done((bf16[2,128,1,128]{3,1,2,0:T(8,128)(2,1)S(1)}, bf16[2,128,1,128]{3,1,2,0:T(8,128)(2,1)S(1)}, u32[]{:S(2)}, u32[]{:S(2)}) %collective-permute-start) | collective-permute-done | bytes 65568 | tf_op jit(solution)/shard_map/ppermute | solution.py:190
  75.8 0.7 maximum_bitcast_fusion
  76.5 1.0 fusion.29
  77.5 8.6 %shard_map.127 = f32[4,260,128]{2,1,0:T(8,128)} custom-call(s32[2]{0:T(128)} %pad_add_fusion.1.scalars, bf16[1024,128]{1,0:T(8,128)(2,1)} %bitcast.83, s32[1024,1]{1,0:T(8,128)} %broadcast_in_dim_reshape.5.qtok_ref, bf16[2048,128]{1,0:T(8,128)(2,1)} %bitcast.78, bf16[2048,128]{1,0:T(8,128)(2,1)} %bitcast.77, bf16[256,128]{1,0:T(8,128)(2,1)} %get-tuple-element.17.kn_ref, ...), custom_call_target="tpu_custom_call" | custom-call | flops 1207959552 | bytes 1966080 | tf_op jit(solution)/shard_map/pallas_call | solution.py:100
  86.1 4.1 %all-to-all-start.1 = ((f32[4,260,128]{2,1,0:T(8,128)}), f32[4,260,128]{2,1,0:T(8,128)S(1)}, u32[]{:S(2)}, u32[]{:S(2)}) async-start(f32[4,260,128]{2,1,0:T(8,128)} %shard_map.127), calls=%async_computation.1 | async-start | bytes 1081344 | tf_op jit(solution)/shard_map/all_to_all | solution.py:214
  90.7 6.6 %all-to-all-done.1 = f32[4,260,128]{2,1,0:T(8,128)S(1)} async-done(((f32[4,260,128]{2,1,0:T(8,128)}), f32[4,260,128]{2,1,0:T(8,128)S(1)}, u32[]{:S(2)}, u32[]{:S(2)}) %all-to-all-start.1) | async-done | bytes 532512 | tf_op jit(solution)/shard_map/all_to_all | solution.py:214
  99.3 19.2 %all_to_all.15 = bf16[128,8,256]{2,0,1:T(8,128)(2,1)S(1)} all-to-all(bf16[128,8,256]{2,0,1:T(8,128)(2,1)S(1)} %bitcast.74), channel_id=1, replica_groups=mesh['sx'=4,'sz'=16,'tp'=8] {'tp'}, dimensions={1} | all-to-all | bytes 1048576 | tf_op jit(solution)/shard_map/all_to_all | solution.py:230
  118.6 0.6 add_convert_fusion
  (63 shorter events, 5.8 us)
Async XLA Ops:
  0.0 99.0 %copy-start = (bf16[256,2048]{1,0:T(8,128)(2,1)S(1)}, bf16[256,2048]{1,0:T(8,128)(2,1)}, u32[]{:S(2)}) copy-start(bf16[256,2048]{1,0:T(8,128)(2,1)} %param.19) | copy-start | bytes 3145732
  0.0 0.7 copy-start.1
  0.8 0.8 copy-start.3
  0.8 0.9 copy-start.4
  3.4 15.9 %copy-start.2 = (bf16[128,256]{1,0:T(8,128)(2,1)S(1)}, bf16[128,256]{1,0:T(8,128)(2,1)}, u32[]{:S(2)}) copy-start(bf16[128,256]{1,0:T(8,128)(2,1)} %param.13) | copy-start | bytes 196612
  3.4 73.1 %all-to-all-start = ((bf16[16,2,128,128]{3,2,1,0:T(8,128)(2,1)}), bf16[16,2,128,128]{3,2,1,0:T(8,128)(2,1)S(1)}, u32[]{:S(2)}, u32[]{:S(2)}) async-start(bf16[16,2,128,128]{3,2,1,0:T(8,128)(2,1)} %gather_fusion.1), calls=%async_computation | async-start | bytes 2097152 | tf_op jit(solution)/shard_map/all_to_all | solution.py:160
  19.2 14.8 %copy-start.7 = (bf16[2048,128]{1,0:T(8,128)(2,1)S(1)}, bf16[2048,128]{1,0:T(8,128)(2,1)}, u32[]{:S(2)}) copy-start(bf16[2048,128]{1,0:T(8,128)(2,1)} %param.16) | copy-start | bytes 1572868
  33.8 0.7 copy-start.10
  34.5 3.6 %copy-start.8 = (bf16[2048,128]{1,0:T(8,128)(2,1)S(1)}, bf16[2048,128]{1,0:T(8,128)(2,1)}, u32[]{:S(2)}) copy-start(bf16[2048,128]{1,0:T(8,128)(2,1)} %param.17) | copy-start | bytes 1572868
  35.1 0.7 copy-start.11
  37.1 0.7 copy-start.5
  38.6 37.2 %collective-permute-start = (bf16[2,128,1,128]{3,1,2,0:T(8,128)(2,1)S(1)}, bf16[2,128,1,128]{3,1,2,0:T(8,128)(2,1)S(1)}, u32[]{:S(2)}, u32[]{:S(2)}) collective-permute-start(bf16[2,128,1,128]{3,1,2,0:T(8,128)(2,1)S(1)} %pad_maximum_fusion.2), channel_id=1, source_target_pairs={{0,64},{8,72},{16,80},{24,88},{32,96},{40,104},{48,112},{56,120},{... | collective-permute-start | bytes 196616 | tf_op jit(solution)/shard_map/ppermute | solution.py:190
  55.9 0.7 copy-start.6
  86.1 4.2 %copy-start.9 = (bf16[2048,2]{0,1:T(2,128)(2,1)S(1)}, bf16[2048,2]{0,1:T(2,128)(2,1)}, u32[]{:S(2)}) copy-start(bf16[2048,2]{0,1:T(2,128)(2,1)} %param.18) | copy-start | bytes 24580
  86.1 11.2 %all-to-all-start.1 = ((f32[4,260,128]{2,1,0:T(8,128)}), f32[4,260,128]{2,1,0:T(8,128)S(1)}, u32[]{:S(2)}, u32[]{:S(2)}) async-start(f32[4,260,128]{2,1,0:T(8,128)} %shard_map.127), calls=%async_computation.1 | async-start | bytes 1081344 | tf_op jit(solution)/shard_map/all_to_all | solution.py:214

commit v15 on v14

--- a/solution.py
+++ b/solution.py
@@ -58,12 +58,15 @@
     return (new_max, new_sum, running_acc * rescale[..., None] + update)
 
 
-def attention_kernel(scalars, q_ref, qtok_ref, kc_ref, vc_ref, kn_ref, vn_ref, ktok_ref, out_ref):
+def attention_kernel(scalars, q_ref, qtok_ref, cache_ref, kn_ref, vn_ref, ktok_ref, out_ref):
     scale = q_ref.shape[-1] ** (-0.5)
     dims = (((1,), (1,)), ((), ()))
     q = q_ref[...]
-    cache_scores = lax.dot_general(q, kc_ref[...], dims, preferred_element_type=jnp.float32) * scale
-    cache_pos = scalars[1] + lax.broadcasted_iota(jnp.int32, (1, kc_ref.shape[0]), 1)
+    sources, _, depth, width = cache_ref.shape
+    keys_cache = cache_ref[:, 0].reshape(sources * depth, width)
+    values_cache = cache_ref[:, 1].reshape(sources * depth, width)
+    cache_scores = lax.dot_general(q, keys_cache, dims, preferred_element_type=jnp.float32) * scale
+    cache_pos = scalars[1] + lax.broadcasted_iota(jnp.int32, (1, sources * depth), 1)
     cache_seen = cache_pos < scalars[0]
     cache_scores = jnp.where(cache_seen, cache_scores, masked_score)
     new_scores = lax.dot_general(q, kn_ref[...], dims, preferred_element_type=jnp.float32) * scale
@@ -76,7 +79,7 @@
     new_expo = jnp.where(new_seen, jnp.exp(new_scores - top), 0.0)
     total = jnp.sum(cache_expo, 1, keepdims=True) + jnp.sum(new_expo, 1, keepdims=True)
     acc = jnp.dot(
-        cache_expo.astype(jnp.bfloat16), vc_ref[...], preferred_element_type=jnp.float32
+        cache_expo.astype(jnp.bfloat16), values_cache, preferred_element_type=jnp.float32
     ) + jnp.dot(new_expo.astype(jnp.bfloat16), vn_ref[...], preferred_element_type=jnp.float32)
     rows, width = acc.shape
     top_t = jnp.transpose(jnp.broadcast_to(top, (rows, width)))[0:1]
@@ -88,9 +91,9 @@
         out_ref[0, rows + rows // width + half : rows + rows // width + half + 1, :] = total_t[:, cols]
 
 
-def attention(scalars, q_rows, q_tok, keys_cache, values_cache, keys_new, values_new, key_tok):
+def attention(scalars, q_rows, q_tok, cache_both, keys_new, values_new, key_tok):
     rows, width = q_rows.shape
-    cache_rows = keys_cache.shape[0]
+    cache_rows = cache_both.shape[0] * cache_both.shape[2]
     new_rows = keys_new.shape[0]
     block = 256
     packed_rows = block + 2 * (block // width)
@@ -106,8 +109,7 @@
             in_specs=[
                 row_block(width),
                 row_block(1),
-                full((cache_rows, width)),
-                full((cache_rows, width)),
+                pl.BlockSpec(cache_both.shape, lambda i, s: (0, 0, 0, 0)),
                 full((new_rows, width)),
                 full((new_rows, width)),
                 full((1, new_rows)),
@@ -119,7 +121,7 @@
             transcendentals=rows * (cache_rows + new_rows),
             bytes_accessed=2 * (rows + 2 * cache_rows + 2 * new_rows) * width + 4 * rows * width,
         ),
-    )(scalars, q_rows, q_tok, keys_cache, values_cache, keys_new, values_new, key_tok)
+    )(scalars, q_rows, q_tok, cache_both, keys_new, values_new, key_tok)
 
 
 def per_device(
@@ -204,8 +206,7 @@
         scalars,
         all_queries.reshape(-1, head_dim),
         jnp.repeat(query_tok, heads_local)[:, None],
-        keys_cache.reshape(cache_rows, head_dim),
-        values_cache.reshape(cache_rows, head_dim),
+        incoming,
         keys_two,
         values_two,
         key_tok[None, :],

time: 121 us -> 121 us (level)
    unnamed x24 -> x26, local copies, waits for them, and re-layouts: 3.05 us -> 4.02 us
where the time goes in v15:
time: 121 us; the launch traced here: 119 us
  blocking collectives  44.8 us (37%)
  starting transfers between devices  32.3 us (27%)
  waiting for transfers between devices  14.4 us (12%)
  local copies, waits for them, and re-layouts  8.95 us (7%)
  Pallas kernels  8.61 us (7%)
  other arithmetic  6.18 us (5%)
  matrix products  2.98 us (2%)
    all_to_all x1, blocking collectives, per_device(): arrived = lax.all_to_all(pieces, 'tp', 1, 1, tiled=True)  19.2 us
    all_to_all x1, starting transfers between devices, per_device(): incoming = lax.all_to_all(cache_both[peer_groups], 'sz', 0, 0, tiled=True)  15.9 us
    all_gather x1, blocking collectives, per_device(): gathered = lax.all_gather(hidden_in, 'tp', axis=1, tiled=True)  14.6 us
    ppermute x1, starting transfers between devices, per_device(): lax.ppermute(jnp.stack([keys_new, values_new]), 'sz', partner_pairs)  12.3 us
    all_gather x1, blocking collectives, per_device(): all_queries = lax.all_gather(queries, 'sx', axis=0, tiled=True)  11 us
    pallas_call x1, Pallas kernels, attention(): pl.pallas_call(attention_kernel, out_shape=jax.ShapeDtypeStruct((rows //...  8.61 us
    ppermute x1, waiting for transfers between devices, per_device(): lax.ppermute(jnp.stack([keys_new, values_new]), 'sz', partner_pairs)  7.87 us
    all_to_all x1, waiting for transfers between devices, per_device(): packed_in = lax.all_to_all(packed, 'sx', 0, 0, tiled=True)  6.57 us
  transfers between devices with their start and end apart: 3, of which 2 were waited for; matrix products, arithmetic and copies ran while one was open for 8% of the time, Pallas kernels for 0%

profile of v15, /device:TPU:1, one launch (start us, length us, event | category | flops | bytes accessed | tf_op | source)
XLA Modules:
  0.0 119.2 jit_solution(4623614880370002976)
XLA Ops:
  0.0 0.7 copy-done.1
  0.8 0.7 gather_fusion
  1.6 1.6 %gather_fusion.1 = bf16[16,2,128,128]{3,2,1,0:T(8,128)(2,1)} fusion(bf16[2,2,128,128]{3,2,0,1:T(8,128)(2,1)S(1)} %pad_maximum_fusion, s32[1024]{0:T(1024)S(1)} %pad_clamp_fusion), kind=kCustom, calls=%fused_computation.1 | custom fusion | bytes 2097216 | tf_op jit(solution)/shard_map/gather | solution.py:162
  3.3 15.9 %all-to-all-start = ((bf16[16,2,128,128]{3,2,1,0:T(8,128)(2,1)}), bf16[16,2,128,128]{3,2,1,0:T(8,128)(2,1)S(1)}, u32[]{:S(2)}, u32[]{:S(2)}) async-start(bf16[16,2,128,128]{3,2,1,0:T(8,128)(2,1)} %gather_fusion.1), calls=%async_computation | async-start | bytes 2097152 | tf_op jit(solution)/shard_map/all_to_all | solution.py:162
  19.2 14.6 %all_gather.6 = bf16[128,2048]{1,0:T(8,128)(2,1)S(1)} all-gather(bf16[128,256]{1,0:T(8,128)(2,1)S(1)} %copy-done.3), channel_id=1, replica_groups=mesh['sx'=4,'sz'=16,'tp'=8] {'tp'}, dimensions={1}, use_global_device_ids=true | all-gather | bytes 589824 | tf_op jit(solution)/shard_map/all_gather | solution.py:168
  34.0 0.5 copy-done.11
  34.5 0.4 multiply_reduce_fusion.1
  35.0 0.6 copy-done.12
  35.7 0.6 dynamic_slice.3
  36.9 0.6 copy-done.6
  38.4 12.3 %collective-permute-start = (bf16[2,128,1,128]{3,1,2,0:T(8,128)(2,1)S(1)}, bf16[2,128,1,128]{3,1,2,0:T(8,128)(2,1)S(1)}, u32[]{:S(2)}, u32[]{:S(2)}) collective-permute-start(bf16[2,128,1,128]{3,1,2,0:T(8,128)(2,1)S(1)} %pad_maximum_fusion.2), channel_id=1, source_target_pairs={{0,64},{8,72},{16,80},{24,88},{32,96},{40,104},{48,112},{56,120},{... | collective-permute-start | bytes 196616 | tf_op jit(solution)/shard_map/ppermute | solution.py:192
  50.9 0.9 broadcast_in_dim_reshape.5.qtok_ref
  51.8 1.6 %fusion.27 = f32[128,256]{1,0:T(8,128)S(1)} fusion(bf16[2048,256]{1,0:T(8,128)(2,1)} %param.15, bf16[128,2048]{1,0:T(8,128)(2,1)S(1)} %all_gather.6, f32[2048]{0:T(1024)S(1)} %copy-done.11, f32[128]{0:T(128)S(1)} %add_rsqrt_fusion.2), kind=kOutput, calls=%fused_computation.73 | convolution fusion | flops 135266304 | bytes 1712640 | tf_op jit(solution)/shard_map/dot_general | solution.py:174
  53.5 1.2 pad_add_fusion.1.scalars
  54.7 0.5 pad_add_fusion
  56.8 11.0 %all_gather.7 = bf16[512,1,2,128]{3,2,1,0:T(2,128)(2,1)} all-gather(bf16[128,1,2,128]{3,2,1,0:T(2,128)(2,1)S(1)} %pad_maximum_fusion.1), channel_id=1, replica_groups=mesh['sx'=4,'sz'=16,'tp'=8] {'sx'}, dimensions={0}, use_global_device_ids=true | all-gather | bytes 327680 | tf_op jit(solution)/shard_map/all_gather | solution.py:194
  67.8 7.9 %collective-permute-done = bf16[2,128,1,128]{3,1,2,0:T(8,128)(2,1)S(1)} collective-permute-done((bf16[2,128,1,128]{3,1,2,0:T(8,128)(2,1)S(1)}, bf16[2,128,1,128]{3,1,2,0:T(8,128)(2,1)S(1)}, u32[]{:S(2)}, u32[]{:S(2)}) %collective-permute-start) | collective-permute-done | bytes 65568 | tf_op jit(solution)/shard_map/ppermute | solution.py:192
  75.7 0.7 maximum_bitcast_fusion
  76.4 1.0 copy-done.2
  77.4 8.6 %shard_map.127 = f32[4,260,128]{2,1,0:T(8,128)} custom-call(s32[2]{0:T(128)} %pad_add_fusion.1.scalars, bf16[1024,128]{1,0:T(8,128)(2,1)} %bitcast.79, s32[1024,1]{1,0:T(8,128)} %broadcast_in_dim_reshape.5.qtok_ref, bf16[16,2,128,128]{3,2,1,0:T(8,128)(2,1)} %copy-done.2, bf16[256,128]{1,0:T(8,128)(2,1)} %get-tuple-element.15.kn_ref, ...), custom_call_target="tpu_custom_call" | custom-call | flops 1207959552 | bytes 1966080 | tf_op jit(solution)/shard_map/pallas_call | solution.py:103
  86.0 4.1 %all-to-all-start.1 = ((f32[4,260,128]{2,1,0:T(8,128)}), f32[4,260,128]{2,1,0:T(8,128)S(1)}, u32[]{:S(2)}, u32[]{:S(2)}) async-start(f32[4,260,128]{2,1,0:T(8,128)} %shard_map.127), calls=%async_computation.1 | async-start | bytes 1081344 | tf_op jit(solution)/shard_map/all_to_all | solution.py:215
  90.6 6.6 %all-to-all-done.1 = f32[4,260,128]{2,1,0:T(8,128)S(1)} async-done(((f32[4,260,128]{2,1,0:T(8,128)}), f32[4,260,128]{2,1,0:T(8,128)S(1)}, u32[]{:S(2)}, u32[]{:S(2)}) %all-to-all-start.1) | async-done | bytes 532512 | tf_op jit(solution)/shard_map/all_to_all | solution.py:215
  99.3 19.2 %all_to_all.15 = bf16[128,8,256]{2,0,1:T(8,128)(2,1)S(1)} all-to-all(bf16[128,8,256]{2,0,1:T(8,128)(2,1)S(1)} %bitcast.72), channel_id=1, replica_groups=mesh['sx'=4,'sz'=16,'tp'=8] {'tp'}, dimensions={1} | all-to-all | bytes 1048576 | tf_op jit(solution)/shard_map/all_to_all | solution.py:231
  118.5 0.6 add_convert_fusion
  (64 shorter events, 5.8 us)
Async XLA Ops:
  0.0 98.9 %copy-start = (bf16[256,2048]{1,0:T(8,128)(2,1)S(1)}, bf16[256,2048]{1,0:T(8,128)(2,1)}, u32[]{:S(2)}) copy-start(bf16[256,2048]{1,0:T(8,128)(2,1)} %param.19) | copy-start | bytes 3145732
  0.0 0.7 copy-start.1
  0.8 0.8 copy-start.4
  0.8 0.9 copy-start.5
  3.3 15.9 %copy-start.3 = (bf16[128,256]{1,0:T(8,128)(2,1)S(1)}, bf16[128,256]{1,0:T(8,128)(2,1)}, u32[]{:S(2)}) copy-start(bf16[128,256]{1,0:T(8,128)(2,1)} %param.13) | copy-start | bytes 196612
  3.3 73.1 %all-to-all-start = ((bf16[16,2,128,128]{3,2,1,0:T(8,128)(2,1)}), bf16[16,2,128,128]{3,2,1,0:T(8,128)(2,1)S(1)}, u32[]{:S(2)}, u32[]{:S(2)}) async-start(bf16[16,2,128,128]{3,2,1,0:T(8,128)(2,1)} %gather_fusion.1), calls=%async_computation | async-start | bytes 2097152 | tf_op jit(solution)/shard_map/all_to_all | solution.py:162
  19.2 14.8 %copy-start.8 = (bf16[2048,128]{1,0:T(8,128)(2,1)S(1)}, bf16[2048,128]{1,0:T(8,128)(2,1)}, u32[]{:S(2)}) copy-start(bf16[2048,128]{1,0:T(8,128)(2,1)} %param.16) | copy-start | bytes 1572868
  33.8 0.7 copy-start.11
  34.4 3.5 %copy-start.9 = (bf16[2048,128]{1,0:T(8,128)(2,1)S(1)}, bf16[2048,128]{1,0:T(8,128)(2,1)}, u32[]{:S(2)}) copy-start(bf16[2048,128]{1,0:T(8,128)(2,1)} %param.17) | copy-start | bytes 1572868
  35.0 0.7 copy-start.12
  36.8 0.7 copy-start.6
  38.4 37.3 %collective-permute-start = (bf16[2,128,1,128]{3,1,2,0:T(8,128)(2,1)S(1)}, bf16[2,128,1,128]{3,1,2,0:T(8,128)(2,1)S(1)}, u32[]{:S(2)}, u32[]{:S(2)}) collective-permute-start(bf16[2,128,1,128]{3,1,2,0:T(8,128)(2,1)S(1)} %pad_maximum_fusion.2), channel_id=1, source_target_pairs={{0,64},{8,72},{16,80},{24,88},{32,96},{40,104},{48,112},{56,120},{... | collective-permute-start | bytes 196616 | tf_op jit(solution)/shard_map/ppermute | solution.py:192
  55.4 0.7 copy-start.7
  76.4 1.0 copy-start.2
  86.0 4.2 %copy-start.10 = (bf16[2048,2]{0,1:T(2,128)(2,1)S(1)}, bf16[2048,2]{0,1:T(2,128)(2,1)}, u32[]{:S(2)}) copy-start(bf16[2048,2]{0,1:T(2,128)(2,1)} %param.18) | copy-start | bytes 24580
  86.0 11.2 %all-to-all-start.1 = ((f32[4,260,128]{2,1,0:T(8,128)}), f32[4,260,128]{2,1,0:T(8,128)S(1)}, u32[]{:S(2)}, u32[]{:S(2)}) async-start(f32[4,260,128]{2,1,0:T(8,128)} %shard_map.127), calls=%async_computation.1 | async-start | bytes 1081344 | tf_op jit(solution)/shard_map/all_to_all | solution.py:215

commit v16 on v15

--- a/solution.py
+++ b/solution.py
@@ -58,7 +58,7 @@
     return (new_max, new_sum, running_acc * rescale[..., None] + update)
 
 
-def attention_kernel(scalars, q_ref, qtok_ref, cache_ref, kn_ref, vn_ref, ktok_ref, out_ref):
+def attention_kernel(scalars, q_ref, qtok_ref, cache_ref, kn_ref, kp_ref, vn_ref, vp_ref, ktok_ref, out_ref):
     scale = q_ref.shape[-1] ** (-0.5)
     dims = (((1,), (1,)), ((), ()))
     q = q_ref[...]
@@ -69,7 +69,9 @@
     cache_pos = scalars[1] + lax.broadcasted_iota(jnp.int32, (1, sources * depth), 1)
     cache_seen = cache_pos < scalars[0]
     cache_scores = jnp.where(cache_seen, cache_scores, masked_score)
-    new_scores = lax.dot_general(q, kn_ref[...], dims, preferred_element_type=jnp.float32) * scale
+    keys_new = jnp.concatenate([kn_ref[...], kp_ref[...]], 0)
+    values_new = jnp.concatenate([vn_ref[...], vp_ref[...]], 0)
+    new_scores = lax.dot_general(q, keys_new, dims, preferred_element_type=jnp.float32) * scale
     new_seen = ktok_ref[...] <= qtok_ref[...]
     new_scores = jnp.where(new_seen, new_scores, masked_score)
     top = jnp.maximum(
@@ -80,7 +82,7 @@
     total = jnp.sum(cache_expo, 1, keepdims=True) + jnp.sum(new_expo, 1, keepdims=True)
     acc = jnp.dot(
         cache_expo.astype(jnp.bfloat16), values_cache, preferred_element_type=jnp.float32
-    ) + jnp.dot(new_expo.astype(jnp.bfloat16), vn_ref[...], preferred_element_type=jnp.float32)
+    ) + jnp.dot(new_expo.astype(jnp.bfloat16), values_new, preferred_element_type=jnp.float32)
     rows, width = acc.shape
     top_t = jnp.transpose(jnp.broadcast_to(top, (rows, width)))[0:1]
     total_t = jnp.transpose(jnp.broadcast_to(total, (rows, width)))[0:1]
@@ -91,10 +93,10 @@
         out_ref[0, rows + rows // width + half : rows + rows // width + half + 1, :] = total_t[:, cols]
 
 
-def attention(scalars, q_rows, q_tok, cache_both, keys_new, values_new, key_tok):
+def attention(scalars, q_rows, q_tok, cache_both, keys_new, keys_partner, values_new, values_partner, key_tok):
     rows, width = q_rows.shape
     cache_rows = cache_both.shape[0] * cache_both.shape[2]
-    new_rows = keys_new.shape[0]
+    new_rows = 2 * keys_new.shape[0]
     block = 256
     packed_rows = block + 2 * (block // width)
     full = lambda shape: pl.BlockSpec(shape, lambda i, s: (0, 0))
@@ -110,8 +112,10 @@
                 row_block(width),
                 row_block(1),
                 pl.BlockSpec(cache_both.shape, lambda i, s: (0, 0, 0, 0)),
-                full((new_rows, width)),
-                full((new_rows, width)),
+                full((new_rows // 2, width)),
+                full((new_rows // 2, width)),
+                full((new_rows // 2, width)),
+                full((new_rows // 2, width)),
                 full((1, new_rows)),
             ],
             out_specs=pl.BlockSpec((1, packed_rows, width), lambda i, s: (i, 0, 0)),
@@ -121,7 +125,7 @@
             transcendentals=rows * (cache_rows + new_rows),
             bytes_accessed=2 * (rows + 2 * cache_rows + 2 * new_rows) * width + 4 * rows * width,
         ),
-    )(scalars, q_rows, q_tok, cache_both, keys_new, values_new, key_tok)
+    )(scalars, q_rows, q_tok, cache_both, keys_new, keys_partner, values_new, values_partner, key_tok)
 
 
 def per_device(
@@ -207,8 +211,10 @@
         all_queries.reshape(-1, head_dim),
         jnp.repeat(query_tok, heads_local)[:, None],
         incoming,
-        keys_two,
-        values_two,
+        keys_new.reshape(-1, head_dim),
+        partner_kv[0].reshape(-1, head_dim),
+        values_new.reshape(-1, head_dim),
+        partner_kv[1].reshape(-1, head_dim),
         key_tok[None, :],
     )
     slot_rows = tok_rows * heads_local

time: 121 us -> 121 us (level)
  waiting for transfers between devices: 14.4 us -> 13.1 us
    ppermute x1, waiting for transfers between devices: 7.87 us -> 6.52 us  [per_device(): lax.ppermute(jnp.stack([keys_new, values_new]), 'sz', partner_pairs)]
    unnamed x26 -> x28, local copies, waits for them, and re-layouts: 4.02 us -> 4.52 us
where the time goes in v16:
time: 121 us; the launch traced here: 119 us
  blocking collectives  44.8 us (37%)
  starting transfers between devices  32.2 us (27%)
  waiting for transfers between devices  13.1 us (11%)
  local copies, waits for them, and re-layouts  10.1 us (8%)
  Pallas kernels  8.63 us (7%)
  other arithmetic  6.22 us (5%)
  matrix products  2.98 us (2%)
    all_to_all x1, blocking collectives, per_device(): arrived = lax.all_to_all(pieces, 'tp', 1, 1, tiled=True)  19.2 us
    all_to_all x1, starting transfers between devices, per_device(): incoming = lax.all_to_all(cache_both[peer_groups], 'sz', 0, 0, tiled=True)  15.9 us
    all_gather x1, blocking collectives, per_device(): gathered = lax.all_gather(hidden_in, 'tp', axis=1, tiled=True)  14.6 us
    ppermute x1, starting transfers between devices, per_device(): lax.ppermute(jnp.stack([keys_new, values_new]), 'sz', partner_pairs)  12.2 us
    all_gather x1, blocking collectives, per_device(): all_queries = lax.all_gather(queries, 'sx', axis=0, tiled=True)  11 us
    pallas_call x1, Pallas kernels, attention(): pl.pallas_call(attention_kernel, out_shape=jax.ShapeDtypeStruct((rows //...  8.63 us
    all_to_all x1, waiting for transfers between devices, per_device(): packed_in = lax.all_to_all(packed, 'sx', 0, 0, tiled=True)  6.57 us
    ppermute x1, waiting for transfers between devices, per_device(): lax.ppermute(jnp.stack([keys_new, values_new]), 'sz', partner_pairs)  6.52 us
  transfers between devices with their start and end apart: 3, of which 2 were waited for; matrix products, arithmetic and copies ran while one was open for 8% of the time, Pallas kernels for 0%

profile of v16, /device:TPU:1, one launch (start us, length us, event | category | flops | bytes accessed | tf_op | source)
XLA Modules:
  0.0 119.1 jit_solution(1435270237060336959)
XLA Ops:
  0.0 0.7 copy-done.1
  0.8 0.7 gather_fusion
  1.6 1.6 %gather_fusion.1 = bf16[16,2,128,128]{3,2,1,0:T(8,128)(2,1)} fusion(bf16[2,2,128,128]{3,2,0,1:T(8,128)(2,1)S(1)} %pad_maximum_fusion, s32[1024]{0:T(1024)S(1)} %pad_clamp_fusion), kind=kCustom, calls=%fused_computation.1 | custom fusion | bytes 2097216 | tf_op jit(solution)/shard_map/gather | solution.py:166
  3.3 15.9 %all-to-all-start = ((bf16[16,2,128,128]{3,2,1,0:T(8,128)(2,1)}), bf16[16,2,128,128]{3,2,1,0:T(8,128)(2,1)S(1)}, u32[]{:S(2)}, u32[]{:S(2)}) async-start(bf16[16,2,128,128]{3,2,1,0:T(8,128)(2,1)} %gather_fusion.1), calls=%async_computation | async-start | bytes 2097152 | tf_op jit(solution)/shard_map/all_to_all | solution.py:166
  19.2 14.6 %all_gather.6 = bf16[128,2048]{1,0:T(8,128)(2,1)S(1)} all-gather(bf16[128,256]{1,0:T(8,128)(2,1)S(1)} %copy-done.3), channel_id=1, replica_groups=mesh['sx'=4,'sz'=16,'tp'=8] {'tp'}, dimensions={1}, use_global_device_ids=true | all-gather | bytes 589824 | tf_op jit(solution)/shard_map/all_gather | solution.py:172
  35.0 0.6 copy-done.13
  35.7 0.6 dynamic_slice.3
  37.0 0.6 copy-done.7
  38.5 0.5 copy-done.6
  39.0 12.2 %collective-permute-start = (bf16[2,128,1,128]{3,1,2,0:T(8,128)(2,1)S(1)}, bf16[2,128,1,128]{3,1,2,0:T(8,128)(2,1)S(1)}, u32[]{:S(2)}, u32[]{:S(2)}) collective-permute-start(bf16[2,128,1,128]{3,1,2,0:T(8,128)(2,1)S(1)} %pad_maximum_fusion.2), channel_id=1, source_target_pairs={{0,64},{8,72},{16,80},{24,88},{32,96},{40,104},{48,112},{56,120},{... | collective-permute-start | bytes 196616 | tf_op jit(solution)/shard_map/ppermute | solution.py:196
  51.5 0.9 broadcast_in_dim_reshape.5.qtok_ref
  52.4 1.6 %fusion.27 = f32[128,256]{1,0:T(8,128)S(1)} fusion(bf16[2048,256]{1,0:T(8,128)(2,1)} %param.15, bf16[128,2048]{1,0:T(8,128)(2,1)S(1)} %all_gather.6, f32[2048]{0:T(1024)S(1)} %copy-done.12, f32[128]{0:T(128)S(1)} %add_rsqrt_fusion.2), kind=kOutput, calls=%fused_computation.72 | convolution fusion | flops 135266304 | bytes 1712640 | tf_op jit(solution)/shard_map/dot_general | solution.py:178
  54.1 1.2 %pad_add_fusion.1.scalars = s32[2]{0:T(128)} fusion(s32[1]{0:T(128)} %bitcast, s32[1]{0:T(128)} %dynamic_slice.3), kind=kLoop, calls=%fused_computation.63 | loop fusion | flops 2 | bytes 16 | tf_op jit(solution)/shard_map/stack | solution.py:208
  55.3 0.6 pad_add_fusion
  55.9 0.7 pad_maximum_fusion.3.kn_ref
  58.2 11.0 %all_gather.7 = bf16[512,1,2,128]{3,2,1,0:T(2,128)(2,1)} all-gather(bf16[128,1,2,128]{3,2,1,0:T(2,128)(2,1)S(1)} %pad_maximum_fusion.1), channel_id=1, replica_groups=mesh['sx'=4,'sz'=16,'tp'=8] {'sx'}, dimensions={0}, use_global_device_ids=true | all-gather | bytes 327680 | tf_op jit(solution)/shard_map/all_gather | solution.py:198
  69.2 6.5 %collective-permute-done = bf16[2,128,1,128]{3,1,2,0:T(8,128)(2,1)S(1)} collective-permute-done((bf16[2,128,1,128]{3,1,2,0:T(8,128)(2,1)S(1)}, bf16[2,128,1,128]{3,1,2,0:T(8,128)(2,1)S(1)}, u32[]{:S(2)}, u32[]{:S(2)}) %collective-permute-start) | collective-permute-done | bytes 65568 | tf_op jit(solution)/shard_map/ppermute | solution.py:196
  75.7 0.6 slice_bitcast_fusion.1
  76.3 1.0 copy-done.2
  77.3 8.6 %shard_map.127 = f32[4,260,128]{2,1,0:T(8,128)} custom-call(s32[2]{0:T(128)} %pad_add_fusion.1.scalars, bf16[1024,128]{1,0:T(8,128)(2,1)} %bitcast.78, s32[1024,1]{1,0:T(8,128)} %broadcast_in_dim_reshape.5.qtok_ref, bf16[16,2,128,128]{3,2,1,0:T(8,128)(2,1)} %copy-done.2, bf16[128,128]{1,0:T(8,128)(2,1)} %pad_maximum_fusion.3.kn_ref, ...), custom_call_target="tpu_custom_call" | custom-call | flops 1207959552 | bytes 1966080 | tf_op jit(solution)/shard_map/pallas_call | solution.py:105
  85.9 4.1 %all-to-all-start.1 = ((f32[4,260,128]{2,1,0:T(8,128)}), f32[4,260,128]{2,1,0:T(8,128)S(1)}, u32[]{:S(2)}, u32[]{:S(2)}) async-start(f32[4,260,128]{2,1,0:T(8,128)} %shard_map.127), calls=%async_computation.1 | async-start | bytes 1081344 | tf_op jit(solution)/shard_map/all_to_all | solution.py:221
  90.5 6.6 %all-to-all-done.1 = f32[4,260,128]{2,1,0:T(8,128)S(1)} async-done(((f32[4,260,128]{2,1,0:T(8,128)}), f32[4,260,128]{2,1,0:T(8,128)S(1)}, u32[]{:S(2)}, u32[]{:S(2)}) %all-to-all-start.1) | async-done | bytes 532512 | tf_op jit(solution)/shard_map/all_to_all | solution.py:221
  99.2 19.2 %all_to_all.15 = bf16[128,8,256]{2,0,1:T(8,128)(2,1)S(1)} all-to-all(bf16[128,8,256]{2,0,1:T(8,128)(2,1)S(1)} %bitcast.69), channel_id=1, replica_groups=mesh['sx'=4,'sz'=16,'tp'=8] {'tp'}, dimensions={1} | all-to-all | bytes 1048576 | tf_op jit(solution)/shard_map/all_to_all | solution.py:237
  118.5 0.6 add_convert_fusion
  (66 shorter events, 6.7 us)
Async XLA Ops:
  0.0 98.8 %copy-start = (bf16[256,2048]{1,0:T(8,128)(2,1)S(1)}, bf16[256,2048]{1,0:T(8,128)(2,1)}, u32[]{:S(2)}) copy-start(bf16[256,2048]{1,0:T(8,128)(2,1)} %param.19) | copy-start | bytes 3145732
  0.0 0.7 copy-start.1
  0.8 0.8 copy-start.4
  0.8 0.9 copy-start.5
  3.3 15.9 %copy-start.3 = (bf16[128,256]{1,0:T(8,128)(2,1)S(1)}, bf16[128,256]{1,0:T(8,128)(2,1)}, u32[]{:S(2)}) copy-start(bf16[128,256]{1,0:T(8,128)(2,1)} %param.13) | copy-start | bytes 196612
  3.3 73.0 %all-to-all-start = ((bf16[16,2,128,128]{3,2,1,0:T(8,128)(2,1)}), bf16[16,2,128,128]{3,2,1,0:T(8,128)(2,1)S(1)}, u32[]{:S(2)}, u32[]{:S(2)}) async-start(bf16[16,2,128,128]{3,2,1,0:T(8,128)(2,1)} %gather_fusion.1), calls=%async_computation | async-start | bytes 2097152 | tf_op jit(solution)/shard_map/all_to_all | solution.py:166
  19.2 14.8 %copy-start.9 = (bf16[2048,128]{1,0:T(8,128)(2,1)S(1)}, bf16[2048,128]{1,0:T(8,128)(2,1)}, u32[]{:S(2)}) copy-start(bf16[2048,128]{1,0:T(8,128)(2,1)} %param.16) | copy-start | bytes 1572868
  33.8 0.7 copy-start.12
  34.5 3.6 %copy-start.10 = (bf16[2048,128]{1,0:T(8,128)(2,1)S(1)}, bf16[2048,128]{1,0:T(8,128)(2,1)}, u32[]{:S(2)}) copy-start(bf16[2048,128]{1,0:T(8,128)(2,1)} %param.17) | copy-start | bytes 1572868
  35.0 0.7 copy-start.13
  37.0 0.7 copy-start.7
  38.4 0.6 copy-start.6
  39.0 36.7 %collective-permute-start = (bf16[2,128,1,128]{3,1,2,0:T(8,128)(2,1)S(1)}, bf16[2,128,1,128]{3,1,2,0:T(8,128)(2,1)S(1)}, u32[]{:S(2)}, u32[]{:S(2)}) collective-permute-start(bf16[2,128,1,128]{3,1,2,0:T(8,128)(2,1)S(1)} %pad_maximum_fusion.2), channel_id=1, source_target_pairs={{0,64},{8,72},{16,80},{24,88},{32,96},{40,104},{48,112},{56,120},{... | collective-permute-start | bytes 196616 | tf_op jit(solution)/shard_map/ppermute | solution.py:196
  56.8 0.7 copy-start.8
  76.3 1.0 copy-start.2
  85.9 4.2 %copy-start.11 = (bf16[2048,2]{0,1:T(2,128)(2,1)S(1)}, bf16[2048,2]{0,1:T(2,128)(2,1)}, u32[]{:S(2)}) copy-start(bf16[2048,2]{0,1:T(2,128)(2,1)} %param.18) | copy-start | bytes 24580
  85.9 11.2 %all-to-all-start.1 = ((f32[4,260,128]{2,1,0:T(8,128)}), f32[4,260,128]{2,1,0:T(8,128)S(1)}, u32[]{:S(2)}, u32[]{:S(2)}) async-start(f32[4,260,128]{2,1,0:T(8,128)} %shard_map.127), calls=%async_computation.1 | async-start | bytes 1081344 | tf_op jit(solution)/shard_map/all_to_all | solution.py:221

commit v17 on v16

--- a/solution.py
+++ b/solution.py
@@ -58,13 +58,24 @@
     return (new_max, new_sum, running_acc * rescale[..., None] + update)
 
 
-def attention_kernel(scalars, q_ref, qtok_ref, cache_ref, kn_ref, kp_ref, vn_ref, vp_ref, ktok_ref, out_ref):
+def attention_kernel(
+    scalars, q_ref, qtok_ref, cache_hbm, kn_ref, kp_ref, vn_ref, vp_ref, ktok_ref, out_ref, cache_ref, sems
+):
+    first = pl.program_id(0) == 0
+    key_copy = pltpu.make_async_copy(cache_hbm.at[:, 0], cache_ref.at[:, 0], sems.at[0])
+    value_copy = pltpu.make_async_copy(cache_hbm.at[:, 1], cache_ref.at[:, 1], sems.at[1])
+
+    @pl.when(first)
+    def _():
+        key_copy.start()
+        value_copy.start()
+        key_copy.wait()
+
     scale = q_ref.shape[-1] ** (-0.5)
     dims = (((1,), (1,)), ((), ()))
     q = q_ref[...]
     sources, _, depth, width = cache_ref.shape
     keys_cache = cache_ref[:, 0].reshape(sources * depth, width)
-    values_cache = cache_ref[:, 1].reshape(sources * depth, width)
     cache_scores = lax.dot_general(q, keys_cache, dims, preferred_element_type=jnp.float32) * scale
     cache_pos = scalars[1] + lax.broadcasted_iota(jnp.int32, (1, sources * depth), 1)
     cache_seen = cache_pos < scalars[0]
@@ -80,6 +91,12 @@
     cache_expo = jnp.where(cache_seen, jnp.exp(cache_scores - top), 0.0)
     new_expo = jnp.where(new_seen, jnp.exp(new_scores - top), 0.0)
     total = jnp.sum(cache_expo, 1, keepdims=True) + jnp.sum(new_expo, 1, keepdims=True)
+
+    @pl.when(first)
+    def _():
+        value_copy.wait()
+
+    values_cache = cache_ref[:, 1].reshape(sources * depth, width)
     acc = jnp.dot(
         cache_expo.astype(jnp.bfloat16), values_cache, preferred_element_type=jnp.float32
     ) + jnp.dot(new_expo.astype(jnp.bfloat16), values_new, preferred_element_type=jnp.float32)
@@ -111,7 +128,7 @@
             in_specs=[
                 row_block(width),
                 row_block(1),
-                pl.BlockSpec(cache_both.shape, lambda i, s: (0, 0, 0, 0)),
+                pl.BlockSpec(memory_space=pl.ANY),
                 full((new_rows // 2, width)),
                 full((new_rows // 2, width)),
                 full((new_rows // 2, width)),
@@ -119,6 +136,10 @@
                 full((1, new_rows)),
             ],
             out_specs=pl.BlockSpec((1, packed_rows, width), lambda i, s: (i, 0, 0)),
+            scratch_shapes=[
+                pltpu.VMEM(cache_both.shape, cache_both.dtype),
+                pltpu.SemaphoreType.DMA((2,)),
+            ],
         ),
         cost_estimate=pl.CostEstimate(
             flops=flops,

time: 121 us -> 122 us (level)
  Pallas kernels: 8.63 us -> 9.86 us
    pallas_call x1, Pallas kernels: 8.63 us -> 9.86 us  [attention(): pl.pallas_call(attention_kernel, out_shape=jax.ShapeDtypeStruct((rows //...]
where the time goes in v17:
time: 122 us; the launch traced here: 120 us
  blocking collectives  44.8 us (37%)
  starting transfers between devices  32.1 us (26%)
  waiting for transfers between devices  13.1 us (11%)
  local copies, waits for them, and re-layouts  10.1 us (8%)
  Pallas kernels  9.86 us (8%)
  other arithmetic  6.22 us (5%)
  matrix products  2.98 us (2%)
    all_to_all x1, blocking collectives, per_device(): arrived = lax.all_to_all(pieces, 'tp', 1, 1, tiled=True)  19.2 us
    all_to_all x1, starting transfers between devices, per_device(): incoming = lax.all_to_all(cache_both[peer_groups], 'sz', 0, 0, tiled=True)  15.9 us
    all_gather x1, blocking collectives, per_device(): gathered = lax.all_gather(hidden_in, 'tp', axis=1, tiled=True)  14.6 us
    ppermute x1, starting transfers between devices, per_device(): lax.ppermute(jnp.stack([keys_new, values_new]), 'sz', partner_pairs)  12.2 us
    all_gather x1, blocking collectives, per_device(): all_queries = lax.all_gather(queries, 'sx', axis=0, tiled=True)  11 us
    pallas_call x1, Pallas kernels, attention(): pl.pallas_call(attention_kernel, out_shape=jax.ShapeDtypeStruct((rows //...  9.86 us
    all_to_all x1, waiting for transfers between devices, per_device(): packed_in = lax.all_to_all(packed, 'sx', 0, 0, tiled=True)  6.57 us
    ppermute x1, waiting for transfers between devices, per_device(): lax.ppermute(jnp.stack([keys_new, values_new]), 'sz', partner_pairs)  6.52 us
  transfers between devices with their start and end apart: 3, of which 2 were waited for; matrix products, arithmetic and copies ran while one was open for 8% of the time, Pallas kernels for 0%

profile of v17, /device:TPU:1, one launch (start us, length us, event | category | flops | bytes accessed | tf_op | source)
XLA Modules:
  0.0 120.2 jit_solution(13049303154607038899)
XLA Ops:
  0.0 0.7 copy-done.1
  0.8 0.7 gather_fusion
  1.6 1.6 %gather_fusion.1 = bf16[16,2,128,128]{3,2,1,0:T(8,128)(2,1)} fusion(bf16[2,2,128,128]{3,2,0,1:T(8,128)(2,1)S(1)} %pad_maximum_fusion, s32[1024]{0:T(1024)S(1)} %pad_clamp_fusion), kind=kCustom, calls=%fused_computation.1 | custom fusion | bytes 2097216 | tf_op jit(solution)/shard_map/gather | solution.py:187
  3.3 15.9 %all-to-all-start = ((bf16[16,2,128,128]{3,2,1,0:T(8,128)(2,1)}), bf16[16,2,128,128]{3,2,1,0:T(8,128)(2,1)S(1)}, u32[]{:S(2)}, u32[]{:S(2)}) async-start(bf16[16,2,128,128]{3,2,1,0:T(8,128)(2,1)} %gather_fusion.1), calls=%async_computation | async-start | bytes 2097152 | tf_op jit(solution)/shard_map/all_to_all | solution.py:187
  19.2 14.6 %all_gather.6 = bf16[128,2048]{1,0:T(8,128)(2,1)S(1)} all-gather(bf16[128,256]{1,0:T(8,128)(2,1)S(1)} %copy-done.3), channel_id=1, replica_groups=mesh['sx'=4,'sz'=16,'tp'=8] {'tp'}, dimensions={1}, use_global_device_ids=true | all-gather | bytes 589824 | tf_op jit(solution)/shard_map/all_gather | solution.py:193
  35.0 0.6 copy-done.13
  35.7 0.6 dynamic_slice.3
  37.0 0.6 copy-done.7
  38.5 0.5 copy-done.6
  39.0 12.2 %collective-permute-start = (bf16[2,128,1,128]{3,1,2,0:T(8,128)(2,1)S(1)}, bf16[2,128,1,128]{3,1,2,0:T(8,128)(2,1)S(1)}, u32[]{:S(2)}, u32[]{:S(2)}) collective-permute-start(bf16[2,128,1,128]{3,1,2,0:T(8,128)(2,1)S(1)} %pad_maximum_fusion.2), channel_id=1, source_target_pairs={{0,64},{8,72},{16,80},{24,88},{32,96},{40,104},{48,112},{56,120},{... | collective-permute-start | bytes 196616 | tf_op jit(solution)/shard_map/ppermute | solution.py:217
  51.5 0.9 broadcast_in_dim_reshape.5.qtok_ref
  52.4 1.6 %fusion.27 = f32[128,256]{1,0:T(8,128)S(1)} fusion(bf16[2048,256]{1,0:T(8,128)(2,1)} %param.15, bf16[128,2048]{1,0:T(8,128)(2,1)S(1)} %all_gather.6, f32[2048]{0:T(1024)S(1)} %copy-done.12, f32[128]{0:T(128)S(1)} %add_rsqrt_fusion.2), kind=kOutput, calls=%fused_computation.72 | convolution fusion | flops 135266304 | bytes 1712640 | tf_op jit(solution)/shard_map/dot_general | solution.py:199
  54.1 1.2 %pad_add_fusion.1.scalars = s32[2]{0:T(128)} fusion(s32[1]{0:T(128)} %bitcast, s32[1]{0:T(128)} %dynamic_slice.3), kind=kLoop, calls=%fused_computation.63 | loop fusion | flops 2 | bytes 16 | tf_op jit(solution)/shard_map/stack | solution.py:229
  55.3 0.6 pad_add_fusion
  55.9 0.7 pad_maximum_fusion.3.kn_ref
  58.2 11.0 %all_gather.7 = bf16[512,1,2,128]{3,2,1,0:T(2,128)(2,1)} all-gather(bf16[128,1,2,128]{3,2,1,0:T(2,128)(2,1)S(1)} %pad_maximum_fusion.1), channel_id=1, replica_groups=mesh['sx'=4,'sz'=16,'tp'=8] {'sx'}, dimensions={0}, use_global_device_ids=true | all-gather | bytes 327680 | tf_op jit(solution)/shard_map/all_gather | solution.py:219
  69.2 6.5 %collective-permute-done = bf16[2,128,1,128]{3,1,2,0:T(8,128)(2,1)S(1)} collective-permute-done((bf16[2,128,1,128]{3,1,2,0:T(8,128)(2,1)S(1)}, bf16[2,128,1,128]{3,1,2,0:T(8,128)(2,1)S(1)}, u32[]{:S(2)}, u32[]{:S(2)}) %collective-permute-start) | collective-permute-done | bytes 65568 | tf_op jit(solution)/shard_map/ppermute | solution.py:217
  75.7 0.6 slice_bitcast_fusion.1
  76.3 1.0 copy-done.2
  77.3 9.9 %shard_map.127 = f32[4,260,128]{2,1,0:T(8,128)} custom-call(s32[2]{0:T(128)} %pad_add_fusion.1.scalars, bf16[1024,128]{1,0:T(8,128)(2,1)} %bitcast.78, s32[1024,1]{1,0:T(8,128)} %broadcast_in_dim_reshape.5.qtok_ref, bf16[16,2,128,128]{3,2,1,0:T(8,128)(2,1)} %copy-done.2, bf16[128,128]{1,0:T(8,128)(2,1)} %pad_maximum_fusion.3.kn_ref, ...), custom_call_target="tpu_custom_call" | custom-call | flops 1207959552 | bytes 1966080 | tf_op jit(solution)/shard_map/pallas_call | solution.py:122
  87.2 4.0 %all-to-all-start.1 = ((f32[4,260,128]{2,1,0:T(8,128)}), f32[4,260,128]{2,1,0:T(8,128)S(1)}, u32[]{:S(2)}, u32[]{:S(2)}) async-start(f32[4,260,128]{2,1,0:T(8,128)} %shard_map.127), calls=%async_computation.1 | async-start | bytes 1081344 | tf_op jit(solution)/shard_map/all_to_all | solution.py:242
  91.7 6.6 %all-to-all-done.1 = f32[4,260,128]{2,1,0:T(8,128)S(1)} async-done(((f32[4,260,128]{2,1,0:T(8,128)}), f32[4,260,128]{2,1,0:T(8,128)S(1)}, u32[]{:S(2)}, u32[]{:S(2)}) %all-to-all-start.1) | async-done | bytes 532512 | tf_op jit(solution)/shard_map/all_to_all | solution.py:242
  100.3 19.2 %all_to_all.15 = bf16[128,8,256]{2,0,1:T(8,128)(2,1)S(1)} all-to-all(bf16[128,8,256]{2,0,1:T(8,128)(2,1)S(1)} %bitcast.69), channel_id=1, replica_groups=mesh['sx'=4,'sz'=16,'tp'=8] {'tp'}, dimensions={1} | all-to-all | bytes 1048576 | tf_op jit(solution)/shard_map/all_to_all | solution.py:258
  119.6 0.6 add_convert_fusion
  (66 shorter events, 6.7 us)
Async XLA Ops:
  0.0 99.9 %copy-start = (bf16[256,2048]{1,0:T(8,128)(2,1)S(1)}, bf16[256,2048]{1,0:T(8,128)(2,1)}, u32[]{:S(2)}) copy-start(bf16[256,2048]{1,0:T(8,128)(2,1)} %param.19) | copy-start | bytes 3145732
  0.0 0.7 copy-start.1
  0.8 0.8 copy-start.4
  0.8 0.9 copy-start.5
  3.3 15.9 %copy-start.3 = (bf16[128,256]{1,0:T(8,128)(2,1)S(1)}, bf16[128,256]{1,0:T(8,128)(2,1)}, u32[]{:S(2)}) copy-start(bf16[128,256]{1,0:T(8,128)(2,1)} %param.13) | copy-start | bytes 196612
  3.3 73.0 %all-to-all-start = ((bf16[16,2,128,128]{3,2,1,0:T(8,128)(2,1)}), bf16[16,2,128,128]{3,2,1,0:T(8,128)(2,1)S(1)}, u32[]{:S(2)}, u32[]{:S(2)}) async-start(bf16[16,2,128,128]{3,2,1,0:T(8,128)(2,1)} %gather_fusion.1), calls=%async_computation | async-start | bytes 2097152 | tf_op jit(solution)/shard_map/all_to_all | solution.py:187
  19.2 14.8 %copy-start.9 = (bf16[2048,128]{1,0:T(8,128)(2,1)S(1)}, bf16[2048,128]{1,0:T(8,128)(2,1)}, u32[]{:S(2)}) copy-start(bf16[2048,128]{1,0:T(8,128)(2,1)} %param.16) | copy-start | bytes 1572868
  33.8 0.7 copy-start.12
  34.5 3.6 %copy-start.10 = (bf16[2048,128]{1,0:T(8,128)(2,1)S(1)}, bf16[2048,128]{1,0:T(8,128)(2,1)}, u32[]{:S(2)}) copy-start(bf16[2048,128]{1,0:T(8,128)(2,1)} %param.17) | copy-start | bytes 1572868
  35.0 0.7 copy-start.13
  37.0 0.7 copy-start.7
  38.4 0.6 copy-start.6
  39.0 36.7 %collective-permute-start = (bf16[2,128,1,128]{3,1,2,0:T(8,128)(2,1)S(1)}, bf16[2,128,1,128]{3,1,2,0:T(8,128)(2,1)S(1)}, u32[]{:S(2)}, u32[]{:S(2)}) collective-permute-start(bf16[2,128,1,128]{3,1,2,0:T(8,128)(2,1)S(1)} %pad_maximum_fusion.2), channel_id=1, source_target_pairs={{0,64},{8,72},{16,80},{24,88},{32,96},{40,104},{48,112},{56,120},{... | collective-permute-start | bytes 196616 | tf_op jit(solution)/shard_map/ppermute | solution.py:217
  56.8 0.7 copy-start.8
  76.3 1.0 copy-start.2
  87.2 4.0 %copy-start.11 = (bf16[2048,2]{0,1:T(2,128)(2,1)S(1)}, bf16[2048,2]{0,1:T(2,128)(2,1)}, u32[]{:S(2)}) copy-start(bf16[2048,2]{0,1:T(2,128)(2,1)} %param.18) | copy-start | bytes 24580
  87.2 11.1 %all-to-all-start.1 = ((f32[4,260,128]{2,1,0:T(8,128)}), f32[4,260,128]{2,1,0:T(8,128)S(1)}, u32[]{:S(2)}, u32[]{:S(2)}) async-start(f32[4,260,128]{2,1,0:T(8,128)} %shard_map.127), calls=%async_computation.1 | async-start | bytes 1081344 | tf_op jit(solution)/shard_map/all_to_all | solution.py:242

commit v18 on v16

--- a/solution.py
+++ b/solution.py
@@ -163,7 +163,8 @@
 
     peer_groups = group_of[jnp.arange(ring_z, dtype=jnp.int32) % req_count]
     cache_both = jnp.stack([cache_keys, cache_values], 1)
-    incoming = lax.all_to_all(cache_both[peer_groups], "sz", 0, 0, tiled=True)
+    outgoing = jnp.where((peer_groups == 0)[:, None, None, None], cache_both[0], cache_both[1])
+    incoming = lax.all_to_all(outgoing, "sz", 0, 0, tiled=True)
     cache_rows = ring_z * cache_keys.shape[1]
     keys_cache = incoming[:, 0].reshape(cache_rows, kv_local, head_dim)
     values_cache = incoming[:, 1].reshape(cache_rows, kv_local, head_dim)

time: 121 us -> 121 us (level)
  local copies, waits for them, and re-layouts: 10.1 us -> 8.58 us
    gather x1 -> x0, local copies, waits for them, and re-layouts: 1.65 us -> none  [per_device(): incoming = lax.all_to_all(cache_both[peer_groups], 'sz', 0, 0, tiled=True)]
where the time goes in v18:
time: 121 us; the launch traced here: 119 us
  blocking collectives  44.8 us (37%)
  starting transfers between devices  32.2 us (27%)
  waiting for transfers between devices  12.9 us (11%)
  Pallas kernels  8.65 us (7%)
  local copies, waits for them, and re-layouts  8.58 us (7%)
  other arithmetic  7.4 us (6%)
  matrix products  2.98 us (2%)
    all_to_all x1, blocking collectives, per_device(): arrived = lax.all_to_all(pieces, 'tp', 1, 1, tiled=True)  19.2 us
    all_to_all x1, starting transfers between devices, per_device(): incoming = lax.all_to_all(outgoing, 'sz', 0, 0, tiled=True)  15.9 us
    all_gather x1, blocking collectives, per_device(): gathered = lax.all_gather(hidden_in, 'tp', axis=1, tiled=True)  14.6 us
    ppermute x1, starting transfers between devices, per_device(): lax.ppermute(jnp.stack([keys_new, values_new]), 'sz', partner_pairs)  12.2 us
    all_gather x1, blocking collectives, per_device(): all_queries = lax.all_gather(queries, 'sx', axis=0, tiled=True)  11 us
    pallas_call x1, Pallas kernels, attention(): pl.pallas_call(attention_kernel, out_shape=jax.ShapeDtypeStruct((rows //...  8.65 us
    all_to_all x1, waiting for transfers between devices, per_device(): packed_in = lax.all_to_all(packed, 'sx', 0, 0, tiled=True)  6.57 us
    ppermute x1, waiting for transfers between devices, per_device(): lax.ppermute(jnp.stack([keys_new, values_new]), 'sz', partner_pairs)  6.31 us
  transfers between devices with their start and end apart: 3, of which 2 were waited for; matrix products, arithmetic and copies ran while one was open for 8% of the time, Pallas kernels for 0%

profile of v18, /device:TPU:1, one launch (start us, length us, event | category | flops | bytes accessed | tf_op | source)
XLA Modules:
  0.0 118.6 jit_solution(14481539209389033668)
XLA Ops:
  0.0 0.7 copy-done.1
  0.8 0.7 gather_fusion
  1.6 1.1 broadcast_select_fusion
  2.8 15.9 %all-to-all-start = ((bf16[16,2,128,128]{3,2,1,0:T(8,128)(2,1)}), bf16[16,2,128,128]{3,2,1,0:T(8,128)(2,1)S(1)}, u32[]{:S(2)}, u32[]{:S(2)}) async-start(bf16[16,2,128,128]{3,2,1,0:T(8,128)(2,1)} %broadcast_select_fusion), calls=%async_computation | async-start | bytes 2097152 | tf_op jit(solution)/shard_map/all_to_all | solution.py:167
  18.7 14.6 %all_gather.6 = bf16[128,2048]{1,0:T(8,128)(2,1)S(1)} all-gather(bf16[128,256]{1,0:T(8,128)(2,1)S(1)} %copy-done.3), channel_id=1, replica_groups=mesh['sx'=4,'sz'=16,'tp'=8] {'tp'}, dimensions={1}, use_global_device_ids=true | all-gather | bytes 589824 | tf_op jit(solution)/shard_map/all_gather | solution.py:173
  34.5 0.6 copy-done.13
  35.1 0.7 dynamic_slice.3
  36.5 0.6 copy-done.7
  38.1 0.5 copy-done.6
  38.6 12.2 %collective-permute-start = (bf16[2,128,1,128]{3,1,2,0:T(8,128)(2,1)S(1)}, bf16[2,128,1,128]{3,1,2,0:T(8,128)(2,1)S(1)}, u32[]{:S(2)}, u32[]{:S(2)}) collective-permute-start(bf16[2,128,1,128]{3,1,2,0:T(8,128)(2,1)S(1)} %pad_maximum_fusion.2), channel_id=1, source_target_pairs={{0,64},{8,72},{16,80},{24,88},{32,96},{40,104},{48,112},{56,120},{... | collective-permute-start | bytes 196616 | tf_op jit(solution)/shard_map/ppermute | solution.py:197
  51.0 1.0 broadcast_in_dim_reshape.5.qtok_ref
  52.0 1.6 %fusion.29 = f32[128,256]{1,0:T(8,128)S(1)} fusion(bf16[2048,256]{1,0:T(8,128)(2,1)} %param.15, bf16[128,2048]{1,0:T(8,128)(2,1)S(1)} %all_gather.6, f32[2048]{0:T(1024)S(1)} %copy-done.12, f32[128]{0:T(128)S(1)} %add_rsqrt_fusion.2), kind=kOutput, calls=%fused_computation.75 | convolution fusion | flops 135266304 | bytes 1712640 | tf_op jit(solution)/shard_map/dot_general | solution.py:179
  53.7 1.3 %pad_add_fusion.1.scalars = s32[2]{0:T(128)} fusion(s32[1]{0:T(128)} %bitcast, s32[1]{0:T(128)} %dynamic_slice.3), kind=kLoop, calls=%fused_computation.65 | loop fusion | flops 2 | bytes 16 | tf_op jit(solution)/shard_map/stack | solution.py:209
  54.9 0.6 pad_add_fusion
  55.5 0.7 pad_maximum_fusion.3.kn_ref
  57.8 11.0 %all_gather.7 = bf16[512,1,2,128]{3,2,1,0:T(2,128)(2,1)} all-gather(bf16[128,1,2,128]{3,2,1,0:T(2,128)(2,1)S(1)} %pad_maximum_fusion.1), channel_id=1, replica_groups=mesh['sx'=4,'sz'=16,'tp'=8] {'sx'}, dimensions={0}, use_global_device_ids=true | all-gather | bytes 327680 | tf_op jit(solution)/shard_map/all_gather | solution.py:199
  68.9 6.3 %collective-permute-done = bf16[2,128,1,128]{3,1,2,0:T(8,128)(2,1)S(1)} collective-permute-done((bf16[2,128,1,128]{3,1,2,0:T(8,128)(2,1)S(1)}, bf16[2,128,1,128]{3,1,2,0:T(8,128)(2,1)S(1)}, u32[]{:S(2)}, u32[]{:S(2)}) %collective-permute-start) | collective-permute-done | bytes 65568 | tf_op jit(solution)/shard_map/ppermute | solution.py:197
  75.2 0.6 slice_bitcast_fusion.1
  75.8 1.0 copy-done.2
  76.8 8.7 %shard_map.127 = f32[4,260,128]{2,1,0:T(8,128)} custom-call(s32[2]{0:T(128)} %pad_add_fusion.1.scalars, bf16[1024,128]{1,0:T(8,128)(2,1)} %bitcast.78, s32[1024,1]{1,0:T(8,128)} %broadcast_in_dim_reshape.5.qtok_ref, bf16[16,2,128,128]{3,2,1,0:T(8,128)(2,1)} %copy-done.2, bf16[128,128]{1,0:T(8,128)(2,1)} %pad_maximum_fusion.3.kn_ref, ...), custom_call_target="tpu_custom_call" | custom-call | flops 1207959552 | bytes 1966080 | tf_op jit(solution)/shard_map/pallas_call | solution.py:105
  85.4 4.1 %all-to-all-start.1 = ((f32[4,260,128]{2,1,0:T(8,128)}), f32[4,260,128]{2,1,0:T(8,128)S(1)}, u32[]{:S(2)}, u32[]{:S(2)}) async-start(f32[4,260,128]{2,1,0:T(8,128)} %shard_map.127), calls=%async_computation.1 | async-start | bytes 1081344 | tf_op jit(solution)/shard_map/all_to_all | solution.py:222
  90.0 6.6 %all-to-all-done.1 = f32[4,260,128]{2,1,0:T(8,128)S(1)} async-done(((f32[4,260,128]{2,1,0:T(8,128)}), f32[4,260,128]{2,1,0:T(8,128)S(1)}, u32[]{:S(2)}, u32[]{:S(2)}) %all-to-all-start.1) | async-done | bytes 532512 | tf_op jit(solution)/shard_map/all_to_all | solution.py:222
  98.7 19.2 %all_to_all.15 = bf16[128,8,256]{2,0,1:T(8,128)(2,1)S(1)} all-to-all(bf16[128,8,256]{2,0,1:T(8,128)(2,1)S(1)} %bitcast.69), channel_id=1, replica_groups=mesh['sx'=4,'sz'=16,'tp'=8] {'tp'}, dimensions={1} | all-to-all | bytes 1048576 | tf_op jit(solution)/shard_map/all_to_all | solution.py:238
  118.0 0.6 add_convert_fusion
  (65 shorter events, 6.7 us)
Async XLA Ops:
  0.0 98.3 %copy-start = (bf16[256,2048]{1,0:T(8,128)(2,1)S(1)}, bf16[256,2048]{1,0:T(8,128)(2,1)}, u32[]{:S(2)}) copy-start(bf16[256,2048]{1,0:T(8,128)(2,1)} %param.19) | copy-start | bytes 3145732
  0.0 0.7 copy-start.1
  0.8 0.8 copy-start.4
  0.8 0.9 copy-start.5
  2.8 15.9 %copy-start.3 = (bf16[128,256]{1,0:T(8,128)(2,1)S(1)}, bf16[128,256]{1,0:T(8,128)(2,1)}, u32[]{:S(2)}) copy-start(bf16[128,256]{1,0:T(8,128)(2,1)} %param.13) | copy-start | bytes 196612
  2.8 73.0 %all-to-all-start = ((bf16[16,2,128,128]{3,2,1,0:T(8,128)(2,1)}), bf16[16,2,128,128]{3,2,1,0:T(8,128)(2,1)S(1)}, u32[]{:S(2)}, u32[]{:S(2)}) async-start(bf16[16,2,128,128]{3,2,1,0:T(8,128)(2,1)} %broadcast_select_fusion), calls=%async_computation | async-start | bytes 2097152 | tf_op jit(solution)/shard_map/all_to_all | solution.py:167
  18.7 14.8 %copy-start.9 = (bf16[2048,128]{1,0:T(8,128)(2,1)S(1)}, bf16[2048,128]{1,0:T(8,128)(2,1)}, u32[]{:S(2)}) copy-start(bf16[2048,128]{1,0:T(8,128)(2,1)} %param.16) | copy-start | bytes 1572868
  33.2 0.7 copy-start.12
  33.9 3.6 %copy-start.10 = (bf16[2048,128]{1,0:T(8,128)(2,1)S(1)}, bf16[2048,128]{1,0:T(8,128)(2,1)}, u32[]{:S(2)}) copy-start(bf16[2048,128]{1,0:T(8,128)(2,1)} %param.17) | copy-start | bytes 1572868
  34.5 0.7 copy-start.13
  36.5 0.7 copy-start.7
  38.0 0.6 copy-start.6
  38.6 36.6 %collective-permute-start = (bf16[2,128,1,128]{3,1,2,0:T(8,128)(2,1)S(1)}, bf16[2,128,1,128]{3,1,2,0:T(8,128)(2,1)S(1)}, u32[]{:S(2)}, u32[]{:S(2)}) collective-permute-start(bf16[2,128,1,128]{3,1,2,0:T(8,128)(2,1)S(1)} %pad_maximum_fusion.2), channel_id=1, source_target_pairs={{0,64},{8,72},{16,80},{24,88},{32,96},{40,104},{48,112},{56,120},{... | collective-permute-start | bytes 196616 | tf_op jit(solution)/shard_map/ppermute | solution.py:197
  56.5 0.7 copy-start.8
  75.8 1.0 copy-start.2
  85.4 4.1 %copy-start.11 = (bf16[2048,2]{0,1:T(2,128)(2,1)S(1)}, bf16[2048,2]{0,1:T(2,128)(2,1)}, u32[]{:S(2)}) copy-start(bf16[2048,2]{0,1:T(2,128)(2,1)} %param.18) | copy-start | bytes 24580
  85.4 11.2 %all-to-all-start.1 = ((f32[4,260,128]{2,1,0:T(8,128)}), f32[4,260,128]{2,1,0:T(8,128)S(1)}, u32[]{:S(2)}, u32[]{:S(2)}) async-start(f32[4,260,128]{2,1,0:T(8,128)} %shard_map.127), calls=%async_computation.1 | async-start | bytes 1081344 | tf_op jit(solution)/shard_map/all_to_all | solution.py:222
